TPU v7x, 512 devices: a whole 4x8x8 slice. The times are simulated.
512 devices in a mesh: seq: 64 (over x, z, core), kvh: 4 (over y_hi), rep: 2 (over y_lo).
Axes of the slice: x: 4, y: 8 (y_hi: 4, y_lo: 2; y = y_hi * 2 + y_lo), z: 8, core: 2. Of those that a mesh axis runs over, the one named last changes fastest.
Arguments:
- vision_states: bfloat16 [64, 384, 1152], P('seq', 'kvh'), may hold values from -24 to 24
- frame_tokens: int32 [64], replicated, may hold values from 128 to 384, as said below
- norm_gain: float32 [1152], replicated, may hold values from 0.1 to 1.9
- projector: bfloat16 [1152, 3584], P(None, ('kvh', 'rep')), may hold values from -0.1875 to 0.1875
- head_weights: bfloat16 [3584, 3072], P(('kvh', 'rep')), may hold values from -4 to 4
Outputs:
- attended: bfloat16 [256, 64, 2048], P(None, 'seq', ('kvh', 'rep'))
Inputs may be any that keep to these rules, and one draw needn't show every extreme that they name: `frame_tokens`: the counts sum to 16384, and some frame has exactly 384 tokens.
All inputs are finite; a program needn't handle non-finite values.
Results may differ from a plain program's by a relative error of at most 0.0062.
Values may be sent and summed in bfloat16 or wider, within the bound.
No kernel may reach another device: no remote copies, remote signals or barrier semaphores. Data moves between devices by JAX's collectives and lax.ppermute only.
A program may use at most 128 MiB of HBM per device.

v0:
```python
import jax
import jax.numpy as jnp
from jax import lax
from jax.sharding import PartitionSpec as P

KV_HEADS = 4
HEAD_DIM = 128
GROUP_HEADS = 4


norm_eps = 1e-06
masked_score = -1e30


def layer_norm(states, norm_gain):
    values = states.astype(jnp.float32)
    center = values - jnp.mean(values, axis=-1, keepdims=True)
    spread = jnp.mean(center * center, axis=-1, keepdims=True)
    return (center * lax.rsqrt(spread + norm_eps) * norm_gain).astype(jnp.bfloat16)


def attention_step(queries, query_pos, key_rows, key_base, seq_count):
    scale = queries.shape[-1] ** (-0.5)

    def add_keys(carry, piece, start):
        context, top, total = carry
        key_piece, value_piece = piece
        number = key_piece.shape[0]
        index = jnp.arange(number, dtype=jnp.int32)
        key_pos = (key_base + index % key_rows) * seq_count + index // key_rows
        allowed = (key_pos[None, :] <= query_pos[:, None])[:, None, :]
        scores = (
            jnp.einsum("qhd,kd->qhk", queries, key_piece, preferred_element_type=jnp.float32)
            * scale
        )
        scores = jnp.where(allowed, scores, masked_score)
        new_top = jnp.maximum(top, jnp.max(scores, axis=-1))
        weights = jnp.where(allowed, jnp.exp(scores - new_top[..., None]), 0.0)
        total = jnp.sum(weights, axis=-1)
        update = jnp.einsum(
            "qhk,kd->qhd",
            weights.astype(jnp.bfloat16),
            value_piece,
            preferred_element_type=jnp.float32,
        )
        return (update, new_top, total)

    return add_keys


def empty_partials(tok_rows, head_count):
    return (
        jnp.zeros((tok_rows, head_count, HEAD_DIM), jnp.float32),
        jnp.full((tok_rows, head_count), masked_score, jnp.float32),
        jnp.zeros((tok_rows, head_count), jnp.float32),
    )


def local(vision_states, frame_tokens, norm_gain, projector, head_weights):
    seq_count = lax.axis_size("seq")
    seq_index = lax.axis_index("seq")
    rep_count = lax.axis_size("rep")
    frames_dev = vision_states.shape[0]
    frame_max = vision_states.shape[1] * lax.axis_size("kvh")
    d_cols = projector.shape[1]
    cap_frame = frame_max // seq_count
    tok_rows = 2 * frames_dev * frame_max // 3
    heads_local = GROUP_HEADS // rep_count
    normed = layer_norm(vision_states, norm_gain)
    hidden = jnp.einsum(
        "frv,vc->frc",
        lax.all_gather(normed, "kvh", axis=1, tiled=True),
        projector,
        preferred_element_type=jnp.float32,
    )
    visual_frames = jax.nn.gelu(hidden, approximate=False).astype(jnp.bfloat16)
    ends = jnp.cumsum(frame_tokens)
    starts_all = ends - frame_tokens
    my_starts = lax.dynamic_slice_in_dim(starts_all, seq_index * frames_dev, frames_dev, 0)
    dest = jnp.arange(seq_count, dtype=jnp.int32)[:, None, None]
    slots = jnp.arange(cap_frame, dtype=jnp.int32)[None, None, :]
    frame_local = jnp.arange(frames_dev, dtype=jnp.int32)[None, :, None]
    row_of = jnp.mod(dest - my_starts[None, :, None], seq_count) + slots * seq_count
    send_index = (frame_local * frame_max + row_of).reshape(-1)
    outgoing = visual_frames.reshape(frames_dev * frame_max, d_cols)[send_index]
    received = lax.all_to_all(outgoing, "seq", split_axis=0, concat_axis=0, tiled=True)
    query_pos = jnp.arange(tok_rows, dtype=jnp.int32) * seq_count + seq_index
    before = ends[None, :] <= query_pos[:, None]
    frame = jnp.sum(before.astype(jnp.int32), axis=1)
    offset = jnp.sum(jnp.where(before, frame_tokens[None, :], 0), axis=1)
    slot_index = frame * cap_frame + (query_pos - offset) // seq_count
    visual = received[slot_index]
    wide = head_weights.reshape(d_cols, KV_HEADS, GROUP_HEADS + 2, HEAD_DIM)
    query_w = wide[:, :, :GROUP_HEADS].reshape(d_cols, KV_HEADS, rep_count, heads_local * HEAD_DIM)
    pair_w = wide[:, :, GROUP_HEADS:].reshape(d_cols, KV_HEADS, 1, 2 * HEAD_DIM)
    pair_w = jnp.broadcast_to(pair_w, (d_cols, KV_HEADS, rep_count, 2 * HEAD_DIM))
    piece_w = jnp.concatenate([query_w, pair_w], axis=3).reshape(
        d_cols, KV_HEADS * rep_count, (heads_local + 2) * HEAD_DIM
    )
    summed = lax.psum_scatter(
        jnp.einsum("tc,cpw->ptw", visual, piece_w, preferred_element_type=jnp.float32),
        ("kvh", "rep"),
        scatter_dimension=0,
        tiled=True,
    )[0]
    head_rows = summed.astype(jnp.bfloat16)
    queries = head_rows[:, : heads_local * HEAD_DIM].reshape(tok_rows, heads_local, HEAD_DIM)
    key_own = head_rows[:, heads_local * HEAD_DIM : (heads_local + 1) * HEAD_DIM]
    value_own = head_rows[:, (heads_local + 1) * HEAD_DIM :]
    add_keys = attention_step(queries, query_pos, tok_rows, 0, seq_count)
    context, top, total = add_keys(
        empty_partials(tok_rows, heads_local),
        (
            lax.all_gather(key_own, "seq", axis=0, tiled=True),
            lax.all_gather(value_own, "seq", axis=0, tiled=True),
        ),
        jnp.int32(0),
    )
    result = (context / total[..., None]).astype(jnp.bfloat16)
    return result.reshape(tok_rows, 1, heads_local * HEAD_DIM)


def solution(mesh):
    placed = (P("seq", "kvh", None), P(), P(), P(None, ("kvh", "rep")), P(("kvh", "rep"), None))
    return jax.shard_map(
        local, mesh=mesh, in_specs=placed, out_specs=P(None, "seq", ("kvh", "rep")), check_vma=False
    )
```

profile of v0, /device:TPU:1, one launch (start us, length us, event | category | flops | bytes accessed | tf_op | source)
XLA Modules:
  0.0 328.2 jit_solution(847766380383886331)
XLA Ops:
  6.5 0.0 copy-start
  6.5 0.8 copy.27
  7.4 0.1 reduce-window.8
  7.5 0.1 reduce.2
  7.6 0.7 sub.59
  8.2 0.6 dynamic_slice.3
  8.8 0.7 and_select_fusion.1
  9.5 0.1 broadcast_add_fusion
  9.6 0.1 add.150
  9.7 1.1 convert_reduce_fusion
  10.8 1.2 fusion.42
  12.0 1.1 fusion.44
  13.1 22.0 %all_gather.9 = bf16[1,384,1152]{2,1,0:T(8,128)(2,1)S(1)} all-gather(bf16[1,96,1152]{2,1,0:T(8,128)(2,1)S(1)} %fusion.44), channel_id=1, replica_groups=mesh['seq'=64,'kvh'=4,'rep'=2] {'kvh'}, dimensions={1}, use_global_device_ids=true | all-gather | bytes 1105920 | tf_op jit(solution)/shard_map/all_gather | solution.py:72
  35.2 0.0 copy-done
  35.2 2.1 fusion.30
  37.3 0.2 copy.28
  37.5 2.1 gather_fusion
  39.5 1.0 all_to_all.8
  40.5 16.4 %all-to-all-start = ((bf16[64,6,448]{2,1,0:T(8,128)(2,1)}), bf16[64,6,448]{2,1,0:T(8,128)(2,1)S(1)}, u32[]{:S(2)}, u32[]{:S(2)}) async-start(bf16[64,6,448]{2,1,0:T(8,128)(2,1)} %all_to_all.8), calls=%async_computation | async-start | bytes 1048576 | tf_op jit(solution)/shard_map/all_to_all | solution.py:86
  57.0 0.0 reduce-scatter.2.cloned.1.call-start
  57.0 0.0 copy-start.2
  57.1 4.6 %copy.23 = bf16[448,3072]{0,1:T(8,128)(2,1)} copy(bf16[448,3072]{1,0:T(8,128)(2,1)} %param.9) | data formatting | bytes 5505024 | tf_op args[4]
  61.6 1.8 slice.24
  63.4 2.3 slice.25
  65.7 2.3 copy.26
  68.1 1.5 copy.25
  69.5 0.0 copy-done.2
  69.5 0.1 fusion.53
  69.7 4.6 %all-to-all-done = bf16[64,6,448]{2,1,0:T(8,128)(2,1)S(1)} async-done(((bf16[64,6,448]{2,1,0:T(8,128)(2,1)}), bf16[64,6,448]{2,1,0:T(8,128)(2,1)S(1)}, u32[]{:S(2)}, u32[]{:S(2)}) %all-to-all-start) | async-done | bytes 344096 | tf_op jit(solution)/shard_map/all_to_all | solution.py:86
  74.3 0.2 all_to_all.10
  74.5 1.2 gather_fusion.1
  75.7 0.1 broadcast_in_dim.58
  75.8 4.8 %fusion.13 = f32[8,256,512]{1,2,0:T(8,128)} fusion(bf16[448,8,256]{2,0,1:T(8,128)(2,1)S(1)} %bitcast.45, bf16[448,8,256]{2,0,1:T(8,128)(2,1)} %copy.26, bf16[256,448]{1,0:T(8,128)(2,1)S(1)} %gather_fusion.1), kind=kOutput, calls=%fused_computation.17 | convolution fusion | flops 946864128 | bytes 8093696 | tf_op jit(solution)/shard_map/tc,cpw->ptw/dot_general | solution.py:101
  80.6 0.0 reduce-scatter.2.cloned.1.call-update
  80.6 0.0 all-gather.3.cloned.1.call-start
  80.7 51.4 %reduce-scatter.2.cloned.1.call-done = f32[1,256,512]{1,2,0:T(8,128)} async-done(((f32[8,256,512]{1,2,0:T(8,128)}), f32[1,256,512]{1,2,0:T(8,128)}) %reduce-scatter.2.cloned.1.call-update) | async-done | bytes 524304 | tf_op jit(solution)/shard_map/reduce_scatter | solution.py:100
  132.1 1.1 convert_bitcast_fusion
  133.1 0.7 fusion.63
  133.8 0.0 all-gather.3.cloned.1.call-update
  133.8 0.0 all-gather.5.cloned.1.call-start
  133.9 0.7 all-gather.5.cloned.1.call-update
  134.6 4.3 %broadcast_compare_fusion = pred[256,16384]{1,0:T(8,128)(4,1)} fusion(s32[16384]{0:T(1024)S(1)} %fusion.54, s32[256]{0:T(256)S(1)} %multiply_add_fusion), kind=kLoop, calls=%fused_computation.9 | loop fusion | flops 4194304 | bytes 4260864 | tf_op jit(solution)/shard_map/le | solution.py:31
  138.9 78.7 %all-gather.3.cloned.1.call-done = bf16[16384,128]{0,1:T(8,128)(2,1)} async-done(((bf16[256,128]{0,1:T(8,128)(2,1)}), bf16[16384,128]{0,1:T(8,128)(2,1)}) %all-gather.3.cloned.1.call-update) | async-done | bytes 4194320 | tf_op jit(solution)/shard_map/all_gather | solution.py:114
  217.6 17.6 %fusion = (f32[256,2]{0,1:T(2,128)S(1)}, f32[256,2,16384]{2,0,1:T(8,128)}) fusion(pred[256,16384]{1,0:T(8,128)(4,1)} %broadcast_compare_fusion, bf16[256,2,128]{0,2,1:T(8,128)(2,1)S(1)} %bitcast.46, bf16[16384,128]{0,1:T(8,128)(2,1)} %all-gather.3.cloned.1.call-done), kind=kOutput, calls=%fused_computation.4 | convolution fusion | flops 2172648960 | bytes 42076160 | tf_op jit(solution)/shard_map/qhd,kd->qhk/dot_general | solution.py:33
  235.2 16.3 %fusion.1 = f32[256,2]{0,1:T(2,128)S(1)} fusion(f32[256,2,16384]{2,0,1:T(8,128)} %get-tuple-element.10, f32[256,2]{0,1:T(2,128)S(1)} %broadcast_maximum_fusion, pred[256,16384]{1,0:T(8,128)(4,1)} %broadcast_compare_fusion), kind=kLoop, calls=%fused_computation.5 | loop fusion | flops 41942528 | bytes 37752832 | tf_op jit(solution)/shard_map/reduce_sum | solution.py:39
  251.5 50.8 %all-gather.5.cloned.1.call-done = bf16[16384,128]{0,1:T(8,128)(2,1)} async-done(((bf16[256,128]{0,1:T(8,128)(2,1)}), bf16[16384,128]{0,1:T(8,128)(2,1)}) %all-gather.5.cloned.1.call-update) | async-done | bytes 4194320 | tf_op jit(solution)/shard_map/all_gather | solution.py:115
  302.3 18.5 %fusion.21 = bf16[256,2,128]{0,2,1:T(8,128)(2,1)S(1)} fusion(bf16[16384,128]{0,1:T(8,128)(2,1)} %all-gather.5.cloned.1.call-done, f32[256,2,16384]{2,0,1:T(8,128)} %get-tuple-element.10, f32[256,2]{0,1:T(2,128)S(1)} %broadcast_maximum_fusion, pred[256,16384]{1,0:T(8,128)(4,1)} %broadcast_compare_fusion, f32[256,2]{0,1:T(2,128)S(1)} %fusion.1), kind=kOutput, calls=%fused_computation.19 | convolution fusion | flops 2189557760 | bytes 42078208 | tf_op jit(solution)/shard_map/qhk,kd->qhd/dot_general | solution.py:40
  320.9 0.8 copy.32
  (14 shorter events, 0.1 us)
Async XLA Ops:
  6.5 28.6 %copy-start = (bf16[1152,448]{0,1:T(8,128)(2,1)S(1)}, bf16[1152,448]{0,1:T(8,128)(2,1)}, u32[]{:S(2)}) copy-start(bf16[1152,448]{0,1:T(8,128)(2,1)} %param.8) | copy-start | bytes 3096580
  40.5 33.8 %all-to-all-start = ((bf16[64,6,448]{2,1,0:T(8,128)(2,1)}), bf16[64,6,448]{2,1,0:T(8,128)(2,1)S(1)}, u32[]{:S(2)}, u32[]{:S(2)}) async-start(bf16[64,6,448]{2,1,0:T(8,128)(2,1)} %all_to_all.8), calls=%async_computation | async-start | bytes 1048576 | tf_op jit(solution)/shard_map/all_to_all | solution.py:86
  57.0 75.1 %reduce-scatter.2.cloned.1.call-start = ((), (), s32[]{:S(2)}) async-start(), calls=%async_computation.2 | async-start | bytes 4718592 | tf_op jit(solution)/shard_map/reduce_scatter | solution.py:100
  57.0 12.5 %copy-start.2 = (s32[64]{0:T(128)S(1)}, s32[64]{0:T(128)}, u32[]{:S(2)}) copy-start(s32[64]{0:T(128)} %param.6) | copy-start | bytes 772
  80.6 137.0 %all-gather.3.cloned.1.call-start = ((), (), s32[]{:S(2)}) async-start(), calls=%async_computation.3 | async-start | bytes 4259840 | tf_op jit(solution)/shard_map/all_gather | solution.py:114
  133.8 168.5 %all-gather.5.cloned.1.call-start = ((), (), s32[]{:S(2)}) async-start(), calls=%async_computation.4 | async-start | bytes 4259840 | tf_op jit(solution)/shard_map/all_gather | solution.py:115
  302.3 19.3 %copy-start.1 = (bf16[1152,448]{0,1:T(8,128)(2,1)S(1)}, bf16[1152,448]{0,1:T(8,128)(2,1)}, u32[]{:S(2)}) copy-start(bf16[1152,448]{0,1:T(8,128)(2,1)} %param.8) | copy-start | bytes 3096580
Sparse Core Ops, SparseCore 0:
  80.7 51.2 reduce-scatter.1
  135.2 82.3 all-gather.2
  220.7 81.5 all-gather.4
where the time goes:
time: 329 us; the launch traced here: 328 us
  waiting for transfers between devices  186 us (57%)
  matrix products  43 us (13%)
  other arithmetic  26.9 us (8%)
  blocking collectives  22 us (7%)
  local copies, waits for them, and re-layouts  20.2 us (6%)
  starting transfers between devices  16.6 us (5%)
  between operations  13.3 us (4%)
    all_gather x1, waiting for transfers between devices, local(): lax.all_gather(key_own, 'seq', axis=0, tiled=True)  78.7 us
    reduce_scatter x1, waiting for transfers between devices, local(): lax.psum_scatter(jnp.einsum('tc,cpw->ptw', visual, piece_w, preferred_ele...  51.4 us
    all_gather x1, waiting for transfers between devices, local(): lax.all_gather(value_own, 'seq', axis=0, tiled=True)  50.8 us
    all_gather x1, blocking collectives, local(): lax.all_gather(normed, 'kvh', axis=1, tiled=True)  22 us
    dot_general x1, matrix products, add_keys(): jnp.einsum('qhk,kd->qhd', weights.astype(jnp.bfloat16), value_piece, pref...  18.5 us
    dot_general x1, matrix products, add_keys(): jnp.einsum('qhd,kd->qhk', queries, key_piece, preferred_element_type=jnp....  17.6 us
    all_to_all x1, starting transfers between devices, local(): lax.all_to_all(outgoing, 'seq', split_axis=0, concat_axis=0, tiled=True)  16.4 us
    reduce_sum x1, other arithmetic, add_keys(): total = jnp.sum(weights, axis=-1)  16.3 us
  transfers between devices with their start and end apart: 4, of which 4 were waited for; matrix products, arithmetic and copies ran while one was open for 15% of the time, Pallas kernels for 0%

commit v1 on v0

--- a/solution.py
+++ b/solution.py
@@ -67,9 +67,10 @@
     tok_rows = 2 * frames_dev * frame_max // 3
     heads_local = GROUP_HEADS // rep_count
     normed = layer_norm(vision_states, norm_gain)
+    frame_rows = lax.all_gather(normed[0], "kvh", axis=0, tiled=False).reshape(1, frame_max, -1)
     hidden = jnp.einsum(
         "frv,vc->frc",
-        lax.all_gather(normed, "kvh", axis=1, tiled=True),
+        frame_rows,
         projector,
         preferred_element_type=jnp.float32,
     )
@@ -105,16 +106,29 @@
     )[0]
     head_rows = summed.astype(jnp.bfloat16)
     queries = head_rows[:, : heads_local * HEAD_DIM].reshape(tok_rows, heads_local, HEAD_DIM)
-    key_own = head_rows[:, heads_local * HEAD_DIM : (heads_local + 1) * HEAD_DIM]
-    value_own = head_rows[:, (heads_local + 1) * HEAD_DIM :]
-    add_keys = attention_step(queries, query_pos, tok_rows, 0, seq_count)
-    context, top, total = add_keys(
-        empty_partials(tok_rows, heads_local),
-        (
-            lax.all_gather(key_own, "seq", axis=0, tiled=True),
-            lax.all_gather(value_own, "seq", axis=0, tiled=True),
-        ),
-        jnp.int32(0),
+    pair_own = head_rows[:, heads_local * HEAD_DIM :]
+    pair_all = lax.all_gather(pair_own, "seq", axis=0, tiled=False)
+    keys = pair_all[..., :HEAD_DIM]
+    values = pair_all[..., HEAD_DIM:]
+    scale = HEAD_DIM ** (-0.5)
+    key_pos = (
+        jnp.arange(tok_rows, dtype=jnp.int32)[None, :] * seq_count
+        + jnp.arange(seq_count, dtype=jnp.int32)[:, None]
+    )
+    allowed = (key_pos[None, :, :] <= query_pos[:, None, None])[:, None, :, :]
+    scores = (
+        jnp.einsum("qhd,skd->qhsk", queries, keys, preferred_element_type=jnp.float32)
+        * scale
+    )
+    scores = jnp.where(allowed, scores, masked_score)
+    top = jnp.max(scores, axis=(2, 3))
+    weights = jnp.where(allowed, jnp.exp(scores - top[..., None, None]), 0.0)
+    total = jnp.sum(weights, axis=(2, 3))
+    context = jnp.einsum(
+        "qhsk,skd->qhd",
+        weights.astype(jnp.bfloat16),
+        values,
+        preferred_element_type=jnp.float32,
     )
     result = (context / total[..., None]).astype(jnp.bfloat16)
     return result.reshape(tok_rows, 1, heads_local * HEAD_DIM)

time: 329 us -> 308 us (0.936)
  waiting for transfers between devices: 186 us -> 143 us
  local copies, waits for them, and re-layouts: 20.2 us -> 42.4 us
    all_gather x2 -> x1, waiting for transfers between devices: 130 us -> 87.2 us  [local(): pair_all = lax.all_gather(pair_own, 'seq', axis=0, tiled=False)]
    unnamed x7 -> x9, local copies, waits for them, and re-layouts: 4.59 us -> 20.8 us
    slice x2, local copies, waits for them, and re-layouts: 0.68 us -> 6.71 us  [the longest x1 6.04 us: local(): values = pair_all[..., HEAD_DIM:]]
  transfers between devices with their start and end apart: 4 -> 3, of which waited for: 4 -> 3; matrix products, arithmetic and copies ran while one was open for 15% -> 6% of each run, Pallas kernels for 0% -> 0%
where the time goes in v1:
time: 308 us; the launch traced here: 307 us
  waiting for transfers between devices  143 us (46%)
  matrix products  42.7 us (14%)
  local copies, waits for them, and re-layouts  42.4 us (14%)
  other arithmetic  26.8 us (9%)
  blocking collectives  22 us (7%)
  starting transfers between devices  16.7 us (5%)
  between operations  13.6 us (4%)
    all_gather x1, waiting for transfers between devices, local(): pair_all = lax.all_gather(pair_own, 'seq', axis=0, tiled=False)  87.2 us
    reduce_scatter x1, waiting for transfers between devices, local(): lax.psum_scatter(jnp.einsum('tc,cpw->ptw', visual, piece_w, preferred_ele...  51.2 us
    all_gather x1, blocking collectives, local(): lax.all_gather(normed[0], 'kvh', axis=0, tiled=False)  22 us
    unnamed x9, local copies, waits for them, and re-layouts  20.8 us
    dot_general x1, matrix products, local(): jnp.einsum('qhsk,skd->qhd', weights.astype(jnp.bfloat16), values, preferr...  18.7 us
    dot_general x1, matrix products, local(): jnp.einsum('qhd,skd->qhsk', queries, keys, preferred_element_type=jnp.flo...  17.1 us
    all_to_all x1, starting transfers between devices, local(): lax.all_to_all(outgoing, 'seq', split_axis=0, concat_axis=0, tiled=True)  16.4 us
    reduce_sum x1, other arithmetic, local(): total = jnp.sum(weights, axis=(2, 3))  15.6 us
  transfers between devices with their start and end apart: 3, of which 3 were waited for; matrix products, arithmetic and copies ran while one was open for 6% of the time, Pallas kernels for 0%

profile of v1, /device:TPU:1, one launch (start us, length us, event | category | flops | bytes accessed | tf_op | source)
XLA Modules:
  0.0 307.3 jit_solution(17120739556069640455)
XLA Ops:
  6.5 0.0 copy-start
  6.5 1.1 convert_reduce_fusion
  7.7 1.2 fusion.36
  8.9 0.8 copy.43
  9.6 0.1 reduce-window.8
  9.7 0.1 reduce.2
  9.8 0.7 sub.52
  10.5 0.6 dynamic_slice.3
  11.1 0.7 and_select_fusion.1
  11.8 0.1 broadcast_add_fusion
  11.8 0.1 add.150
  12.0 1.1 fusion.38
  13.1 22.0 %all_gather.9 = bf16[4,96,1152]{2,1,0:T(8,128)(2,1)S(1)} all-gather(bf16[1,96,1152]{2,1,0:T(8,128)(2,1)S(1)} %fusion.38), channel_id=1, replica_groups=mesh['seq'=64,'kvh'=4,'rep'=2] {'kvh'}, dimensions={0}, use_global_device_ids=true | all-gather | bytes 1105920 | tf_op jit(solution)/shard_map/all_gather | solution.py:70
  35.2 2.1 fusion.26
  37.3 0.2 copy.44
  37.5 2.1 gather_fusion
  39.5 1.0 all_to_all.8
  40.5 16.4 %all-to-all-start = ((bf16[64,6,448]{2,1,0:T(8,128)(2,1)}), bf16[64,6,448]{2,1,0:T(8,128)(2,1)S(1)}, u32[]{:S(2)}, u32[]{:S(2)}) async-start(bf16[64,6,448]{2,1,0:T(8,128)(2,1)} %all_to_all.8), calls=%async_computation | async-start | bytes 1048576 | tf_op jit(solution)/shard_map/all_to_all | solution.py:87
  57.0 0.0 reduce-scatter.2.cloned.1.call-start
  57.0 0.0 copy-start.2
  57.1 4.6 %copy.39 = bf16[448,3072]{0,1:T(8,128)(2,1)} copy(bf16[448,3072]{1,0:T(8,128)(2,1)} %param.9) | data formatting | bytes 5505024 | tf_op args[4]
  61.6 2.3 slice.29
  63.9 1.8 slice.28
  65.7 2.4 copy.42
  68.1 1.5 copy.41
  69.6 0.1 fusion.41
  69.7 4.6 %all-to-all-done = bf16[64,6,448]{2,1,0:T(8,128)(2,1)S(1)} async-done(((bf16[64,6,448]{2,1,0:T(8,128)(2,1)}), bf16[64,6,448]{2,1,0:T(8,128)(2,1)S(1)}, u32[]{:S(2)}, u32[]{:S(2)}) %all-to-all-start) | async-done | bytes 344096 | tf_op jit(solution)/shard_map/all_to_all | solution.py:87
  74.3 0.2 all_to_all.10
  74.5 1.2 gather_fusion.1
  75.7 0.1 broadcast_in_dim.36
  75.8 4.8 %fusion.12 = f32[8,256,512]{1,2,0:T(8,128)} fusion(bf16[448,8,256]{2,0,1:T(8,128)(2,1)S(1)} %bitcast.61, bf16[448,8,256]{2,0,1:T(8,128)(2,1)} %copy.42, bf16[256,448]{1,0:T(8,128)(2,1)S(1)} %gather_fusion.1), kind=kOutput, calls=%fused_computation.17 | convolution fusion | flops 946864128 | bytes 8093696 | tf_op jit(solution)/shard_map/tc,cpw->ptw/dot_general | solution.py:102
  80.6 0.0 reduce-scatter.2.cloned.1.call-update
  80.6 0.2 all-gather.3.cloned.1.call-start
  80.8 51.2 %reduce-scatter.2.cloned.1.call-done = f32[1,256,512]{1,2,0:T(8,128)} async-done(((f32[8,256,512]{1,2,0:T(8,128)}), f32[1,256,512]{1,2,0:T(8,128)}) %reduce-scatter.2.cloned.1.call-update) | async-done | bytes 524304 | tf_op jit(solution)/shard_map/reduce_scatter | solution.py:101
  132.1 1.1 convert_bitcast_fusion
  133.1 0.7 fusion.49
  133.8 0.0 all-gather.3.cloned.1.call-update
  133.9 5.0 %broadcast_compare_fusion = pred[256,64,256]{0,2,1:T(8,128)(4,1)} fusion(s32[256]{0:T(256)S(1)} %broadcast_add_fusion.1, s32[64,256]{1,0:T(8,128)S(1)} %iota_add_fusion), kind=kLoop, calls=%fused_computation.9 | loop fusion | flops 4194304 | bytes 4260864 | tf_op jit(solution)/shard_map/le | solution.py:118
  138.9 87.2 %all-gather.3.cloned.1.call-done = bf16[16384,256]{0,1:T(8,128)(2,1)} async-done(((bf16[256,256]{0,1:T(8,128)(2,1)}), bf16[16384,256]{0,1:T(8,128)(2,1)}) %all-gather.3.cloned.1.call-update) | async-done | bytes 8388624 | tf_op jit(solution)/shard_map/all_gather | solution.py:110
  226.0 9.4 %copy.62 = bf16[32,8,64,256]{3,2,1,0:T(8,128)(2,1)} copy(bf16[32,8,64,256]{3,1,2,0:T(8,128)(2,1)} %bitcast.58) | data formatting | bytes 16777216
  235.4 6.0 %fusion.48 = (bf16[64,256,128]{1,0,2:T(8,128)(2,1)}, bf16[64,256,128]{1,0,2:T(8,128)(2,1)}) fusion(bf16[64,256,256]{1,0,2:T(8,128)(2,1)} %bitcast.55), kind=kLoop, calls=%fused_computation.78 | loop fusion | bytes 16777216 | tf_op jit(solution)/shard_map/slice | solution.py:112
  241.4 6.8 %copy.61 = bf16[64,256,128]{2,1,0:T(8,128)(2,1)} copy(bf16[64,256,128]{1,0,2:T(8,128)(2,1)} %get-tuple-element.8) | data formatting | bytes 8388608
  248.3 17.1 %fusion = (f32[256,2]{0,1:T(2,128)S(1)}, f32[256,2,64,256]{0,3,2,1:T(8,128)}) fusion(pred[256,64,256]{0,2,1:T(8,128)(4,1)} %broadcast_compare_fusion, bf16[256,2,128,1]{0,2,3,1:T(8,128)(2,1)S(1)} %bitcast.64, bf16[64,256,128]{2,1,0:T(8,128)(2,1)} %copy.61), kind=kOutput, calls=%fused_computation.4 | convolution fusion | flops 2172648960 | bytes 42076160 | tf_op jit(solution)/shard_map/qhd,skd->qhsk/dot_general | solution.py:120
  265.4 15.6 %fusion.1 = f32[256,2]{0,1:T(2,128)S(1)} fusion(f32[256,2,64,256]{0,3,2,1:T(8,128)} %get-tuple-element.12, f32[256,2]{0,1:T(2,128)S(1)} %get-tuple-element.11, pred[256,64,256]{0,2,1:T(8,128)(4,1)} %broadcast_compare_fusion), kind=kLoop, calls=%fused_computation.5 | loop fusion | flops 41942528 | bytes 37752832 | tf_op jit(solution)/shard_map/reduce_sum | solution.py:126
  281.0 0.0 copy-start.1
  281.0 18.7 %fusion.21 = bf16[256,2,128]{0,2,1:T(8,128)(2,1)S(1)} fusion(f32[256,2,64,256]{0,3,2,1:T(8,128)} %get-tuple-element.12, f32[256,2]{0,1:T(2,128)S(1)} %get-tuple-element.11, pred[256,64,256]{0,2,1:T(8,128)(4,1)} %broadcast_compare_fusion, bf16[64,256,128]{1,0,2:T(8,128)(2,1)} %get-tuple-element.7, f32[256,2]{0,1:T(2,128)S(1)} %fusion.1), kind=kOutput, calls=%fused_computation.21 | convolution fusion | flops 2189557760 | bytes 42078208 | tf_op jit(solution)/shard_map/qhsk,skd->qhd/dot_general | solution.py:127
  299.7 0.8 copy.50
  300.4 0.0 copy-done.1
  (13 shorter events, 0.1 us)
Async XLA Ops:
  6.5 28.6 %copy-start = (bf16[1152,448]{0,1:T(8,128)(2,1)S(1)}, bf16[1152,448]{0,1:T(8,128)(2,1)}, u32[]{:S(2)}) copy-start(bf16[1152,448]{0,1:T(8,128)(2,1)} %param.8) | copy-start | bytes 3096580
  40.5 33.8 %all-to-all-start = ((bf16[64,6,448]{2,1,0:T(8,128)(2,1)}), bf16[64,6,448]{2,1,0:T(8,128)(2,1)S(1)}, u32[]{:S(2)}, u32[]{:S(2)}) async-start(bf16[64,6,448]{2,1,0:T(8,128)(2,1)} %all_to_all.8), calls=%async_computation | async-start | bytes 1048576 | tf_op jit(solution)/shard_map/all_to_all | solution.py:87
  57.0 75.1 %reduce-scatter.2.cloned.1.call-start = ((), (), s32[]{:S(2)}) async-start(), calls=%async_computation.2 | async-start | bytes 4718592 | tf_op jit(solution)/shard_map/reduce_scatter | solution.py:101
  57.0 12.5 %copy-start.2 = (s32[64]{0:T(128)S(1)}, s32[64]{0:T(128)}, u32[]{:S(2)}) copy-start(s32[64]{0:T(128)} %param.6) | copy-start | bytes 772
  80.6 145.4 %all-gather.3.cloned.1.call-start = ((), (), s32[]{:S(2)}) async-start(), calls=%async_computation.3 | async-start | bytes 8519680 | tf_op jit(solution)/shard_map/all_gather | solution.py:110
  281.0 19.4 %copy-start.1 = (bf16[1152,448]{0,1:T(8,128)(2,1)S(1)}, bf16[1152,448]{0,1:T(8,128)(2,1)}, u32[]{:S(2)}) copy-start(bf16[1152,448]{0,1:T(8,128)(2,1)} %param.8) | copy-start | bytes 3096580
Sparse Core Ops, SparseCore 0:
  80.7 51.2 reduce-scatter.1
  135.2 90.7 all-gather.2

commit v2 on v0

--- a/solution.py
+++ b/solution.py
@@ -1,6 +1,10 @@
+import functools
+
 import jax
 import jax.numpy as jnp
 from jax import lax
+from jax.experimental import pallas as pl
+from jax.experimental.pallas import tpu as pltpu
 from jax.sharding import PartitionSpec as P
 
 KV_HEADS = 4
@@ -19,40 +23,77 @@
     return (center * lax.rsqrt(spread + norm_eps) * norm_gain).astype(jnp.bfloat16)
 
 
-def attention_step(queries, query_pos, key_rows, key_base, seq_count):
-    scale = queries.shape[-1] ** (-0.5)
+def attention_kernel(seq_ref, q_ref, kv_ref, o_ref, *, shards, tok_rows, block):
+    seq_index = seq_ref[0]
+    scale = HEAD_DIM ** (-0.5)
+    rows = q_ref.shape[0] // (tok_rows // block)
+    for qb in range(tok_rows // block):
+        width = min(tok_rows, (qb + 1) * block)
+        width = -(-width // 128) * 128
+        q = q_ref[qb * rows : (qb + 1) * rows, :]
+        row_j = qb * block + lax.broadcasted_iota(jnp.int32, (rows, 1), 0) % block
+        query_pos = row_j * shards + seq_index
+        lane_j = lax.broadcasted_iota(jnp.int32, (1, width), 1) * shards
 
-    def add_keys(carry, piece, start):
-        context, top, total = carry
-        key_piece, value_piece = piece
-        number = key_piece.shape[0]
-        index = jnp.arange(number, dtype=jnp.int32)
-        key_pos = (key_base + index % key_rows) * seq_count + index // key_rows
-        allowed = (key_pos[None, :] <= query_pos[:, None])[:, None, :]
-        scores = (
-            jnp.einsum("qhd,kd->qhk", queries, key_piece, preferred_element_type=jnp.float32)
-            * scale
+        def body(src, carry):
+            top, total, context = carry
+            col = pl.multiple_of(src * tok_rows, tok_rows)
+            key_t = kv_ref[:HEAD_DIM, pl.ds(col, width)]
+            value_t = kv_ref[HEAD_DIM:, pl.ds(col, width)]
+            scores = jnp.dot(q, key_t, preferred_element_type=jnp.float32) * scale
+            allowed = (lane_j + src) <= query_pos
+            scores = jnp.where(allowed, scores, masked_score)
+            new_top = jnp.maximum(top, jnp.max(scores, axis=1, keepdims=True))
+            shrink = jnp.exp(top - new_top)
+            weights = jnp.exp(scores - new_top)
+            total = shrink * total + jnp.sum(weights, axis=1, keepdims=True)
+            update = lax.dot_general(
+                weights.astype(jnp.bfloat16),
+                value_t,
+                (((1,), (1,)), ((), ())),
+                preferred_element_type=jnp.float32,
+            )
+            return new_top, total, shrink * context + update
+
+        start = (
+            jnp.full((rows, 1), masked_score, jnp.float32),
+            jnp.zeros((rows, 1), jnp.float32),
+            jnp.zeros((rows, HEAD_DIM), jnp.float32),
         )
-        scores = jnp.where(allowed, scores, masked_score)
-        new_top = jnp.maximum(top, jnp.max(scores, axis=-1))
-        weights = jnp.where(allowed, jnp.exp(scores - new_top[..., None]), 0.0)
-        total = jnp.sum(weights, axis=-1)
-        update = jnp.einsum(
-            "qhk,kd->qhd",
-            weights.astype(jnp.bfloat16),
-            value_piece,
-            preferred_element_type=jnp.float32,
-        )
-        return (update, new_top, total)
-
-    return add_keys
+        top, total, context = lax.fori_loop(0, shards, body, start)
+        o_ref[qb * rows : (qb + 1) * rows, :] = (context / total).astype(o_ref.dtype)
 
 
-def empty_partials(tok_rows, head_count):
+def causal_attention(seq_index, queries, pair_all, block=128):
+    tok_rows, heads_local, _ = queries.shape
+    shards = pair_all.shape[0]
+    blocks = tok_rows // block
+    q_rows = (
+        queries.reshape(blocks, block, heads_local, HEAD_DIM)
+        .transpose(0, 2, 1, 3)
+        .reshape(tok_rows * heads_local, HEAD_DIM)
+    )
+    kv_t = pair_all.reshape(shards * tok_rows, 2 * HEAD_DIM).T
+    out = pl.pallas_call(
+        functools.partial(attention_kernel, shards=shards, tok_rows=tok_rows, block=block),
+        out_shape=jax.ShapeDtypeStruct((tok_rows * heads_local, HEAD_DIM), jnp.bfloat16),
+        in_specs=[
+            pl.BlockSpec(memory_space=pltpu.SMEM),
+            pl.BlockSpec(memory_space=pltpu.VMEM),
+            pl.BlockSpec(memory_space=pltpu.VMEM),
+        ],
+        out_specs=pl.BlockSpec(memory_space=pltpu.VMEM),
+        compiler_params=pltpu.CompilerParams(vmem_limit_bytes=48 * 1024 * 1024),
+        cost_estimate=pl.CostEstimate(
+            flops=4 * tok_rows * heads_local * shards * tok_rows * HEAD_DIM * 3 // 4,
+            transcendentals=tok_rows * heads_local * shards * tok_rows * 3 // 4,
+            bytes_accessed=kv_t.size * 2 + 2 * q_rows.size * 2,
+        ),
+    )(jnp.reshape(seq_index, (1,)).astype(jnp.int32), q_rows, kv_t)
     return (
-        jnp.zeros((tok_rows, head_count, HEAD_DIM), jnp.float32),
-        jnp.full((tok_rows, head_count), masked_score, jnp.float32),
-        jnp.zeros((tok_rows, head_count), jnp.float32),
+        out.reshape(blocks, heads_local, block, HEAD_DIM)
+        .transpose(0, 2, 1, 3)
+        .reshape(tok_rows, 1, heads_local * HEAD_DIM)
     )
 
 
@@ -67,9 +108,10 @@
     tok_rows = 2 * frames_dev * frame_max // 3
     heads_local = GROUP_HEADS // rep_count
     normed = layer_norm(vision_states, norm_gain)
+    frame_rows = lax.all_gather(normed[0], "kvh", axis=0, tiled=False).reshape(1, frame_max, -1)
     hidden = jnp.einsum(
         "frv,vc->frc",
-        lax.all_gather(normed, "kvh", axis=1, tiled=True),
+        frame_rows,
         projector,
         preferred_element_type=jnp.float32,
     )
@@ -105,19 +147,9 @@
     )[0]
     head_rows = summed.astype(jnp.bfloat16)
     queries = head_rows[:, : heads_local * HEAD_DIM].reshape(tok_rows, heads_local, HEAD_DIM)
-    key_own = head_rows[:, heads_local * HEAD_DIM : (heads_local + 1) * HEAD_DIM]
-    value_own = head_rows[:, (heads_local + 1) * HEAD_DIM :]
-    add_keys = attention_step(queries, query_pos, tok_rows, 0, seq_count)
-    context, top, total = add_keys(
-        empty_partials(tok_rows, heads_local),
-        (
-            lax.all_gather(key_own, "seq", axis=0, tiled=True),
-            lax.all_gather(value_own, "seq", axis=0, tiled=True),
-        ),
-        jnp.int32(0),
-    )
-    result = (context / total[..., None]).astype(jnp.bfloat16)
-    return result.reshape(tok_rows, 1, heads_local * HEAD_DIM)
+    pair_own = head_rows[:, heads_local * HEAD_DIM :]
+    pair_all = lax.all_gather(pair_own, "seq", axis=0, tiled=False)
+    return causal_attention(seq_index, queries, pair_all)
 
 
 def solution(mesh):

time: 329 us -> 292 us (0.89)
  Pallas kernels: 0 us -> 56.3 us
  waiting for transfers between devices: 186 us -> 148 us
  matrix products: 43 us -> 6.89 us
  other arithmetic: 26.9 us -> 6.25 us
    pallas_call x0 -> x1, Pallas kernels: none -> 56.3 us  [causal_attention(): pl.pallas_call(functools.partial(attention_kernel, shards=shards, tok_row...]
    all_gather x2 -> x1, waiting for transfers between devices: 130 us -> 92.1 us  [local(): pair_all = lax.all_gather(pair_own, 'seq', axis=0, tiled=False)]
    dot_general x3 -> x1, matrix products: 38.2 us -> 2.12 us  [local(): jnp.einsum('frv,vc->frc', frame_rows, projector, preferred_element_type=j...]
    reduce_sum x1 -> x0, other arithmetic: 16.3 us -> none  [add_keys(): total = jnp.sum(weights, axis=-1)]
    le x1 -> x0, other arithmetic: 4.31 us -> none  [add_keys(): allowed = (key_pos[None, :] <= query_pos[:, None])[:, None, :]]
  transfers between devices with their start and end apart: 4 -> 3, of which waited for: 4 -> 3; matrix products, arithmetic and copies ran while one was open for 15% -> 4% of each run, Pallas kernels for 0% -> 0%
where the time goes in v2:
time: 292 us; the launch traced here: 291 us
  waiting for transfers between devices  148 us (51%)
  Pallas kernels  56.3 us (19%)
  blocking collectives  22 us (8%)
  local copies, waits for them, and re-layouts  21.5 us (7%)
  starting transfers between devices  16.7 us (6%)
  between operations  13.6 us (5%)
  matrix products  6.89 us (2%)
  other arithmetic  6.25 us (2%)
    all_gather x1, waiting for transfers between devices, local(): pair_all = lax.all_gather(pair_own, 'seq', axis=0, tiled=False)  92.1 us
    pallas_call x1, Pallas kernels, causal_attention(): pl.pallas_call(functools.partial(attention_kernel, shards=shards, tok_row...  56.3 us
    reduce_scatter x1, waiting for transfers between devices, local(): lax.psum_scatter(jnp.einsum('tc,cpw->ptw', visual, piece_w, preferred_ele...  51.4 us
    all_gather x1, blocking collectives, local(): lax.all_gather(normed[0], 'kvh', axis=0, tiled=False)  22 us
    all_to_all x1, starting transfers between devices, local(): lax.all_to_all(outgoing, 'seq', split_axis=0, concat_axis=0, tiled=True)  16.6 us
  transfers between devices with their start and end apart: 3, of which 3 were waited for; matrix products, arithmetic and copies ran while one was open for 4% of the time, Pallas kernels for 0%

profile of v2, /device:TPU:1, one launch (start us, length us, event | category | flops | bytes accessed | tf_op | source)
XLA Modules:
  0.0 291.3 jit_solution(5987754186102865771)
XLA Ops:
  6.5 0.0 copy-start
  6.5 1.1 convert_reduce_fusion
  7.7 1.2 fusion.19
  8.9 0.8 copy.34
  9.6 0.1 reduce-window.8
  9.7 0.1 reduce.2
  9.8 0.7 sub.44
  10.5 0.6 dynamic_slice.3
  11.1 0.7 and_select_fusion.1
  11.8 0.1 broadcast_add_fusion
  11.8 0.1 add.124
  12.0 1.1 fusion.21
  13.1 22.0 %all_gather.9 = bf16[4,96,1152]{2,1,0:T(8,128)(2,1)S(1)} all-gather(bf16[1,96,1152]{2,1,0:T(8,128)(2,1)S(1)} %fusion.21), channel_id=1, replica_groups=mesh['seq'=64,'kvh'=4,'rep'=2] {'kvh'}, dimensions={0}, use_global_device_ids=true | all-gather | bytes 1105920 | tf_op jit(solution)/shard_map/all_gather | solution.py:111
  35.2 0.0 copy-done
  35.2 2.1 fusion.9
  37.3 0.2 copy.35
  37.5 2.1 gather_fusion
  39.6 1.0 all_to_all.8
  40.5 16.6 %all-to-all-start = ((bf16[64,6,448]{2,1,0:T(8,128)(2,1)}), bf16[64,6,448]{2,1,0:T(8,128)(2,1)}, u32[]{:S(2)}, u32[]{:S(2)}) async-start(bf16[64,6,448]{2,1,0:T(8,128)(2,1)} %all_to_all.8), calls=%async_computation | async-start | bytes 1048576 | tf_op jit(solution)/shard_map/all_to_all | solution.py:128
  57.2 0.0 reduce-scatter.2.cloned.1.call-start
  57.2 4.6 %copy.30 = bf16[448,3072]{0,1:T(8,128)(2,1)} copy(bf16[448,3072]{1,0:T(8,128)(2,1)} %param.9) | data formatting | bytes 5505024 | tf_op args[4]
  61.8 2.3 slice.21
  64.1 1.8 slice.20
  65.9 0.0 copy-start.1
  65.9 2.4 copy.33
  68.3 1.5 copy.32
  69.7 0.0 copy-done.1
  69.7 0.1 fusion.24
  69.9 4.5 %all-to-all-done = bf16[64,6,448]{2,1,0:T(8,128)(2,1)} async-done(((bf16[64,6,448]{2,1,0:T(8,128)(2,1)}), bf16[64,6,448]{2,1,0:T(8,128)(2,1)}, u32[]{:S(2)}, u32[]{:S(2)}) %all-to-all-start) | async-done | bytes 344096 | tf_op jit(solution)/shard_map/all_to_all | solution.py:128
  74.4 1.3 all_to_all.10
  75.7 1.2 gather_fusion.1
  76.8 0.1 broadcast_in_dim.13
  77.0 4.8 %fusion.4 = f32[8,256,512]{1,2,0:T(8,128)} fusion(bf16[448,8,256]{2,0,1:T(8,128)(2,1)S(1)} %bitcast.38, bf16[448,8,256]{2,0,1:T(8,128)(2,1)} %copy.33, bf16[256,448]{1,0:T(8,128)(2,1)S(1)} %gather_fusion.1), kind=kOutput, calls=%fused_computation.6 | convolution fusion | flops 946864128 | bytes 8093696 | tf_op jit(solution)/shard_map/tc,cpw->ptw/dot_general | solution.py:143
  81.7 0.0 reduce-scatter.2.cloned.1.call-update
  81.8 0.0 all-gather.3.cloned.1.call-start
  81.8 51.4 %reduce-scatter.2.cloned.1.call-done = f32[1,256,512]{1,2,0:T(8,128)} async-done(((f32[8,256,512]{1,2,0:T(8,128)}), f32[1,256,512]{1,2,0:T(8,128)}) %reduce-scatter.2.cloned.1.call-update) | async-done | bytes 524304 | tf_op jit(solution)/shard_map/reduce_scatter | solution.py:142
  133.2 1.1 convert_bitcast_fusion
  134.3 0.7 fusion.28
  135.0 0.0 all-gather.3.cloned.1.call-update
  135.0 0.1 copy.37
  135.2 92.1 %all-gather.3.cloned.1.call-done = bf16[16384,256]{0,1:T(8,128)(2,1)} async-done(((bf16[256,256]{0,1:T(8,128)(2,1)}), bf16[16384,256]{0,1:T(8,128)(2,1)}) %all-gather.3.cloned.1.call-update) | async-done | bytes 8388624 | tf_op jit(solution)/shard_map/all_gather | solution.py:151
  227.2 56.3 %shard_map.55 = bf16[512,128]{1,0:T(8,128)(2,1)S(1)} custom-call(s32[1]{0:T(128)} %bitcast.seq_ref, bf16[512,128]{1,0:T(8,128)(2,1)S(1)} %bitcast.32, bf16[256,16384]{1,0:T(8,128)(2,1)} %bitcast.45), custom_call_target="tpu_custom_call" | custom-call | flops 3221225472 | bytes 8650752 | tf_op jit(solution)/shard_map/pallas_call | solution.py:77
  283.5 0.1 copy.38
  283.7 0.7 reshape.317
  (10 shorter events, 0.1 us)
Async XLA Ops:
  6.5 28.6 %copy-start = (bf16[1152,448]{0,1:T(8,128)(2,1)S(1)}, bf16[1152,448]{0,1:T(8,128)(2,1)}, u32[]{:S(2)}) copy-start(bf16[1152,448]{0,1:T(8,128)(2,1)} %param.8) | copy-start | bytes 3096580
  40.5 33.9 %all-to-all-start = ((bf16[64,6,448]{2,1,0:T(8,128)(2,1)}), bf16[64,6,448]{2,1,0:T(8,128)(2,1)}, u32[]{:S(2)}, u32[]{:S(2)}) async-start(bf16[64,6,448]{2,1,0:T(8,128)(2,1)} %all_to_all.8), calls=%async_computation | async-start | bytes 1048576 | tf_op jit(solution)/shard_map/all_to_all | solution.py:128
  57.2 76.0 %reduce-scatter.2.cloned.1.call-start = ((), (), s32[]{:S(2)}) async-start(), calls=%async_computation.2 | async-start | bytes 4718592 | tf_op jit(solution)/shard_map/reduce_scatter | solution.py:142
  65.9 3.9 %copy-start.1 = (s32[64]{0:T(128)S(1)}, s32[64]{0:T(128)}, u32[]{:S(2)}) copy-start(s32[64]{0:T(128)} %param.6) | copy-start | bytes 772
  81.8 145.4 %all-gather.3.cloned.1.call-start = ((), (), s32[]{:S(2)}) async-start(), calls=%async_computation.3 | async-start | bytes 8519680 | tf_op jit(solution)/shard_map/all_gather | solution.py:151
Sparse Core Ops, SparseCore 0:
  81.9 51.2 reduce-scatter.1
  136.3 90.8 all-gather.2

commit v3 on v2

--- a/solution.py
+++ b/solution.py
@@ -14,6 +14,7 @@
 
 norm_eps = 1e-06
 masked_score = -1e30
+UNROLL = 8
 
 
 def layer_norm(states, norm_gain):
@@ -28,12 +29,11 @@
     scale = HEAD_DIM ** (-0.5)
     rows = q_ref.shape[0] // (tok_rows // block)
     for qb in range(tok_rows // block):
-        width = min(tok_rows, (qb + 1) * block)
-        width = -(-width // 128) * 128
+        width = (((qb + 1) * block - 1) // 128 + 1) * 128
         q = q_ref[qb * rows : (qb + 1) * rows, :]
         row_j = qb * block + lax.broadcasted_iota(jnp.int32, (rows, 1), 0) % block
         query_pos = row_j * shards + seq_index
-        lane_j = lax.broadcasted_iota(jnp.int32, (1, width), 1) * shards
+        lane_pos = lax.broadcasted_iota(jnp.int32, (1, width), 1) * shards
 
         def body(src, carry):
             top, total, context = carry
@@ -41,7 +41,7 @@
             key_t = kv_ref[:HEAD_DIM, pl.ds(col, width)]
             value_t = kv_ref[HEAD_DIM:, pl.ds(col, width)]
             scores = jnp.dot(q, key_t, preferred_element_type=jnp.float32) * scale
-            allowed = (lane_j + src) <= query_pos
+            allowed = lane_pos <= query_pos - src
             scores = jnp.where(allowed, scores, masked_score)
             new_top = jnp.maximum(top, jnp.max(scores, axis=1, keepdims=True))
             shrink = jnp.exp(top - new_top)
@@ -60,7 +60,7 @@
             jnp.zeros((rows, 1), jnp.float32),
             jnp.zeros((rows, HEAD_DIM), jnp.float32),
         )
-        top, total, context = lax.fori_loop(0, shards, body, start)
+        top, total, context = lax.fori_loop(0, shards, body, start, unroll=UNROLL)
         o_ref[qb * rows : (qb + 1) * rows, :] = (context / total).astype(o_ref.dtype)
 
 

time: 292 us -> 257 us (0.88)
  Pallas kernels: 56.3 us -> 21.1 us
    pallas_call x1, Pallas kernels: 56.3 us -> 21.1 us  [causal_attention(): pl.pallas_call(functools.partial(attention_kernel, shards=shards, tok_row...]
  transfers between devices with their start and end apart: 3 -> 3, of which waited for: 3 -> 3; matrix products, arithmetic and copies ran while one was open for 4% -> 5% of each run, Pallas kernels for 0% -> 0%
where the time goes in v3:
time: 257 us; the launch traced here: 256 us
  waiting for transfers between devices  148 us (58%)
  blocking collectives  22 us (9%)
  local copies, waits for them, and re-layouts  21.5 us (8%)
  Pallas kernels  21.1 us (8%)
  starting transfers between devices  16.7 us (6%)
  between operations  13.6 us (5%)
  matrix products  6.89 us (3%)
  other arithmetic  6.25 us (2%)
    all_gather x1, waiting for transfers between devices, local(): pair_all = lax.all_gather(pair_own, 'seq', axis=0, tiled=False)  92.1 us
    reduce_scatter x1, waiting for transfers between devices, local(): lax.psum_scatter(jnp.einsum('tc,cpw->ptw', visual, piece_w, preferred_ele...  51.4 us
    all_gather x1, blocking collectives, local(): lax.all_gather(normed[0], 'kvh', axis=0, tiled=False)  22 us
    pallas_call x1, Pallas kernels, causal_attention(): pl.pallas_call(functools.partial(attention_kernel, shards=shards, tok_row...  21.1 us
    all_to_all x1, starting transfers between devices, local(): lax.all_to_all(outgoing, 'seq', split_axis=0, concat_axis=0, tiled=True)  16.6 us
  transfers between devices with their start and end apart: 3, of which 3 were waited for; matrix products, arithmetic and copies ran while one was open for 5% of the time, Pallas kernels for 0%

profile of v3, /device:TPU:1, one launch (start us, length us, event | category | flops | bytes accessed | tf_op | source)
XLA Modules:
  0.0 256.0 jit_solution(10322525785480633183)
XLA Ops:
  6.5 0.0 copy-start
  6.5 1.1 convert_reduce_fusion
  7.7 1.2 fusion.19
  8.9 0.8 copy.34
  9.6 0.1 reduce-window.8
  9.7 0.1 reduce.2
  9.8 0.7 sub.44
  10.5 0.6 dynamic_slice.3
  11.1 0.7 and_select_fusion.1
  11.8 0.1 broadcast_add_fusion
  11.8 0.1 add.124
  12.0 1.1 fusion.21
  13.1 22.0 %all_gather.9 = bf16[4,96,1152]{2,1,0:T(8,128)(2,1)S(1)} all-gather(bf16[1,96,1152]{2,1,0:T(8,128)(2,1)S(1)} %fusion.21), channel_id=1, replica_groups=mesh['seq'=64,'kvh'=4,'rep'=2] {'kvh'}, dimensions={0}, use_global_device_ids=true | all-gather | bytes 1105920 | tf_op jit(solution)/shard_map/all_gather | solution.py:111
  35.2 0.0 copy-done
  35.2 2.1 fusion.9
  37.3 0.2 copy.35
  37.5 2.1 gather_fusion
  39.6 1.0 all_to_all.8
  40.5 16.6 %all-to-all-start = ((bf16[64,6,448]{2,1,0:T(8,128)(2,1)}), bf16[64,6,448]{2,1,0:T(8,128)(2,1)}, u32[]{:S(2)}, u32[]{:S(2)}) async-start(bf16[64,6,448]{2,1,0:T(8,128)(2,1)} %all_to_all.8), calls=%async_computation | async-start | bytes 1048576 | tf_op jit(solution)/shard_map/all_to_all | solution.py:128
  57.2 0.0 reduce-scatter.2.cloned.1.call-start
  57.2 4.6 %copy.30 = bf16[448,3072]{0,1:T(8,128)(2,1)} copy(bf16[448,3072]{1,0:T(8,128)(2,1)} %param.9) | data formatting | bytes 5505024 | tf_op args[4]
  61.8 2.3 slice.21
  64.1 1.8 slice.20
  65.9 0.0 copy-start.1
  65.9 2.4 copy.33
  68.3 1.5 copy.32
  69.7 0.0 copy-done.1
  69.7 0.1 fusion.24
  69.9 4.5 %all-to-all-done = bf16[64,6,448]{2,1,0:T(8,128)(2,1)} async-done(((bf16[64,6,448]{2,1,0:T(8,128)(2,1)}), bf16[64,6,448]{2,1,0:T(8,128)(2,1)}, u32[]{:S(2)}, u32[]{:S(2)}) %all-to-all-start) | async-done | bytes 344096 | tf_op jit(solution)/shard_map/all_to_all | solution.py:128
  74.4 1.3 all_to_all.10
  75.7 1.2 gather_fusion.1
  76.8 0.1 broadcast_in_dim.13
  77.0 4.8 %fusion.4 = f32[8,256,512]{1,2,0:T(8,128)} fusion(bf16[448,8,256]{2,0,1:T(8,128)(2,1)S(1)} %bitcast.38, bf16[448,8,256]{2,0,1:T(8,128)(2,1)} %copy.33, bf16[256,448]{1,0:T(8,128)(2,1)S(1)} %gather_fusion.1), kind=kOutput, calls=%fused_computation.6 | convolution fusion | flops 946864128 | bytes 8093696 | tf_op jit(solution)/shard_map/tc,cpw->ptw/dot_general | solution.py:143
  81.7 0.0 reduce-scatter.2.cloned.1.call-update
  81.8 0.0 all-gather.3.cloned.1.call-start
  81.8 51.4 %reduce-scatter.2.cloned.1.call-done = f32[1,256,512]{1,2,0:T(8,128)} async-done(((f32[8,256,512]{1,2,0:T(8,128)}), f32[1,256,512]{1,2,0:T(8,128)}) %reduce-scatter.2.cloned.1.call-update) | async-done | bytes 524304 | tf_op jit(solution)/shard_map/reduce_scatter | solution.py:142
  133.2 1.1 convert_bitcast_fusion
  134.3 0.7 fusion.28
  135.0 0.0 all-gather.3.cloned.1.call-update
  135.0 0.1 copy.37
  135.2 92.1 %all-gather.3.cloned.1.call-done = bf16[16384,256]{0,1:T(8,128)(2,1)} async-done(((bf16[256,256]{0,1:T(8,128)(2,1)}), bf16[16384,256]{0,1:T(8,128)(2,1)}) %all-gather.3.cloned.1.call-update) | async-done | bytes 8388624 | tf_op jit(solution)/shard_map/all_gather | solution.py:151
  227.2 21.1 %shard_map.55 = bf16[512,128]{1,0:T(8,128)(2,1)S(1)} custom-call(s32[1]{0:T(128)} %bitcast.seq_ref, bf16[512,128]{1,0:T(8,128)(2,1)S(1)} %bitcast.32, bf16[256,16384]{1,0:T(8,128)(2,1)} %bitcast.45), custom_call_target="tpu_custom_call" | custom-call | flops 3221225472 | bytes 8650752 | tf_op jit(solution)/shard_map/pallas_call | solution.py:77
  248.3 0.1 copy.38
  248.4 0.7 reshape.317
  (10 shorter events, 0.1 us)
Async XLA Ops:
  6.5 28.6 %copy-start = (bf16[1152,448]{0,1:T(8,128)(2,1)S(1)}, bf16[1152,448]{0,1:T(8,128)(2,1)}, u32[]{:S(2)}) copy-start(bf16[1152,448]{0,1:T(8,128)(2,1)} %param.8) | copy-start | bytes 3096580
  40.5 33.9 %all-to-all-start = ((bf16[64,6,448]{2,1,0:T(8,128)(2,1)}), bf16[64,6,448]{2,1,0:T(8,128)(2,1)}, u32[]{:S(2)}, u32[]{:S(2)}) async-start(bf16[64,6,448]{2,1,0:T(8,128)(2,1)} %all_to_all.8), calls=%async_computation | async-start | bytes 1048576 | tf_op jit(solution)/shard_map/all_to_all | solution.py:128
  57.2 76.0 %reduce-scatter.2.cloned.1.call-start = ((), (), s32[]{:S(2)}) async-start(), calls=%async_computation.2 | async-start | bytes 4718592 | tf_op jit(solution)/shard_map/reduce_scatter | solution.py:142
  65.9 3.9 %copy-start.1 = (s32[64]{0:T(128)S(1)}, s32[64]{0:T(128)}, u32[]{:S(2)}) copy-start(s32[64]{0:T(128)} %param.6) | copy-start | bytes 772
  81.8 145.4 %all-gather.3.cloned.1.call-start = ((), (), s32[]{:S(2)}) async-start(), calls=%async_computation.3 | async-start | bytes 8519680 | tf_op jit(solution)/shard_map/all_gather | solution.py:151
Sparse Core Ops, SparseCore 0:
  81.9 51.2 reduce-scatter.1
  136.3 90.8 all-gather.2

commit v4 on v3

--- a/solution.py
+++ b/solution.py
@@ -97,6 +97,23 @@
     )
 
 
+def ring_reduce_scatter(parts):
+    count = parts.shape[0]
+    axes = ("kvh", "rep")
+    index = lax.axis_index("kvh") * lax.axis_size("rep") + lax.axis_index("rep")
+    half = parts.shape[-1] // 2
+    sums = []
+    for step_dir, piece in ((1, parts[..., :half]), (-1, parts[..., half:])):
+        perm = [(i, (i + step_dir) % count) for i in range(count)]
+        buf = lax.dynamic_index_in_dim(piece, (index - step_dir) % count, 0, keepdims=False)
+        for t in range(1, count):
+            buf = lax.ppermute(buf, axes, perm)
+            own = lax.dynamic_index_in_dim(piece, (index - step_dir * (t + 1)) % count, 0, keepdims=False)
+            buf = buf + own
+        sums.append(buf)
+    return jnp.concatenate(sums, axis=-1)
+
+
 def local(vision_states, frame_tokens, norm_gain, projector, head_weights):
     seq_count = lax.axis_size("seq")
     seq_index = lax.axis_index("seq")
@@ -133,21 +150,18 @@
     slot_index = frame * cap_frame + (query_pos - offset) // seq_count
     visual = received[slot_index]
     wide = head_weights.reshape(d_cols, KV_HEADS, GROUP_HEADS + 2, HEAD_DIM)
-    query_w = wide[:, :, :GROUP_HEADS].reshape(d_cols, KV_HEADS, rep_count, heads_local * HEAD_DIM)
-    pair_w = wide[:, :, GROUP_HEADS:].reshape(d_cols, KV_HEADS, 1, 2 * HEAD_DIM)
-    pair_w = jnp.broadcast_to(pair_w, (d_cols, KV_HEADS, rep_count, 2 * HEAD_DIM))
-    piece_w = jnp.concatenate([query_w, pair_w], axis=3).reshape(
-        d_cols, KV_HEADS * rep_count, (heads_local + 2) * HEAD_DIM
-    )
-    summed = lax.psum_scatter(
-        jnp.einsum("tc,cpw->ptw", visual, piece_w, preferred_element_type=jnp.float32),
-        ("kvh", "rep"),
-        scatter_dimension=0,
-        tiled=True,
-    )[0]
-    head_rows = summed.astype(jnp.bfloat16)
-    queries = head_rows[:, : heads_local * HEAD_DIM].reshape(tok_rows, heads_local, HEAD_DIM)
-    pair_own = head_rows[:, heads_local * HEAD_DIM :]
+    query_w = wide[:, :, :GROUP_HEADS].reshape(d_cols, KV_HEADS * rep_count, heads_local * HEAD_DIM)
+    pair_w = wide[:, :, GROUP_HEADS:].reshape(d_cols, KV_HEADS, 2 * HEAD_DIM)
+    pair_part = jnp.einsum("tc,cgw->gtw", visual, pair_w, preferred_element_type=jnp.float32)
+    pair_part = jnp.broadcast_to(
+        pair_part[:, None], (KV_HEADS, rep_count) + pair_part.shape[1:]
+    ).reshape((KV_HEADS * rep_count,) + pair_part.shape[1:])
+    pair_own = lax.psum_scatter(
+        pair_part, ("kvh", "rep"), scatter_dimension=0, tiled=True
+    )[0].astype(jnp.bfloat16)
+    query_part = jnp.einsum("tc,cpw->ptw", visual, query_w, preferred_element_type=jnp.float32)
+    queries = ring_reduce_scatter(query_part).astype(jnp.bfloat16)
+    queries = queries.reshape(tok_rows, heads_local, HEAD_DIM)
     pair_all = lax.all_gather(pair_own, "seq", axis=0, tiled=False)
     return causal_attention(seq_index, queries, pair_all)
 

time: 257 us -> 250 us (0.973)
  waiting for transfers between devices: 148 us -> 88.1 us
  starting transfers between devices: 16.7 us -> 63.5 us
  local copies, waits for them, and re-layouts: 21.5 us -> 30 us
  matrix products: 6.89 us -> 3.34 us
    all_gather x1, waiting for transfers between devices: 92.1 us -> 37.5 us  [local(): pair_all = lax.all_gather(pair_own, 'seq', axis=0, tiled=False)]
    ppermute x0 -> x14, starting transfers between devices: none -> 47 us  [ring_reduce_scatter(): buf = lax.ppermute(buf, axes, perm)]
    reduce_scatter x1, waiting for transfers between devices: 51.4 us -> 34.1 us  [local(): lax.psum_scatter(pair_part, ('kvh', 'rep'), scatter_dimension=0, tiled=True)]
    reshape x0 -> x1, local copies, waits for them, and re-layouts: none -> 11.8 us  [causal_attention(): kv_t = pair_all.reshape(shards * tok_rows, 2 * HEAD_DIM).T]
    all_to_all x1, waiting for transfers between devices: 4.51 us -> 11.1 us  [local(): lax.all_to_all(outgoing, 'seq', split_axis=0, concat_axis=0, tiled=True)]
    ppermute x0 -> x14, waiting for transfers between devices: none -> 5.3 us  [ring_reduce_scatter(): buf = lax.ppermute(buf, axes, perm)]
    dot_general x1 -> x2, matrix products: 4.76 us -> 1.22 us  [the longest x1 0.74 us: local(): jnp.einsum('tc,cpw->ptw', visual, query_w, preferred_element_type=jnp.flo...]
  transfers between devices with their start and end apart: 3 -> 17, of which waited for: 3 -> 11; matrix products, arithmetic and copies ran while one was open for 5% -> 4% of each run, Pallas kernels for 0% -> 0%
where the time goes in v4:
time: 250 us; the launch traced here: 249 us
  waiting for transfers between devices  88.1 us (35%)
  starting transfers between devices  63.5 us (25%)
  local copies, waits for them, and re-layouts  30 us (12%)
  blocking collectives  22 us (9%)
  Pallas kernels  21.1 us (8%)
  between operations  14.3 us (6%)
  other arithmetic  7.08 us (3%)
  matrix products  3.34 us (1%)
    ppermute x14, starting transfers between devices, ring_reduce_scatter(): buf = lax.ppermute(buf, axes, perm)  47 us
    all_gather x1, waiting for transfers between devices, local(): pair_all = lax.all_gather(pair_own, 'seq', axis=0, tiled=False)  37.5 us
    reduce_scatter x1, waiting for transfers between devices, local(): lax.psum_scatter(pair_part, ('kvh', 'rep'), scatter_dimension=0, tiled=True)  34.1 us
    all_gather x1, blocking collectives, local(): lax.all_gather(normed[0], 'kvh', axis=0, tiled=False)  22 us
    pallas_call x1, Pallas kernels, causal_attention(): pl.pallas_call(functools.partial(attention_kernel, shards=shards, tok_row...  21.1 us
    all_to_all x1, starting transfers between devices, local(): lax.all_to_all(outgoing, 'seq', split_axis=0, concat_axis=0, tiled=True)  16.4 us
    reshape x1, local copies, waits for them, and re-layouts, causal_attention(): kv_t = pair_all.reshape(shards * tok_rows, 2 * HEAD_DIM).T  11.8 us
    all_to_all x1, waiting for transfers between devices, local(): lax.all_to_all(outgoing, 'seq', split_axis=0, concat_axis=0, tiled=True)  11.1 us
  transfers between devices with their start and end apart: 17, of which 11 were waited for; matrix products, arithmetic and copies ran while one was open for 4% of the time, Pallas kernels for 0%

profile of v4, /device:TPU:1, one launch (start us, length us, event | category | flops | bytes accessed | tf_op | source)
XLA Modules:
  0.0 249.3 jit_solution(14717623966116384006)
XLA Ops:
  6.5 1.1 convert_reduce_fusion
  7.7 1.2 fusion.12
  8.9 0.8 copy.78
  9.8 0.7 sub.92
  10.5 0.6 dynamic_slice.52
  11.1 0.7 and_select_fusion.1
  12.0 1.1 fusion.14
  13.1 22.0 %all_gather.7 = bf16[4,96,1152]{2,1,0:T(8,128)(2,1)S(1)} all-gather(bf16[1,96,1152]{2,1,0:T(8,128)(2,1)S(1)} %fusion.14), channel_id=1, replica_groups=mesh['seq'=64,'kvh'=4,'rep'=2] {'kvh'}, dimensions={0}, use_global_device_ids=true | all-gather | bytes 1105920 | tf_op jit(solution)/shard_map/all_gather | solution.py:128
  35.2 2.1 fusion.2
  37.5 2.1 gather_fusion
  39.5 1.0 all_to_all.8
  40.5 16.4 %all-to-all-start = ((bf16[64,6,448]{2,1,0:T(8,128)(2,1)}), bf16[64,6,448]{2,1,0:T(8,128)(2,1)S(1)}, u32[]{:S(2)}, u32[]{:S(2)}) async-start(bf16[64,6,448]{2,1,0:T(8,128)(2,1)} %all_to_all.8), calls=%async_computation | async-start | bytes 1048576 | tf_op jit(solution)/shard_map/all_to_all | solution.py:145
  57.0 4.6 %copy.80 = bf16[448,3072]{0,1:T(8,128)(2,1)} copy(bf16[448,3072]{1,0:T(8,128)(2,1)} %param.9) | data formatting | bytes 5505024 | tf_op args[4]
  61.6 1.3 slice.23
  63.2 11.1 %all-to-all-done = bf16[64,6,448]{2,1,0:T(8,128)(2,1)S(1)} async-done(((bf16[64,6,448]{2,1,0:T(8,128)(2,1)}), bf16[64,6,448]{2,1,0:T(8,128)(2,1)S(1)}, u32[]{:S(2)}, u32[]{:S(2)}) %all-to-all-start) | async-done | bytes 344096 | tf_op jit(solution)/shard_map/all_to_all | solution.py:145
  74.3 0.2 all_to_all.10
  74.5 1.2 gather_fusion.1
  75.7 0.5 convolution_bitcast_fusion.1
  76.2 1.5 broadcast_in_dim.12
  77.8 34.1 %reduce-scatter.2.cloned.1.call-done = f32[1,256,256]{2,1,0:T(8,128)} async-done(((f32[8,256,256]{2,1,0:T(8,128)}), f32[1,256,256]{2,1,0:T(8,128)}) %reduce-scatter.2.cloned.1.call-update) | async-done | bytes 262160 | tf_op jit(solution)/shard_map/reduce_scatter | solution.py:159
  111.9 1.6 convert_element_type.27
  113.8 1.8 slice.20
  115.7 0.7 convolution_bitcast_fusion
  116.6 0.2 constant_dynamic-slice_fusion
  116.9 2.4 collective-permute-start
  120.8 4.1 %collective-permute-start.7 = (f32[256,128]{1,0:T(8,128)S(1)}, f32[256,128]{1,0:T(8,128)S(1)}, u32[]{:S(2)}, u32[]{:S(2)}) collective-permute-start(f32[256,128]{1,0:T(8,128)S(1)} %bitcast.82), channel_id=1, source_target_pairs={{0,7},{1,0},{2,1},{3,2},{4,3},{5,4},{6,5},{7,6},{8,15},{9,8},{10,9... | collective-permute-start | bytes 393224 | tf_op jit(solution)/shard_map/ppermute | solution.py:110
  125.0 1.9 collective-permute-start.1
  127.0 4.9 %collective-permute-start.8 = (f32[256,128]{1,0:T(8,128)S(1)}, f32[256,128]{1,0:T(8,128)S(1)}, u32[]{:S(2)}, u32[]{:S(2)}) collective-permute-start(f32[256,128]{1,0:T(8,128)S(1)} %bitcast_add_fusion.6), channel_id=1, source_target_pairs={{0,7},{1,0},{2,1},{3,2},{4,3},{5,4},{6,5},{7,6},{8,15},{9,8},{10,9... | collective-permute-start | bytes 393224 | tf_op jit(solution)/shard_map/ppermute | solution.py:110
  131.9 1.9 collective-permute-start.2
  133.9 0.3 collective-permute-done.8
  134.2 4.7 %collective-permute-start.9 = (f32[256,128]{1,0:T(8,128)S(1)}, f32[256,128]{1,0:T(8,128)S(1)}, u32[]{:S(2)}, u32[]{:S(2)}) collective-permute-start(f32[256,128]{1,0:T(8,128)S(1)} %bitcast_add_fusion.5), channel_id=1, source_target_pairs={{0,7},{1,0},{2,1},{3,2},{4,3},{5,4},{6,5},{7,6},{8,15},{9,8},{10,9... | collective-permute-start | bytes 393224 | tf_op jit(solution)/shard_map/ppermute | solution.py:110
  139.1 1.9 collective-permute-start.3
  141.0 0.8 collective-permute-done.9
  141.8 5.0 %collective-permute-start.10 = (f32[256,128]{1,0:T(8,128)S(1)}, f32[256,128]{1,0:T(8,128)S(1)}, u32[]{:S(2)}, u32[]{:S(2)}) collective-permute-start(f32[256,128]{1,0:T(8,128)S(1)} %bitcast_add_fusion.4), channel_id=1, source_target_pairs={{0,7},{1,0},{2,1},{3,2},{4,3},{5,4},{6,5},{7,6},{8,15},{9,8},{10,9... | collective-permute-start | bytes 393224 | tf_op jit(solution)/shard_map/ppermute | solution.py:110
  146.9 0.8 collective-permute-done.3
  147.7 1.9 collective-permute-start.4
  149.6 5.0 %collective-permute-start.11 = (f32[256,128]{1,0:T(8,128)S(1)}, f32[256,128]{1,0:T(8,128)S(1)}, u32[]{:S(2)}, u32[]{:S(2)}) collective-permute-start(f32[256,128]{1,0:T(8,128)S(1)} %bitcast_add_fusion.3), channel_id=1, source_target_pairs={{0,7},{1,0},{2,1},{3,2},{4,3},{5,4},{6,5},{7,6},{8,15},{9,8},{10,9... | collective-permute-start | bytes 393224 | tf_op jit(solution)/shard_map/ppermute | solution.py:110
  154.7 1.1 collective-permute-done.4
  155.8 1.9 collective-permute-start.5
  157.7 4.6 %collective-permute-start.12 = (f32[256,128]{1,0:T(8,128)S(1)}, f32[256,128]{1,0:T(8,128)S(1)}, u32[]{:S(2)}, u32[]{:S(2)}) collective-permute-start(f32[256,128]{1,0:T(8,128)S(1)} %bitcast_add_fusion.2), channel_id=1, source_target_pairs={{0,7},{1,0},{2,1},{3,2},{4,3},{5,4},{6,5},{7,6},{8,15},{9,8},{10,9... | collective-permute-start | bytes 393224 | tf_op jit(solution)/shard_map/ppermute | solution.py:110
  162.3 0.4 collective-permute-done.5
  162.7 1.9 collective-permute-start.6
  164.7 4.8 %collective-permute-start.13 = (f32[256,128]{1,0:T(8,128)S(1)}, f32[256,128]{1,0:T(8,128)S(1)}, u32[]{:S(2)}, u32[]{:S(2)}) collective-permute-start(f32[256,128]{1,0:T(8,128)S(1)} %bitcast_add_fusion.1), channel_id=1, source_target_pairs={{0,7},{1,0},{2,1},{3,2},{4,3},{5,4},{6,5},{7,6},{8,15},{9,8},{10,9... | collective-permute-start | bytes 393224 | tf_op jit(solution)/shard_map/ppermute | solution.py:110
  169.6 1.5 collective-permute-done.13
  171.3 37.5 %all-gather.2.cloned.1.call-done = bf16[64,256,256]{2,1,0:T(8,128)(2,1)} async-done(((bf16[1,256,256]{2,1,0:T(8,128)(2,1)}), bf16[64,256,256]{2,1,0:T(8,128)(2,1)}) %all-gather.2.cloned.1.call-update) | async-done | bytes 8388624 | tf_op jit(solution)/shard_map/all_gather | solution.py:165
  208.7 11.8 %copy.112 = bf16[16384,256]{0,1:T(8,128)(2,1)} copy(bf16[16384,256]{1,0:T(8,128)(2,1)} %bitcast.74) | data formatting | bytes 16777216 | tf_op jit(solution)/shard_map/reshape | solution.py:76
  220.5 21.1 %shard_map.55 = bf16[512,128]{1,0:T(8,128)(2,1)S(1)} custom-call(s32[1]{0:T(128)} %bitcast.seq_ref, bf16[512,128]{1,0:T(8,128)(2,1)S(1)} %bitcast.70, bf16[256,16384]{1,0:T(8,128)(2,1)} %bitcast.75), custom_call_target="tpu_custom_call" | custom-call | flops 3221225472 | bytes 8650752 | tf_op jit(solution)/shard_map/pallas_call | solution.py:77
  241.8 0.7 reshape.324
  (66 shorter events, 3.4 us)
Async XLA Ops:
  6.5 28.6 %copy-start = (bf16[1152,448]{0,1:T(8,128)(2,1)S(1)}, bf16[1152,448]{0,1:T(8,128)(2,1)}, u32[]{:S(2)}) copy-start(bf16[1152,448]{0,1:T(8,128)(2,1)} %param.8) | copy-start | bytes 3096580
  40.5 33.8 %all-to-all-start = ((bf16[64,6,448]{2,1,0:T(8,128)(2,1)}), bf16[64,6,448]{2,1,0:T(8,128)(2,1)S(1)}, u32[]{:S(2)}, u32[]{:S(2)}) async-start(bf16[64,6,448]{2,1,0:T(8,128)(2,1)} %all_to_all.8), calls=%async_computation | async-start | bytes 1048576 | tf_op jit(solution)/shard_map/all_to_all | solution.py:145
  57.0 54.9 %reduce-scatter.2.cloned.1.call-start = ((), (), s32[]{:S(2)}) async-start(), calls=%async_computation.2 | async-start | bytes 2359296 | tf_op jit(solution)/shard_map/reduce_scatter | solution.py:159
  61.6 1.4 copy-start.1
  77.7 131.0 %all-gather.2.cloned.1.call-start = ((), (), s32[]{:S(2)}) async-start(), calls=%async_computation.3 | async-start | bytes 8519680 | tf_op jit(solution)/shard_map/all_gather | solution.py:165
  116.9 8.0 %collective-permute-start = (f32[256,128]{1,0:T(8,128)S(1)}, f32[256,128]{1,0:T(8,128)S(1)}, u32[]{:S(2)}, u32[]{:S(2)}) collective-permute-start(f32[256,128]{1,0:T(8,128)S(1)} %bitcast.81), channel_id=1, source_target_pairs={{0,1},{1,2},{2,3},{3,4},{4,5},{5,6},{6,7},{7,0},{8,9},{9,10},{10,1... | collective-permute-start | bytes 393224 | tf_op jit(solution)/shard_map/ppermute | solution.py:110
  120.8 6.1 %collective-permute-start.7 = (f32[256,128]{1,0:T(8,128)S(1)}, f32[256,128]{1,0:T(8,128)S(1)}, u32[]{:S(2)}, u32[]{:S(2)}) collective-permute-start(f32[256,128]{1,0:T(8,128)S(1)} %bitcast.82), channel_id=1, source_target_pairs={{0,7},{1,0},{2,1},{3,2},{4,3},{5,4},{6,5},{7,6},{8,15},{9,8},{10,9... | collective-permute-start | bytes 393224 | tf_op jit(solution)/shard_map/ppermute | solution.py:110
  125.0 6.9 %collective-permute-start.1 = (f32[256,128]{1,0:T(8,128)S(1)}, f32[256,128]{1,0:T(8,128)S(1)}, u32[]{:S(2)}, u32[]{:S(2)}) collective-permute-start(f32[256,128]{1,0:T(8,128)S(1)} %bitcast_add_fusion.13), channel_id=1, source_target_pairs={{0,1},{1,2},{2,3},{3,4},{4,5},{5,6},{6,7},{7,0},{8,9},{9,10},{10,1... | collective-permute-start | bytes 393224 | tf_op jit(solution)/shard_map/ppermute | solution.py:110
  127.0 7.2 %collective-permute-start.8 = (f32[256,128]{1,0:T(8,128)S(1)}, f32[256,128]{1,0:T(8,128)S(1)}, u32[]{:S(2)}, u32[]{:S(2)}) collective-permute-start(f32[256,128]{1,0:T(8,128)S(1)} %bitcast_add_fusion.6), channel_id=1, source_target_pairs={{0,7},{1,0},{2,1},{3,2},{4,3},{5,4},{6,5},{7,6},{8,15},{9,8},{10,9... | collective-permute-start | bytes 393224 | tf_op jit(solution)/shard_map/ppermute | solution.py:110
  131.9 7.1 %collective-permute-start.2 = (f32[256,128]{1,0:T(8,128)S(1)}, f32[256,128]{1,0:T(8,128)S(1)}, u32[]{:S(2)}, u32[]{:S(2)}) collective-permute-start(f32[256,128]{1,0:T(8,128)S(1)} %bitcast_add_fusion.12), channel_id=1, source_target_pairs={{0,1},{1,2},{2,3},{3,4},{4,5},{5,6},{6,7},{7,0},{8,9},{9,10},{10,1... | collective-permute-start | bytes 393224 | tf_op jit(solution)/shard_map/ppermute | solution.py:110
  134.2 7.6 %collective-permute-start.9 = (f32[256,128]{1,0:T(8,128)S(1)}, f32[256,128]{1,0:T(8,128)S(1)}, u32[]{:S(2)}, u32[]{:S(2)}) collective-permute-start(f32[256,128]{1,0:T(8,128)S(1)} %bitcast_add_fusion.5), channel_id=1, source_target_pairs={{0,7},{1,0},{2,1},{3,2},{4,3},{5,4},{6,5},{7,6},{8,15},{9,8},{10,9... | collective-permute-start | bytes 393224 | tf_op jit(solution)/shard_map/ppermute | solution.py:110
  139.1 8.6 %collective-permute-start.3 = (f32[256,128]{1,0:T(8,128)S(1)}, f32[256,128]{1,0:T(8,128)S(1)}, u32[]{:S(2)}, u32[]{:S(2)}) collective-permute-start(f32[256,128]{1,0:T(8,128)S(1)} %bitcast_add_fusion.11), channel_id=1, source_target_pairs={{0,1},{1,2},{2,3},{3,4},{4,5},{5,6},{6,7},{7,0},{8,9},{9,10},{10,1... | collective-permute-start | bytes 393224 | tf_op jit(solution)/shard_map/ppermute | solution.py:110
  141.8 7.8 %collective-permute-start.10 = (f32[256,128]{1,0:T(8,128)S(1)}, f32[256,128]{1,0:T(8,128)S(1)}, u32[]{:S(2)}, u32[]{:S(2)}) collective-permute-start(f32[256,128]{1,0:T(8,128)S(1)} %bitcast_add_fusion.4), channel_id=1, source_target_pairs={{0,7},{1,0},{2,1},{3,2},{4,3},{5,4},{6,5},{7,6},{8,15},{9,8},{10,9... | collective-permute-start | bytes 393224 | tf_op jit(solution)/shard_map/ppermute | solution.py:110
  147.7 8.0 %collective-permute-start.4 = (f32[256,128]{1,0:T(8,128)S(1)}, f32[256,128]{1,0:T(8,128)S(1)}, u32[]{:S(2)}, u32[]{:S(2)}) collective-permute-start(f32[256,128]{1,0:T(8,128)S(1)} %bitcast_add_fusion.10), channel_id=1, source_target_pairs={{0,1},{1,2},{2,3},{3,4},{4,5},{5,6},{6,7},{7,0},{8,9},{9,10},{10,1... | collective-permute-start | bytes 393224 | tf_op jit(solution)/shard_map/ppermute | solution.py:110
  149.6 8.0 %collective-permute-start.11 = (f32[256,128]{1,0:T(8,128)S(1)}, f32[256,128]{1,0:T(8,128)S(1)}, u32[]{:S(2)}, u32[]{:S(2)}) collective-permute-start(f32[256,128]{1,0:T(8,128)S(1)} %bitcast_add_fusion.3), channel_id=1, source_target_pairs={{0,7},{1,0},{2,1},{3,2},{4,3},{5,4},{6,5},{7,6},{8,15},{9,8},{10,9... | collective-permute-start | bytes 393224 | tf_op jit(solution)/shard_map/ppermute | solution.py:110
  155.8 6.9 %collective-permute-start.5 = (f32[256,128]{1,0:T(8,128)S(1)}, f32[256,128]{1,0:T(8,128)S(1)}, u32[]{:S(2)}, u32[]{:S(2)}) collective-permute-start(f32[256,128]{1,0:T(8,128)S(1)} %bitcast_add_fusion.9), channel_id=1, source_target_pairs={{0,1},{1,2},{2,3},{3,4},{4,5},{5,6},{6,7},{7,0},{8,9},{9,10},{10,1... | collective-permute-start | bytes 393224 | tf_op jit(solution)/shard_map/ppermute | solution.py:110
  157.7 6.9 %collective-permute-start.12 = (f32[256,128]{1,0:T(8,128)S(1)}, f32[256,128]{1,0:T(8,128)S(1)}, u32[]{:S(2)}, u32[]{:S(2)}) collective-permute-start(f32[256,128]{1,0:T(8,128)S(1)} %bitcast_add_fusion.2), channel_id=1, source_target_pairs={{0,7},{1,0},{2,1},{3,2},{4,3},{5,4},{6,5},{7,6},{8,15},{9,8},{10,9... | collective-permute-start | bytes 393224 | tf_op jit(solution)/shard_map/ppermute | solution.py:110
  162.7 6.9 %collective-permute-start.6 = (f32[256,128]{1,0:T(8,128)S(1)}, f32[256,128]{1,0:T(8,128)S(1)}, u32[]{:S(2)}, u32[]{:S(2)}) collective-permute-start(f32[256,128]{1,0:T(8,128)S(1)} %bitcast_add_fusion.8), channel_id=1, source_target_pairs={{0,1},{1,2},{2,3},{3,4},{4,5},{5,6},{6,7},{7,0},{8,9},{9,10},{10,1... | collective-permute-start | bytes 393224 | tf_op jit(solution)/shard_map/ppermute | solution.py:110
  164.7 6.5 %collective-permute-start.13 = (f32[256,128]{1,0:T(8,128)S(1)}, f32[256,128]{1,0:T(8,128)S(1)}, u32[]{:S(2)}, u32[]{:S(2)}) collective-permute-start(f32[256,128]{1,0:T(8,128)S(1)} %bitcast_add_fusion.1), channel_id=1, source_target_pairs={{0,7},{1,0},{2,1},{3,2},{4,3},{5,4},{6,5},{7,6},{8,15},{9,8},{10,9... | collective-permute-start | bytes 393224 | tf_op jit(solution)/shard_map/ppermute | solution.py:110
Sparse Core Ops, SparseCore 0:
  77.8 34.0 reduce-scatter.1
  115.3 93.4 all-gather.1

commit v5 on v4

--- a/solution.py
+++ b/solution.py
@@ -37,21 +37,20 @@
 
         def body(src, carry):
             top, total, context = carry
-            col = pl.multiple_of(src * tok_rows, tok_rows)
-            key_t = kv_ref[:HEAD_DIM, pl.ds(col, width)]
-            value_t = kv_ref[HEAD_DIM:, pl.ds(col, width)]
-            scores = jnp.dot(q, key_t, preferred_element_type=jnp.float32) * scale
+            first = pl.multiple_of(src * tok_rows, tok_rows)
+            key = kv_ref[pl.ds(first, width), :HEAD_DIM]
+            value = kv_ref[pl.ds(first, width), HEAD_DIM:]
+            scores = lax.dot_general(
+                q, key, (((1,), (1,)), ((), ())), preferred_element_type=jnp.float32
+            ) * scale
             allowed = lane_pos <= query_pos - src
             scores = jnp.where(allowed, scores, masked_score)
             new_top = jnp.maximum(top, jnp.max(scores, axis=1, keepdims=True))
             shrink = jnp.exp(top - new_top)
             weights = jnp.exp(scores - new_top)
             total = shrink * total + jnp.sum(weights, axis=1, keepdims=True)
-            update = lax.dot_general(
-                weights.astype(jnp.bfloat16),
-                value_t,
-                (((1,), (1,)), ((), ())),
-                preferred_element_type=jnp.float32,
+            update = jnp.dot(
+                weights.astype(jnp.bfloat16), value, preferred_element_type=jnp.float32
             )
             return new_top, total, shrink * context + update
 
@@ -73,7 +72,7 @@
         .transpose(0, 2, 1, 3)
         .reshape(tok_rows * heads_local, HEAD_DIM)
     )
-    kv_t = pair_all.reshape(shards * tok_rows, 2 * HEAD_DIM).T
+    kv_rows = pair_all.reshape(shards * tok_rows, 2 * HEAD_DIM)
     out = pl.pallas_call(
         functools.partial(attention_kernel, shards=shards, tok_rows=tok_rows, block=block),
         out_shape=jax.ShapeDtypeStruct((tok_rows * heads_local, HEAD_DIM), jnp.bfloat16),
@@ -87,9 +86,9 @@
         cost_estimate=pl.CostEstimate(
             flops=4 * tok_rows * heads_local * shards * tok_rows * HEAD_DIM * 3 // 4,
             transcendentals=tok_rows * heads_local * shards * tok_rows * 3 // 4,
-            bytes_accessed=kv_t.size * 2 + 2 * q_rows.size * 2,
+            bytes_accessed=kv_rows.size * 2 + 2 * q_rows.size * 2,
         ),
-    )(jnp.reshape(seq_index, (1,)).astype(jnp.int32), q_rows, kv_t)
+    )(jnp.reshape(seq_index, (1,)).astype(jnp.int32), q_rows, kv_rows)
     return (
         out.reshape(blocks, heads_local, block, HEAD_DIM)
         .transpose(0, 2, 1, 3)

time: 250 us -> 241 us (0.964)
  local copies, waits for them, and re-layouts: 30 us -> 18.2 us
  Pallas kernels: 21.1 us -> 23.7 us
    reshape x1 -> x0, local copies, waits for them, and re-layouts: 11.8 us -> none  [causal_attention(): kv_t = pair_all.reshape(shards * tok_rows, 2 * HEAD_DIM).T]
    pallas_call x1, Pallas kernels: 21.1 us -> 23.7 us  [causal_attention(): pl.pallas_call(functools.partial(attention_kernel, shards=shards, tok_row...]
  transfers between devices with their start and end apart: 17 -> 17, of which waited for: 11 -> 8; matrix products, arithmetic and copies ran while one was open for 4% -> 5% of each run, Pallas kernels for 0% -> 0%
where the time goes in v5:
time: 241 us; the launch traced here: 240 us
  waiting for transfers between devices  86.6 us (36%)
  starting transfers between devices  64.9 us (27%)
  Pallas kernels  23.7 us (10%)
  blocking collectives  22 us (9%)
  local copies, waits for them, and re-layouts  18.2 us (8%)
  between operations  14.3 us (6%)
  other arithmetic  7.08 us (3%)
  matrix products  3.34 us (1%)
    ppermute x14, starting transfers between devices, ring_reduce_scatter(): buf = lax.ppermute(buf, axes, perm)  48.4 us
    all_gather x1, waiting for transfers between devices, local(): pair_all = lax.all_gather(pair_own, 'seq', axis=0, tiled=False)  37.7 us
    reduce_scatter x1, waiting for transfers between devices, local(): lax.psum_scatter(pair_part, ('kvh', 'rep'), scatter_dimension=0, tiled=True)  34.2 us
    pallas_call x1, Pallas kernels, causal_attention(): pl.pallas_call(functools.partial(attention_kernel, shards=shards, tok_row...  23.7 us
    all_gather x1, blocking collectives, local(): lax.all_gather(normed[0], 'kvh', axis=0, tiled=False)  22 us
    all_to_all x1, starting transfers between devices, local(): lax.all_to_all(outgoing, 'seq', split_axis=0, concat_axis=0, tiled=True)  16.4 us
    all_to_all x1, waiting for transfers between devices, local(): lax.all_to_all(outgoing, 'seq', split_axis=0, concat_axis=0, tiled=True)  11.1 us
  transfers between devices with their start and end apart: 17, of which 8 were waited for; matrix products, arithmetic and copies ran while one was open for 5% of the time, Pallas kernels for 0%

profile of v5, /device:TPU:1, one launch (start us, length us, event | category | flops | bytes accessed | tf_op | source)
XLA Modules:
  0.0 240.1 jit_solution(2654083094865569286)
XLA Ops:
  6.5 1.1 convert_reduce_fusion
  7.7 1.2 fusion.12
  8.9 0.8 copy.74
  9.8 0.7 sub.92
  10.5 0.6 dynamic_slice.52
  11.1 0.7 and_select_fusion.1
  12.0 1.1 fusion.14
  13.1 22.0 %all_gather.7 = bf16[4,96,1152]{2,1,0:T(8,128)(2,1)S(1)} all-gather(bf16[1,96,1152]{2,1,0:T(8,128)(2,1)S(1)} %fusion.14), channel_id=1, replica_groups=mesh['seq'=64,'kvh'=4,'rep'=2] {'kvh'}, dimensions={0}, use_global_device_ids=true | all-gather | bytes 1105920 | tf_op jit(solution)/shard_map/all_gather | solution.py:127
  35.2 2.1 fusion.2
  37.3 0.2 copy.75
  37.5 2.1 gather_fusion
  39.5 1.0 all_to_all.8
  40.5 16.4 %all-to-all-start = ((bf16[64,6,448]{2,1,0:T(8,128)(2,1)}), bf16[64,6,448]{2,1,0:T(8,128)(2,1)S(1)}, u32[]{:S(2)}, u32[]{:S(2)}) async-start(bf16[64,6,448]{2,1,0:T(8,128)(2,1)} %all_to_all.8), calls=%async_computation | async-start | bytes 1048576 | tf_op jit(solution)/shard_map/all_to_all | solution.py:144
  57.0 4.6 %copy.76 = bf16[448,3072]{0,1:T(8,128)(2,1)} copy(bf16[448,3072]{1,0:T(8,128)(2,1)} %param.9) | data formatting | bytes 5505024 | tf_op args[4]
  61.6 1.3 slice.23
  63.2 11.1 %all-to-all-done = bf16[64,6,448]{2,1,0:T(8,128)(2,1)S(1)} async-done(((bf16[64,6,448]{2,1,0:T(8,128)(2,1)}), bf16[64,6,448]{2,1,0:T(8,128)(2,1)S(1)}, u32[]{:S(2)}, u32[]{:S(2)}) %all-to-all-start) | async-done | bytes 344096 | tf_op jit(solution)/shard_map/all_to_all | solution.py:144
  74.3 0.2 all_to_all.10
  74.5 1.2 gather_fusion.1
  75.7 0.5 convolution_bitcast_fusion.1
  76.2 1.5 broadcast_in_dim.12
  77.8 34.2 %reduce-scatter.2.cloned.1.call-done = f32[1,256,256]{2,1,0:T(8,128)} async-done(((f32[8,256,256]{2,1,0:T(8,128)}), f32[1,256,256]{2,1,0:T(8,128)}) %reduce-scatter.2.cloned.1.call-update) | async-done | bytes 262160 | tf_op jit(solution)/shard_map/reduce_scatter | solution.py:158
  112.0 1.6 convert_element_type.27
  113.9 1.8 slice.20
  115.7 0.7 convolution_bitcast_fusion
  116.5 0.2 fusion.23
  116.7 0.2 constant_dynamic-slice_fusion
  117.0 2.4 %collective-permute-start = (f32[256,128]{1,0:T(8,128)S(1)}, f32[256,128]{1,0:T(8,128)S(1)}, u32[]{:S(2)}, u32[]{:S(2)}) collective-permute-start(f32[256,128]{1,0:T(8,128)S(1)} %bitcast.78), channel_id=1, source_target_pairs={{0,1},{1,2},{2,3},{3,4},{4,5},{5,6},{6,7},{7,0},{8,9},{9,10},{10,1... | collective-permute-start | bytes 393224 | tf_op jit(solution)/shard_map/ppermute | solution.py:109
  121.0 4.1 %collective-permute-start.7 = (f32[256,128]{1,0:T(8,128)S(1)}, f32[256,128]{1,0:T(8,128)S(1)}, u32[]{:S(2)}, u32[]{:S(2)}) collective-permute-start(f32[256,128]{1,0:T(8,128)S(1)} %bitcast.79), channel_id=1, source_target_pairs={{0,7},{1,0},{2,1},{3,2},{4,3},{5,4},{6,5},{7,6},{8,15},{9,8},{10,9... | collective-permute-start | bytes 393224 | tf_op jit(solution)/shard_map/ppermute | solution.py:109
  125.1 1.9 collective-permute-start.1
  127.0 4.9 %collective-permute-start.8 = (f32[256,128]{1,0:T(8,128)S(1)}, f32[256,128]{1,0:T(8,128)S(1)}, u32[]{:S(2)}, u32[]{:S(2)}) collective-permute-start(f32[256,128]{1,0:T(8,128)S(1)} %bitcast_add_fusion.6), channel_id=1, source_target_pairs={{0,7},{1,0},{2,1},{3,2},{4,3},{5,4},{6,5},{7,6},{8,15},{9,8},{10,9... | collective-permute-start | bytes 393224 | tf_op jit(solution)/shard_map/ppermute | solution.py:109
  132.0 1.9 collective-permute-start.2
  133.9 0.3 collective-permute-done.8
  134.2 4.7 %collective-permute-start.9 = (f32[256,128]{1,0:T(8,128)S(1)}, f32[256,128]{1,0:T(8,128)S(1)}, u32[]{:S(2)}, u32[]{:S(2)}) collective-permute-start(f32[256,128]{1,0:T(8,128)S(1)} %bitcast_add_fusion.5), channel_id=1, source_target_pairs={{0,7},{1,0},{2,1},{3,2},{4,3},{5,4},{6,5},{7,6},{8,15},{9,8},{10,9... | collective-permute-start | bytes 393224 | tf_op jit(solution)/shard_map/ppermute | solution.py:109
  139.0 1.9 collective-permute-start.3
  140.9 0.7 collective-permute-done.9
  141.6 5.0 %collective-permute-start.10 = (f32[256,128]{1,0:T(8,128)S(1)}, f32[256,128]{1,0:T(8,128)S(1)}, u32[]{:S(2)}, u32[]{:S(2)}) collective-permute-start(f32[256,128]{1,0:T(8,128)S(1)} %bitcast_add_fusion.4), channel_id=1, source_target_pairs={{0,7},{1,0},{2,1},{3,2},{4,3},{5,4},{6,5},{7,6},{8,15},{9,8},{10,9... | collective-permute-start | bytes 393224 | tf_op jit(solution)/shard_map/ppermute | solution.py:109
  146.6 0.3 collective-permute-done.3
  146.9 1.9 collective-permute-start.4
  148.9 0.6 collective-permute-done.10
  149.5 5.3 %collective-permute-start.11 = (f32[256,128]{1,0:T(8,128)S(1)}, f32[256,128]{1,0:T(8,128)S(1)}, u32[]{:S(2)}, u32[]{:S(2)}) collective-permute-start(f32[256,128]{1,0:T(8,128)S(1)} %bitcast_add_fusion.3), channel_id=1, source_target_pairs={{0,7},{1,0},{2,1},{3,2},{4,3},{5,4},{6,5},{7,6},{8,15},{9,8},{10,9... | collective-permute-start | bytes 393224 | tf_op jit(solution)/shard_map/ppermute | solution.py:109
  154.8 1.9 collective-permute-start.5
  156.8 5.3 %collective-permute-start.12 = (f32[256,128]{1,0:T(8,128)S(1)}, f32[256,128]{1,0:T(8,128)S(1)}, u32[]{:S(2)}, u32[]{:S(2)}) collective-permute-start(f32[256,128]{1,0:T(8,128)S(1)} %bitcast_add_fusion.2), channel_id=1, source_target_pairs={{0,7},{1,0},{2,1},{3,2},{4,3},{5,4},{6,5},{7,6},{8,15},{9,8},{10,9... | collective-permute-start | bytes 393224 | tf_op jit(solution)/shard_map/ppermute | solution.py:109
  162.1 1.9 collective-permute-start.6
  164.1 5.1 %collective-permute-start.13 = (f32[256,128]{1,0:T(8,128)S(1)}, f32[256,128]{1,0:T(8,128)S(1)}, u32[]{:S(2)}, u32[]{:S(2)}) collective-permute-start(f32[256,128]{1,0:T(8,128)S(1)} %bitcast_add_fusion.1), channel_id=1, source_target_pairs={{0,7},{1,0},{2,1},{3,2},{4,3},{5,4},{6,5},{7,6},{8,15},{9,8},{10,9... | collective-permute-start | bytes 393224 | tf_op jit(solution)/shard_map/ppermute | solution.py:109
  169.2 1.7 collective-permute-done.13
  171.0 37.7 %all-gather.2.cloned.1.call-done = bf16[64,256,256]{2,1,0:T(8,128)(2,1)} async-done(((bf16[1,256,256]{2,1,0:T(8,128)(2,1)}), bf16[64,256,256]{2,1,0:T(8,128)(2,1)}) %all-gather.2.cloned.1.call-update) | async-done | bytes 8388624 | tf_op jit(solution)/shard_map/all_gather | solution.py:164
  208.7 23.7 %shard_map.55 = bf16[512,128]{1,0:T(8,128)(2,1)S(1)} custom-call(s32[1]{0:T(128)} %bitcast.seq_ref, bf16[512,128]{1,0:T(8,128)(2,1)S(1)} %bitcast.69, bf16[16384,256]{1,0:T(8,128)(2,1)} %bitcast.84), custom_call_target="tpu_custom_call" | custom-call | flops 3221225472 | bytes 8650752 | tf_op jit(solution)/shard_map/pallas_call | solution.py:76
  232.5 0.7 reshape.324
  (65 shorter events, 2.7 us)
Async XLA Ops:
  6.5 28.6 %copy-start = (bf16[1152,448]{0,1:T(8,128)(2,1)S(1)}, bf16[1152,448]{0,1:T(8,128)(2,1)}, u32[]{:S(2)}) copy-start(bf16[1152,448]{0,1:T(8,128)(2,1)} %param.8) | copy-start | bytes 3096580
  40.5 33.8 %all-to-all-start = ((bf16[64,6,448]{2,1,0:T(8,128)(2,1)}), bf16[64,6,448]{2,1,0:T(8,128)(2,1)S(1)}, u32[]{:S(2)}, u32[]{:S(2)}) async-start(bf16[64,6,448]{2,1,0:T(8,128)(2,1)} %all_to_all.8), calls=%async_computation | async-start | bytes 1048576 | tf_op jit(solution)/shard_map/all_to_all | solution.py:144
  57.0 55.0 %reduce-scatter.2.cloned.1.call-start = ((), (), s32[]{:S(2)}) async-start(), calls=%async_computation.2 | async-start | bytes 2359296 | tf_op jit(solution)/shard_map/reduce_scatter | solution.py:158
  61.6 1.4 copy-start.1
  77.7 131.0 %all-gather.2.cloned.1.call-start = ((), (), s32[]{:S(2)}) async-start(), calls=%async_computation.3 | async-start | bytes 8519680 | tf_op jit(solution)/shard_map/all_gather | solution.py:164
  117.0 8.0 %collective-permute-start = (f32[256,128]{1,0:T(8,128)S(1)}, f32[256,128]{1,0:T(8,128)S(1)}, u32[]{:S(2)}, u32[]{:S(2)}) collective-permute-start(f32[256,128]{1,0:T(8,128)S(1)} %bitcast.78), channel_id=1, source_target_pairs={{0,1},{1,2},{2,3},{3,4},{4,5},{5,6},{6,7},{7,0},{8,9},{9,10},{10,1... | collective-permute-start | bytes 393224 | tf_op jit(solution)/shard_map/ppermute | solution.py:109
  121.0 6.0 %collective-permute-start.7 = (f32[256,128]{1,0:T(8,128)S(1)}, f32[256,128]{1,0:T(8,128)S(1)}, u32[]{:S(2)}, u32[]{:S(2)}) collective-permute-start(f32[256,128]{1,0:T(8,128)S(1)} %bitcast.79), channel_id=1, source_target_pairs={{0,7},{1,0},{2,1},{3,2},{4,3},{5,4},{6,5},{7,6},{8,15},{9,8},{10,9... | collective-permute-start | bytes 393224 | tf_op jit(solution)/shard_map/ppermute | solution.py:109
  125.1 6.9 %collective-permute-start.1 = (f32[256,128]{1,0:T(8,128)S(1)}, f32[256,128]{1,0:T(8,128)S(1)}, u32[]{:S(2)}, u32[]{:S(2)}) collective-permute-start(f32[256,128]{1,0:T(8,128)S(1)} %bitcast_add_fusion.13), channel_id=1, source_target_pairs={{0,1},{1,2},{2,3},{3,4},{4,5},{5,6},{6,7},{7,0},{8,9},{9,10},{10,1... | collective-permute-start | bytes 393224 | tf_op jit(solution)/shard_map/ppermute | solution.py:109
  127.0 7.2 %collective-permute-start.8 = (f32[256,128]{1,0:T(8,128)S(1)}, f32[256,128]{1,0:T(8,128)S(1)}, u32[]{:S(2)}, u32[]{:S(2)}) collective-permute-start(f32[256,128]{1,0:T(8,128)S(1)} %bitcast_add_fusion.6), channel_id=1, source_target_pairs={{0,7},{1,0},{2,1},{3,2},{4,3},{5,4},{6,5},{7,6},{8,15},{9,8},{10,9... | collective-permute-start | bytes 393224 | tf_op jit(solution)/shard_map/ppermute | solution.py:109
  132.0 7.0 %collective-permute-start.2 = (f32[256,128]{1,0:T(8,128)S(1)}, f32[256,128]{1,0:T(8,128)S(1)}, u32[]{:S(2)}, u32[]{:S(2)}) collective-permute-start(f32[256,128]{1,0:T(8,128)S(1)} %bitcast_add_fusion.12), channel_id=1, source_target_pairs={{0,1},{1,2},{2,3},{3,4},{4,5},{5,6},{6,7},{7,0},{8,9},{9,10},{10,1... | collective-permute-start | bytes 393224 | tf_op jit(solution)/shard_map/ppermute | solution.py:109
  134.2 7.4 %collective-permute-start.9 = (f32[256,128]{1,0:T(8,128)S(1)}, f32[256,128]{1,0:T(8,128)S(1)}, u32[]{:S(2)}, u32[]{:S(2)}) collective-permute-start(f32[256,128]{1,0:T(8,128)S(1)} %bitcast_add_fusion.5), channel_id=1, source_target_pairs={{0,7},{1,0},{2,1},{3,2},{4,3},{5,4},{6,5},{7,6},{8,15},{9,8},{10,9... | collective-permute-start | bytes 393224 | tf_op jit(solution)/shard_map/ppermute | solution.py:109
  139.0 7.9 %collective-permute-start.3 = (f32[256,128]{1,0:T(8,128)S(1)}, f32[256,128]{1,0:T(8,128)S(1)}, u32[]{:S(2)}, u32[]{:S(2)}) collective-permute-start(f32[256,128]{1,0:T(8,128)S(1)} %bitcast_add_fusion.11), channel_id=1, source_target_pairs={{0,1},{1,2},{2,3},{3,4},{4,5},{5,6},{6,7},{7,0},{8,9},{9,10},{10,1... | collective-permute-start | bytes 393224 | tf_op jit(solution)/shard_map/ppermute | solution.py:109
  141.6 7.9 %collective-permute-start.10 = (f32[256,128]{1,0:T(8,128)S(1)}, f32[256,128]{1,0:T(8,128)S(1)}, u32[]{:S(2)}, u32[]{:S(2)}) collective-permute-start(f32[256,128]{1,0:T(8,128)S(1)} %bitcast_add_fusion.4), channel_id=1, source_target_pairs={{0,7},{1,0},{2,1},{3,2},{4,3},{5,4},{6,5},{7,6},{8,15},{9,8},{10,9... | collective-permute-start | bytes 393224 | tf_op jit(solution)/shard_map/ppermute | solution.py:109
  146.9 7.9 %collective-permute-start.4 = (f32[256,128]{1,0:T(8,128)S(1)}, f32[256,128]{1,0:T(8,128)S(1)}, u32[]{:S(2)}, u32[]{:S(2)}) collective-permute-start(f32[256,128]{1,0:T(8,128)S(1)} %bitcast_add_fusion.10), channel_id=1, source_target_pairs={{0,1},{1,2},{2,3},{3,4},{4,5},{5,6},{6,7},{7,0},{8,9},{9,10},{10,1... | collective-permute-start | bytes 393224 | tf_op jit(solution)/shard_map/ppermute | solution.py:109
  149.5 7.3 %collective-permute-start.11 = (f32[256,128]{1,0:T(8,128)S(1)}, f32[256,128]{1,0:T(8,128)S(1)}, u32[]{:S(2)}, u32[]{:S(2)}) collective-permute-start(f32[256,128]{1,0:T(8,128)S(1)} %bitcast_add_fusion.3), channel_id=1, source_target_pairs={{0,7},{1,0},{2,1},{3,2},{4,3},{5,4},{6,5},{7,6},{8,15},{9,8},{10,9... | collective-permute-start | bytes 393224 | tf_op jit(solution)/shard_map/ppermute | solution.py:109
  154.8 7.2 %collective-permute-start.5 = (f32[256,128]{1,0:T(8,128)S(1)}, f32[256,128]{1,0:T(8,128)S(1)}, u32[]{:S(2)}, u32[]{:S(2)}) collective-permute-start(f32[256,128]{1,0:T(8,128)S(1)} %bitcast_add_fusion.9), channel_id=1, source_target_pairs={{0,1},{1,2},{2,3},{3,4},{4,5},{5,6},{6,7},{7,0},{8,9},{9,10},{10,1... | collective-permute-start | bytes 393224 | tf_op jit(solution)/shard_map/ppermute | solution.py:109
  156.8 7.2 %collective-permute-start.12 = (f32[256,128]{1,0:T(8,128)S(1)}, f32[256,128]{1,0:T(8,128)S(1)}, u32[]{:S(2)}, u32[]{:S(2)}) collective-permute-start(f32[256,128]{1,0:T(8,128)S(1)} %bitcast_add_fusion.2), channel_id=1, source_target_pairs={{0,7},{1,0},{2,1},{3,2},{4,3},{5,4},{6,5},{7,6},{8,15},{9,8},{10,9... | collective-permute-start | bytes 393224 | tf_op jit(solution)/shard_map/ppermute | solution.py:109
  162.1 7.1 %collective-permute-start.6 = (f32[256,128]{1,0:T(8,128)S(1)}, f32[256,128]{1,0:T(8,128)S(1)}, u32[]{:S(2)}, u32[]{:S(2)}) collective-permute-start(f32[256,128]{1,0:T(8,128)S(1)} %bitcast_add_fusion.8), channel_id=1, source_target_pairs={{0,1},{1,2},{2,3},{3,4},{4,5},{5,6},{6,7},{7,0},{8,9},{9,10},{10,1... | collective-permute-start | bytes 393224 | tf_op jit(solution)/shard_map/ppermute | solution.py:109
  164.1 6.9 %collective-permute-start.13 = (f32[256,128]{1,0:T(8,128)S(1)}, f32[256,128]{1,0:T(8,128)S(1)}, u32[]{:S(2)}, u32[]{:S(2)}) collective-permute-start(f32[256,128]{1,0:T(8,128)S(1)} %bitcast_add_fusion.1), channel_id=1, source_target_pairs={{0,7},{1,0},{2,1},{3,2},{4,3},{5,4},{6,5},{7,6},{8,15},{9,8},{10,9... | collective-permute-start | bytes 393224 | tf_op jit(solution)/shard_map/ppermute | solution.py:109
Sparse Core Ops, SparseCore 0:
  77.8 34.0 reduce-scatter.1
  115.3 93.3 all-gather.1

commit v6 on v5

--- a/solution.py
+++ b/solution.py
@@ -27,17 +27,22 @@
 def attention_kernel(seq_ref, q_ref, kv_ref, o_ref, *, shards, tok_rows, block):
     seq_index = seq_ref[0]
     scale = HEAD_DIM ** (-0.5)
-    rows = q_ref.shape[0] // (tok_rows // block)
-    for qb in range(tok_rows // block):
+    blocks = tok_rows // block
+    rows = q_ref.shape[0] // blocks
+    setups = []
+    for qb in range(blocks):
         width = (((qb + 1) * block - 1) // 128 + 1) * 128
-        q = q_ref[qb * rows : (qb + 1) * rows, :]
         row_j = qb * block + lax.broadcasted_iota(jnp.int32, (rows, 1), 0) % block
-        query_pos = row_j * shards + seq_index
         lane_pos = lax.broadcasted_iota(jnp.int32, (1, width), 1) * shards
-
-        def body(src, carry):
-            top, total, context = carry
-            first = pl.multiple_of(src * tok_rows, tok_rows)
+        setups.append((width, row_j * shards + seq_index, lane_pos))
+
+    def body(src, carry):
+        first = pl.multiple_of(src * tok_rows, tok_rows)
+        out = []
+        for qb in range(blocks):
+            width, query_pos, lane_pos = setups[qb]
+            top, total, context = carry[qb]
+            q = q_ref[qb * rows : (qb + 1) * rows, :]
             key = kv_ref[pl.ds(first, width), :HEAD_DIM]
             value = kv_ref[pl.ds(first, width), HEAD_DIM:]
             scores = lax.dot_general(
@@ -52,14 +57,20 @@
             update = jnp.dot(
                 weights.astype(jnp.bfloat16), value, preferred_element_type=jnp.float32
             )
-            return new_top, total, shrink * context + update
-
-        start = (
+            out.append((new_top, total, shrink * context + update))
+        return tuple(out)
+
+    start = tuple(
+        (
             jnp.full((rows, 1), masked_score, jnp.float32),
             jnp.zeros((rows, 1), jnp.float32),
             jnp.zeros((rows, HEAD_DIM), jnp.float32),
         )
-        top, total, context = lax.fori_loop(0, shards, body, start, unroll=UNROLL)
+        for _ in range(blocks)
+    )
+    final = lax.fori_loop(0, shards, body, start, unroll=UNROLL)
+    for qb in range(blocks):
+        _, total, context = final[qb]
         o_ref[qb * rows : (qb + 1) * rows, :] = (context / total).astype(o_ref.dtype)
 
 
@@ -96,6 +107,22 @@
     )
 
 
+def ring_all_gather(block, axis):
+    count = lax.axis_size(axis)
+    forward = [(i, (i + 1) % count) for i in range(count)]
+    backward = [(i, (i - 1) % count) for i in range(count)]
+    placed = {0: block}
+    ahead, behind = block, block
+    for step in range(1, (count - 1) // 2 + 1):
+        behind = lax.ppermute(behind, axis, forward)
+        ahead = lax.ppermute(ahead, axis, backward)
+        placed[count - step] = behind
+        placed[step] = ahead
+    if count % 2 == 0 and count > 1:
+        placed[count // 2] = lax.ppermute(behind, axis, forward)
+    return jnp.stack([placed[k] for k in range(count)])
+
+
 def ring_reduce_scatter(parts):
     count = parts.shape[0]
     axes = ("kvh", "rep")
@@ -124,7 +151,9 @@
     tok_rows = 2 * frames_dev * frame_max // 3
     heads_local = GROUP_HEADS // rep_count
     normed = layer_norm(vision_states, norm_gain)
-    frame_rows = lax.all_gather(normed[0], "kvh", axis=0, tiled=False).reshape(1, frame_max, -1)
+    kvh_index = lax.axis_index("kvh")
+    rows_dev = vision_states.shape[1]
+    frame_rows = ring_all_gather(normed[0], "kvh").reshape(1, frame_max, -1)
     hidden = jnp.einsum(
         "frv,vc->frc",
         frame_rows,
@@ -139,6 +168,7 @@
     slots = jnp.arange(cap_frame, dtype=jnp.int32)[None, None, :]
     frame_local = jnp.arange(frames_dev, dtype=jnp.int32)[None, :, None]
     row_of = jnp.mod(dest - my_starts[None, :, None], seq_count) + slots * seq_count
+    row_of = jnp.mod(row_of // rows_dev - kvh_index, lax.axis_size("kvh")) * rows_dev + row_of % rows_dev
     send_index = (frame_local * frame_max + row_of).reshape(-1)
     outgoing = visual_frames.reshape(frames_dev * frame_max, d_cols)[send_index]
     received = lax.all_to_all(outgoing, "seq", split_axis=0, concat_axis=0, tiled=True)

time: 241 us -> 246 us (1.021)
  blocking collectives: 22 us -> 0 us
  waiting for transfers between devices: 86.6 us -> 101 us
  starting transfers between devices: 64.9 us -> 77.3 us
    all_gather x1 -> x0, blocking collectives: 22 us -> none  [local(): lax.all_gather(normed[0], 'kvh', axis=0, tiled=False)]
    ppermute x0 -> x3, starting transfers between devices: none -> 14.6 us  [the longest x1 5.99 us: ring_all_gather(): placed[count // 2] = lax.ppermute(behind, axis, forward)]
    ppermute x0 -> x3, waiting for transfers between devices: none -> 8.32 us  [the longest x1 6.64 us: ring_all_gather(): placed[count // 2] = lax.ppermute(behind, axis, forward)]
    reduce_scatter x1, waiting for transfers between devices: 34.2 us -> 39.4 us  [local(): lax.psum_scatter(pair_part, ('kvh', 'rep'), scatter_dimension=0, tiled=True)]
  transfers between devices with their start and end apart: 17 -> 20, of which waited for: 8 -> 13; matrix products, arithmetic and copies ran while one was open for 5% -> 6% of each run, Pallas kernels for 0% -> 0%
where the time goes in v6:
time: 246 us; the launch traced here: 245 us
  waiting for transfers between devices  101 us (41%)
  starting transfers between devices  77.3 us (31%)
  Pallas kernels  21.6 us (9%)
  local copies, waits for them, and re-layouts  18.5 us (8%)
  between operations  14.4 us (6%)
  other arithmetic  8.45 us (3%)
  matrix products  3.33 us (1%)
    ppermute x14, starting transfers between devices, ring_reduce_scatter(): buf = lax.ppermute(buf, axes, perm)  47.6 us
    reduce_scatter x1, waiting for transfers between devices, local(): lax.psum_scatter(pair_part, ('kvh', 'rep'), scatter_dimension=0, tiled=True)  39.4 us
    all_gather x1, waiting for transfers between devices, local(): pair_all = lax.all_gather(pair_own, 'seq', axis=0, tiled=False)  37.9 us
    pallas_call x1, Pallas kernels, causal_attention(): pl.pallas_call(functools.partial(attention_kernel, shards=shards, tok_row...  21.6 us
    all_to_all x1, starting transfers between devices, local(): lax.all_to_all(outgoing, 'seq', split_axis=0, concat_axis=0, tiled=True)  15 us
    all_to_all x1, waiting for transfers between devices, local(): lax.all_to_all(outgoing, 'seq', split_axis=0, concat_axis=0, tiled=True)  11.1 us
    ppermute x1, waiting for transfers between devices, ring_all_gather(): placed[count // 2] = lax.ppermute(behind, axis, forward)  6.64 us
    ppermute x1, starting transfers between devices, ring_all_gather(): placed[count // 2] = lax.ppermute(behind, axis, forward)  5.99 us
  transfers between devices with their start and end apart: 20, of which 13 were waited for; matrix products, arithmetic and copies ran while one was open for 6% of the time, Pallas kernels for 0%

profile of v6, /device:TPU:1, one launch (start us, length us, event | category | flops | bytes accessed | tf_op | source)
XLA Modules:
  0.0 244.6 jit_solution(10036686898746562924)
XLA Ops:
  6.5 1.1 convert_reduce_fusion
  7.7 1.2 fusion.12
  8.9 1.1 fusion.32
  10.0 5.0 %collective-permute-start.1 = (bf16[96,1152]{1,0:T(8,128)(2,1)S(1)}, bf16[96,1152]{1,0:T(8,128)(2,1)S(1)}, u32[]{:S(2)}, u32[]{:S(2)}) collective-permute-start(bf16[96,1152]{1,0:T(8,128)(2,1)S(1)} %fusion.32), channel_id=1, source_target_pairs={{0,2},{2,4},{4,6},{6,0},{1,3},{3,5},{5,7},{7,1},{8,10},{10,12},{12... | collective-permute-start | bytes 663560 | tf_op jit(solution)/shard_map/ppermute | solution.py:117
  15.1 3.6 %collective-permute-start = (bf16[96,1152]{1,0:T(8,128)(2,1)S(1)}, bf16[96,1152]{1,0:T(8,128)(2,1)S(1)}, u32[]{:S(2)}, u32[]{:S(2)}) collective-permute-start(bf16[96,1152]{1,0:T(8,128)(2,1)S(1)} %fusion.32), channel_id=1, source_target_pairs={{0,6},{2,0},{4,2},{6,4},{1,7},{3,1},{5,3},{7,5},{8,14},{10,8},{12,... | collective-permute-start | bytes 663560 | tf_op jit(solution)/shard_map/ppermute | solution.py:118
  18.7 1.1 fusion.14
  19.8 0.7 copy.74
  20.8 0.7 sub.114
  21.4 0.6 dynamic_slice.52
  22.0 0.7 and_select_fusion.4
  23.3 6.0 %collective-permute-start.2 = (bf16[96,1152]{1,0:T(8,128)(2,1)S(1)}, bf16[96,1152]{1,0:T(8,128)(2,1)S(1)}, u32[]{:S(2)}, u32[]{:S(2)}) collective-permute-start(bf16[96,1152]{1,0:T(8,128)(2,1)S(1)} %collective-permute-done.1), channel_id=1, source_target_pairs={{0,2},{2,4},{4,6},{6,0},{1,3},{3,5},{5,7},{7,1},{8,10},{10,12},{12... | collective-permute-start | bytes 663560 | tf_op jit(solution)/shard_map/ppermute | solution.py:122
  29.3 1.7 collective-permute-done
  31.0 6.6 %collective-permute-done.2 = bf16[96,1152]{1,0:T(8,128)(2,1)S(1)} collective-permute-done((bf16[96,1152]{1,0:T(8,128)(2,1)S(1)}, bf16[96,1152]{1,0:T(8,128)(2,1)S(1)}, u32[]{:S(2)}, u32[]{:S(2)}) %collective-permute-start.2) | collective-permute-done | bytes 221216 | tf_op jit(solution)/shard_map/ppermute | solution.py:122
  37.8 2.1 fusion.2
  40.1 2.1 gather_fusion
  42.2 1.0 all_to_all.8
  43.1 15.0 %all-to-all-start = ((bf16[64,6,448]{2,1,0:T(8,128)(2,1)}), bf16[64,6,448]{2,1,0:T(8,128)(2,1)S(1)}, u32[]{:S(2)}, u32[]{:S(2)}) async-start(bf16[64,6,448]{2,1,0:T(8,128)(2,1)} %all_to_all.8), calls=%async_computation | async-start | bytes 1048576 | tf_op jit(solution)/shard_map/all_to_all | solution.py:174
  58.2 4.6 %copy.76 = bf16[448,3072]{0,1:T(8,128)(2,1)} copy(bf16[448,3072]{1,0:T(8,128)(2,1)} %param.9) | data formatting | bytes 5505024 | tf_op args[4]
  62.9 1.3 slice.23
  64.4 11.1 %all-to-all-done = bf16[64,6,448]{2,1,0:T(8,128)(2,1)S(1)} async-done(((bf16[64,6,448]{2,1,0:T(8,128)(2,1)}), bf16[64,6,448]{2,1,0:T(8,128)(2,1)S(1)}, u32[]{:S(2)}, u32[]{:S(2)}) %all-to-all-start) | async-done | bytes 344096 | tf_op jit(solution)/shard_map/all_to_all | solution.py:174
  75.8 1.2 gather_fusion.1
  76.9 0.5 convolution_bitcast_fusion.1
  77.4 1.5 broadcast_in_dim.12
  79.0 39.4 %reduce-scatter.2.cloned.1.call-done = f32[1,256,256]{2,1,0:T(8,128)} async-done(((f32[8,256,256]{2,1,0:T(8,128)}), f32[1,256,256]{2,1,0:T(8,128)}) %reduce-scatter.2.cloned.1.call-update) | async-done | bytes 262160 | tf_op jit(solution)/shard_map/reduce_scatter | solution.py:188
  118.4 1.6 convert_element_type.27
  120.3 1.8 slice.20
  122.2 0.7 convolution_bitcast_fusion
  123.5 2.3 collective-permute-start.3
  127.3 4.2 %collective-permute-start.10 = (f32[256,128]{1,0:T(8,128)S(1)}, f32[256,128]{1,0:T(8,128)S(1)}, u32[]{:S(2)}, u32[]{:S(2)}) collective-permute-start(f32[256,128]{1,0:T(8,128)S(1)} %bitcast.95), channel_id=1, source_target_pairs={{0,7},{1,0},{2,1},{3,2},{4,3},{5,4},{6,5},{7,6},{8,15},{9,8},{10,9... | collective-permute-start | bytes 393224 | tf_op jit(solution)/shard_map/ppermute | solution.py:136
  131.5 1.9 collective-permute-start.4
  133.5 4.9 %collective-permute-start.11 = (f32[256,128]{1,0:T(8,128)S(1)}, f32[256,128]{1,0:T(8,128)S(1)}, u32[]{:S(2)}, u32[]{:S(2)}) collective-permute-start(f32[256,128]{1,0:T(8,128)S(1)} %bitcast_add_fusion.6), channel_id=1, source_target_pairs={{0,7},{1,0},{2,1},{3,2},{4,3},{5,4},{6,5},{7,6},{8,15},{9,8},{10,9... | collective-permute-start | bytes 393224 | tf_op jit(solution)/shard_map/ppermute | solution.py:136
  138.5 1.9 collective-permute-start.5
  140.6 4.8 %collective-permute-start.12 = (f32[256,128]{1,0:T(8,128)S(1)}, f32[256,128]{1,0:T(8,128)S(1)}, u32[]{:S(2)}, u32[]{:S(2)}) collective-permute-start(f32[256,128]{1,0:T(8,128)S(1)} %bitcast_add_fusion.5), channel_id=1, source_target_pairs={{0,7},{1,0},{2,1},{3,2},{4,3},{5,4},{6,5},{7,6},{8,15},{9,8},{10,9... | collective-permute-start | bytes 393224 | tf_op jit(solution)/shard_map/ppermute | solution.py:136
  145.4 1.9 collective-permute-start.6
  147.4 0.7 collective-permute-done.12
  148.1 5.0 %collective-permute-start.13 = (f32[256,128]{1,0:T(8,128)S(1)}, f32[256,128]{1,0:T(8,128)S(1)}, u32[]{:S(2)}, u32[]{:S(2)}) collective-permute-start(f32[256,128]{1,0:T(8,128)S(1)} %bitcast_add_fusion.4), channel_id=1, source_target_pairs={{0,7},{1,0},{2,1},{3,2},{4,3},{5,4},{6,5},{7,6},{8,15},{9,8},{10,9... | collective-permute-start | bytes 393224 | tf_op jit(solution)/shard_map/ppermute | solution.py:136
  153.5 1.9 collective-permute-start.7
  155.4 0.5 collective-permute-done.13
  155.9 5.3 %collective-permute-start.14 = (f32[256,128]{1,0:T(8,128)S(1)}, f32[256,128]{1,0:T(8,128)S(1)}, u32[]{:S(2)}, u32[]{:S(2)}) collective-permute-start(f32[256,128]{1,0:T(8,128)S(1)} %bitcast_add_fusion.3), channel_id=1, source_target_pairs={{0,7},{1,0},{2,1},{3,2},{4,3},{5,4},{6,5},{7,6},{8,15},{9,8},{10,9... | collective-permute-start | bytes 393224 | tf_op jit(solution)/shard_map/ppermute | solution.py:136
  161.4 1.9 collective-permute-start.8
  163.4 4.8 %collective-permute-start.15 = (f32[256,128]{1,0:T(8,128)S(1)}, f32[256,128]{1,0:T(8,128)S(1)}, u32[]{:S(2)}, u32[]{:S(2)}) collective-permute-start(f32[256,128]{1,0:T(8,128)S(1)} %bitcast_add_fusion.2), channel_id=1, source_target_pairs={{0,7},{1,0},{2,1},{3,2},{4,3},{5,4},{6,5},{7,6},{8,15},{9,8},{10,9... | collective-permute-start | bytes 393224 | tf_op jit(solution)/shard_map/ppermute | solution.py:136
  168.1 0.6 collective-permute-done.8
  168.8 1.9 collective-permute-start.9
  170.7 4.8 %collective-permute-start.16 = (f32[256,128]{1,0:T(8,128)S(1)}, f32[256,128]{1,0:T(8,128)S(1)}, u32[]{:S(2)}, u32[]{:S(2)}) collective-permute-start(f32[256,128]{1,0:T(8,128)S(1)} %bitcast_add_fusion.1), channel_id=1, source_target_pairs={{0,7},{1,0},{2,1},{3,2},{4,3},{5,4},{6,5},{7,6},{8,15},{9,8},{10,9... | collective-permute-start | bytes 393224 | tf_op jit(solution)/shard_map/ppermute | solution.py:136
  175.7 1.5 collective-permute-done.16
  177.3 37.9 %all-gather.2.cloned.1.call-done = bf16[64,256,256]{2,1,0:T(8,128)(2,1)} async-done(((bf16[1,256,256]{2,1,0:T(8,128)(2,1)}), bf16[64,256,256]{2,1,0:T(8,128)(2,1)}) %all-gather.2.cloned.1.call-update) | async-done | bytes 8388624 | tf_op jit(solution)/shard_map/all_gather | solution.py:194
  215.2 21.6 %shard_map.55 = bf16[512,128]{1,0:T(8,128)(2,1)S(1)} custom-call(s32[1]{0:T(128)} %bitcast.seq_ref, bf16[512,128]{1,0:T(8,128)(2,1)S(1)} %bitcast.82, bf16[16384,256]{1,0:T(8,128)(2,1)} %bitcast.100), custom_call_target="tpu_custom_call" | custom-call | flops 3221225472 | bytes 8650752 | tf_op jit(solution)/shard_map/pallas_call | solution.py:87
  237.0 0.7 reshape.432
  (75 shorter events, 4.9 us)
Async XLA Ops:
  6.5 31.3 %copy-start = (bf16[1152,448]{0,1:T(8,128)(2,1)S(1)}, bf16[1152,448]{0,1:T(8,128)(2,1)}, u32[]{:S(2)}) copy-start(bf16[1152,448]{0,1:T(8,128)(2,1)} %param.8) | copy-start | bytes 3096580
  10.0 13.3 %collective-permute-start.1 = (bf16[96,1152]{1,0:T(8,128)(2,1)S(1)}, bf16[96,1152]{1,0:T(8,128)(2,1)S(1)}, u32[]{:S(2)}, u32[]{:S(2)}) collective-permute-start(bf16[96,1152]{1,0:T(8,128)(2,1)S(1)} %fusion.32), channel_id=1, source_target_pairs={{0,2},{2,4},{4,6},{6,0},{1,3},{3,5},{5,7},{7,1},{8,10},{10,12},{12... | collective-permute-start | bytes 663560 | tf_op jit(solution)/shard_map/ppermute | solution.py:117
  15.1 15.9 %collective-permute-start = (bf16[96,1152]{1,0:T(8,128)(2,1)S(1)}, bf16[96,1152]{1,0:T(8,128)(2,1)S(1)}, u32[]{:S(2)}, u32[]{:S(2)}) collective-permute-start(bf16[96,1152]{1,0:T(8,128)(2,1)S(1)} %fusion.32), channel_id=1, source_target_pairs={{0,6},{2,0},{4,2},{6,4},{1,7},{3,1},{5,3},{7,5},{8,14},{10,8},{12,... | collective-permute-start | bytes 663560 | tf_op jit(solution)/shard_map/ppermute | solution.py:118
  23.3 14.4 %collective-permute-start.2 = (bf16[96,1152]{1,0:T(8,128)(2,1)S(1)}, bf16[96,1152]{1,0:T(8,128)(2,1)S(1)}, u32[]{:S(2)}, u32[]{:S(2)}) collective-permute-start(bf16[96,1152]{1,0:T(8,128)(2,1)S(1)} %collective-permute-done.1), channel_id=1, source_target_pairs={{0,2},{2,4},{4,6},{6,0},{1,3},{3,5},{5,7},{7,1},{8,10},{10,12},{12... | collective-permute-start | bytes 663560 | tf_op jit(solution)/shard_map/ppermute | solution.py:122
  43.1 32.4 %all-to-all-start = ((bf16[64,6,448]{2,1,0:T(8,128)(2,1)}), bf16[64,6,448]{2,1,0:T(8,128)(2,1)S(1)}, u32[]{:S(2)}, u32[]{:S(2)}) async-start(bf16[64,6,448]{2,1,0:T(8,128)(2,1)} %all_to_all.8), calls=%async_computation | async-start | bytes 1048576 | tf_op jit(solution)/shard_map/all_to_all | solution.py:174
  58.2 60.2 %reduce-scatter.2.cloned.1.call-start = ((), (), s32[]{:S(2)}) async-start(), calls=%async_computation.2 | async-start | bytes 2359296 | tf_op jit(solution)/shard_map/reduce_scatter | solution.py:188
  62.9 1.4 copy-start.1
  78.9 136.3 %all-gather.2.cloned.1.call-start = ((), (), s32[]{:S(2)}) async-start(), calls=%async_computation.3 | async-start | bytes 8519680 | tf_op jit(solution)/shard_map/all_gather | solution.py:194
  123.5 8.0 %collective-permute-start.3 = (f32[256,128]{1,0:T(8,128)S(1)}, f32[256,128]{1,0:T(8,128)S(1)}, u32[]{:S(2)}, u32[]{:S(2)}) collective-permute-start(f32[256,128]{1,0:T(8,128)S(1)} %bitcast.94), channel_id=1, source_target_pairs={{0,1},{1,2},{2,3},{3,4},{4,5},{5,6},{6,7},{7,0},{8,9},{9,10},{10,1... | collective-permute-start | bytes 393224 | tf_op jit(solution)/shard_map/ppermute | solution.py:136
  127.3 6.2 %collective-permute-start.10 = (f32[256,128]{1,0:T(8,128)S(1)}, f32[256,128]{1,0:T(8,128)S(1)}, u32[]{:S(2)}, u32[]{:S(2)}) collective-permute-start(f32[256,128]{1,0:T(8,128)S(1)} %bitcast.95), channel_id=1, source_target_pairs={{0,7},{1,0},{2,1},{3,2},{4,3},{5,4},{6,5},{7,6},{8,15},{9,8},{10,9... | collective-permute-start | bytes 393224 | tf_op jit(solution)/shard_map/ppermute | solution.py:136
  131.5 6.9 %collective-permute-start.4 = (f32[256,128]{1,0:T(8,128)S(1)}, f32[256,128]{1,0:T(8,128)S(1)}, u32[]{:S(2)}, u32[]{:S(2)}) collective-permute-start(f32[256,128]{1,0:T(8,128)S(1)} %bitcast_add_fusion.13), channel_id=1, source_target_pairs={{0,1},{1,2},{2,3},{3,4},{4,5},{5,6},{6,7},{7,0},{8,9},{9,10},{10,1... | collective-permute-start | bytes 393224 | tf_op jit(solution)/shard_map/ppermute | solution.py:136
  133.5 7.1 %collective-permute-start.11 = (f32[256,128]{1,0:T(8,128)S(1)}, f32[256,128]{1,0:T(8,128)S(1)}, u32[]{:S(2)}, u32[]{:S(2)}) collective-permute-start(f32[256,128]{1,0:T(8,128)S(1)} %bitcast_add_fusion.6), channel_id=1, source_target_pairs={{0,7},{1,0},{2,1},{3,2},{4,3},{5,4},{6,5},{7,6},{8,15},{9,8},{10,9... | collective-permute-start | bytes 393224 | tf_op jit(solution)/shard_map/ppermute | solution.py:136
  138.5 7.0 %collective-permute-start.5 = (f32[256,128]{1,0:T(8,128)S(1)}, f32[256,128]{1,0:T(8,128)S(1)}, u32[]{:S(2)}, u32[]{:S(2)}) collective-permute-start(f32[256,128]{1,0:T(8,128)S(1)} %bitcast_add_fusion.12), channel_id=1, source_target_pairs={{0,1},{1,2},{2,3},{3,4},{4,5},{5,6},{6,7},{7,0},{8,9},{9,10},{10,1... | collective-permute-start | bytes 393224 | tf_op jit(solution)/shard_map/ppermute | solution.py:136
  140.6 7.5 %collective-permute-start.12 = (f32[256,128]{1,0:T(8,128)S(1)}, f32[256,128]{1,0:T(8,128)S(1)}, u32[]{:S(2)}, u32[]{:S(2)}) collective-permute-start(f32[256,128]{1,0:T(8,128)S(1)} %bitcast_add_fusion.5), channel_id=1, source_target_pairs={{0,7},{1,0},{2,1},{3,2},{4,3},{5,4},{6,5},{7,6},{8,15},{9,8},{10,9... | collective-permute-start | bytes 393224 | tf_op jit(solution)/shard_map/ppermute | solution.py:136
  145.4 8.0 %collective-permute-start.6 = (f32[256,128]{1,0:T(8,128)S(1)}, f32[256,128]{1,0:T(8,128)S(1)}, u32[]{:S(2)}, u32[]{:S(2)}) collective-permute-start(f32[256,128]{1,0:T(8,128)S(1)} %bitcast_add_fusion.11), channel_id=1, source_target_pairs={{0,1},{1,2},{2,3},{3,4},{4,5},{5,6},{6,7},{7,0},{8,9},{9,10},{10,1... | collective-permute-start | bytes 393224 | tf_op jit(solution)/shard_map/ppermute | solution.py:136
  148.1 7.8 %collective-permute-start.13 = (f32[256,128]{1,0:T(8,128)S(1)}, f32[256,128]{1,0:T(8,128)S(1)}, u32[]{:S(2)}, u32[]{:S(2)}) collective-permute-start(f32[256,128]{1,0:T(8,128)S(1)} %bitcast_add_fusion.4), channel_id=1, source_target_pairs={{0,7},{1,0},{2,1},{3,2},{4,3},{5,4},{6,5},{7,6},{8,15},{9,8},{10,9... | collective-permute-start | bytes 393224 | tf_op jit(solution)/shard_map/ppermute | solution.py:136
  153.5 7.9 %collective-permute-start.7 = (f32[256,128]{1,0:T(8,128)S(1)}, f32[256,128]{1,0:T(8,128)S(1)}, u32[]{:S(2)}, u32[]{:S(2)}) collective-permute-start(f32[256,128]{1,0:T(8,128)S(1)} %bitcast_add_fusion.10), channel_id=1, source_target_pairs={{0,1},{1,2},{2,3},{3,4},{4,5},{5,6},{6,7},{7,0},{8,9},{9,10},{10,1... | collective-permute-start | bytes 393224 | tf_op jit(solution)/shard_map/ppermute | solution.py:136
  155.9 7.5 %collective-permute-start.14 = (f32[256,128]{1,0:T(8,128)S(1)}, f32[256,128]{1,0:T(8,128)S(1)}, u32[]{:S(2)}, u32[]{:S(2)}) collective-permute-start(f32[256,128]{1,0:T(8,128)S(1)} %bitcast_add_fusion.3), channel_id=1, source_target_pairs={{0,7},{1,0},{2,1},{3,2},{4,3},{5,4},{6,5},{7,6},{8,15},{9,8},{10,9... | collective-permute-start | bytes 393224 | tf_op jit(solution)/shard_map/ppermute | solution.py:136
  161.4 7.3 %collective-permute-start.8 = (f32[256,128]{1,0:T(8,128)S(1)}, f32[256,128]{1,0:T(8,128)S(1)}, u32[]{:S(2)}, u32[]{:S(2)}) collective-permute-start(f32[256,128]{1,0:T(8,128)S(1)} %bitcast_add_fusion.9), channel_id=1, source_target_pairs={{0,1},{1,2},{2,3},{3,4},{4,5},{5,6},{6,7},{7,0},{8,9},{9,10},{10,1... | collective-permute-start | bytes 393224 | tf_op jit(solution)/shard_map/ppermute | solution.py:136
  163.4 7.3 %collective-permute-start.15 = (f32[256,128]{1,0:T(8,128)S(1)}, f32[256,128]{1,0:T(8,128)S(1)}, u32[]{:S(2)}, u32[]{:S(2)}) collective-permute-start(f32[256,128]{1,0:T(8,128)S(1)} %bitcast_add_fusion.2), channel_id=1, source_target_pairs={{0,7},{1,0},{2,1},{3,2},{4,3},{5,4},{6,5},{7,6},{8,15},{9,8},{10,9... | collective-permute-start | bytes 393224 | tf_op jit(solution)/shard_map/ppermute | solution.py:136
  168.8 6.9 %collective-permute-start.9 = (f32[256,128]{1,0:T(8,128)S(1)}, f32[256,128]{1,0:T(8,128)S(1)}, u32[]{:S(2)}, u32[]{:S(2)}) collective-permute-start(f32[256,128]{1,0:T(8,128)S(1)} %bitcast_add_fusion.8), channel_id=1, source_target_pairs={{0,1},{1,2},{2,3},{3,4},{4,5},{5,6},{6,7},{7,0},{8,9},{9,10},{10,1... | collective-permute-start | bytes 393224 | tf_op jit(solution)/shard_map/ppermute | solution.py:136
  170.7 6.5 %collective-permute-start.16 = (f32[256,128]{1,0:T(8,128)S(1)}, f32[256,128]{1,0:T(8,128)S(1)}, u32[]{:S(2)}, u32[]{:S(2)}) collective-permute-start(f32[256,128]{1,0:T(8,128)S(1)} %bitcast_add_fusion.1), channel_id=1, source_target_pairs={{0,7},{1,0},{2,1},{3,2},{4,3},{5,4},{6,5},{7,6},{8,15},{9,8},{10,9... | collective-permute-start | bytes 393224 | tf_op jit(solution)/shard_map/ppermute | solution.py:136
Sparse Core Ops, SparseCore 0:
  79.1 39.3 reduce-scatter.1
  121.8 93.3 all-gather.1

commit v7 on v6

--- a/solution.py
+++ b/solution.py
@@ -107,22 +107,6 @@
     )
 
 
-def ring_all_gather(block, axis):
-    count = lax.axis_size(axis)
-    forward = [(i, (i + 1) % count) for i in range(count)]
-    backward = [(i, (i - 1) % count) for i in range(count)]
-    placed = {0: block}
-    ahead, behind = block, block
-    for step in range(1, (count - 1) // 2 + 1):
-        behind = lax.ppermute(behind, axis, forward)
-        ahead = lax.ppermute(ahead, axis, backward)
-        placed[count - step] = behind
-        placed[step] = ahead
-    if count % 2 == 0 and count > 1:
-        placed[count // 2] = lax.ppermute(behind, axis, forward)
-    return jnp.stack([placed[k] for k in range(count)])
-
-
 def ring_reduce_scatter(parts):
     count = parts.shape[0]
     axes = ("kvh", "rep")
@@ -151,9 +135,7 @@
     tok_rows = 2 * frames_dev * frame_max // 3
     heads_local = GROUP_HEADS // rep_count
     normed = layer_norm(vision_states, norm_gain)
-    kvh_index = lax.axis_index("kvh")
-    rows_dev = vision_states.shape[1]
-    frame_rows = ring_all_gather(normed[0], "kvh").reshape(1, frame_max, -1)
+    frame_rows = lax.all_gather(normed[0], "kvh", axis=0, tiled=False).reshape(1, frame_max, -1)
     hidden = jnp.einsum(
         "frv,vc->frc",
         frame_rows,
@@ -168,7 +150,6 @@
     slots = jnp.arange(cap_frame, dtype=jnp.int32)[None, None, :]
     frame_local = jnp.arange(frames_dev, dtype=jnp.int32)[None, :, None]
     row_of = jnp.mod(dest - my_starts[None, :, None], seq_count) + slots * seq_count
-    row_of = jnp.mod(row_of // rows_dev - kvh_index, lax.axis_size("kvh")) * rows_dev + row_of % rows_dev
     send_index = (frame_local * frame_max + row_of).reshape(-1)
     outgoing = visual_frames.reshape(frames_dev * frame_max, d_cols)[send_index]
     received = lax.all_to_all(outgoing, "seq", split_axis=0, concat_axis=0, tiled=True)

time: 246 us -> 239 us (0.972)
  blocking collectives: 0 us -> 22 us
  waiting for transfers between devices: 101 us -> 86.6 us
  starting transfers between devices: 77.3 us -> 64.9 us
    all_gather x0 -> x1, blocking collectives: none -> 22 us  [local(): lax.all_gather(normed[0], 'kvh', axis=0, tiled=False)]
    ppermute x3 -> x0, starting transfers between devices: 14.6 us -> none  [the longest x1 5.99 us: ring_all_gather(): placed[count // 2] = lax.ppermute(behind, axis, forward)]
    ppermute x3 -> x0, waiting for transfers between devices: 8.32 us -> none  [the longest x1 6.64 us: ring_all_gather(): placed[count // 2] = lax.ppermute(behind, axis, forward)]
    reduce_scatter x1, waiting for transfers between devices: 39.4 us -> 34.2 us  [local(): lax.psum_scatter(pair_part, ('kvh', 'rep'), scatter_dimension=0, tiled=True)]
  transfers between devices with their start and end apart: 20 -> 17, of which waited for: 13 -> 8; matrix products, arithmetic and copies ran while one was open for 6% -> 5% of each run, Pallas kernels for 0% -> 0%
where the time goes in v7:
time: 239 us; the launch traced here: 238 us
  waiting for transfers between devices  86.6 us (36%)
  starting transfers between devices  64.9 us (27%)
  blocking collectives  22 us (9%)
  Pallas kernels  21.6 us (9%)
  local copies, waits for them, and re-layouts  18.2 us (8%)
  between operations  14.3 us (6%)
  other arithmetic  7.08 us (3%)
  matrix products  3.34 us (1%)
    ppermute x14, starting transfers between devices, ring_reduce_scatter(): buf = lax.ppermute(buf, axes, perm)  48.4 us
    all_gather x1, waiting for transfers between devices, local(): pair_all = lax.all_gather(pair_own, 'seq', axis=0, tiled=False)  37.7 us
    reduce_scatter x1, waiting for transfers between devices, local(): lax.psum_scatter(pair_part, ('kvh', 'rep'), scatter_dimension=0, tiled=True)  34.2 us
    all_gather x1, blocking collectives, local(): lax.all_gather(normed[0], 'kvh', axis=0, tiled=False)  22 us
    pallas_call x1, Pallas kernels, causal_attention(): pl.pallas_call(functools.partial(attention_kernel, shards=shards, tok_row...  21.6 us
    all_to_all x1, starting transfers between devices, local(): lax.all_to_all(outgoing, 'seq', split_axis=0, concat_axis=0, tiled=True)  16.4 us
    all_to_all x1, waiting for transfers between devices, local(): lax.all_to_all(outgoing, 'seq', split_axis=0, concat_axis=0, tiled=True)  11.1 us
  transfers between devices with their start and end apart: 17, of which 8 were waited for; matrix products, arithmetic and copies ran while one was open for 5% of the time, Pallas kernels for 0%

profile of v7, /device:TPU:1, one launch (start us, length us, event | category | flops | bytes accessed | tf_op | source)
XLA Modules:
  0.0 238.1 jit_solution(15175093350700181127)
XLA Ops:
  6.5 1.1 convert_reduce_fusion
  7.7 1.2 fusion.12
  8.9 0.8 copy.74
  9.8 0.7 sub.92
  10.5 0.6 dynamic_slice.52
  11.1 0.7 and_select_fusion.1
  12.0 1.1 fusion.14
  13.1 22.0 %all_gather.7 = bf16[4,96,1152]{2,1,0:T(8,128)(2,1)S(1)} all-gather(bf16[1,96,1152]{2,1,0:T(8,128)(2,1)S(1)} %fusion.14), channel_id=1, replica_groups=mesh['seq'=64,'kvh'=4,'rep'=2] {'kvh'}, dimensions={0}, use_global_device_ids=true | all-gather | bytes 1105920 | tf_op jit(solution)/shard_map/all_gather | solution.py:138
  35.2 2.1 fusion.2
  37.3 0.2 copy.75
  37.5 2.1 gather_fusion
  39.5 1.0 all_to_all.8
  40.5 16.4 %all-to-all-start = ((bf16[64,6,448]{2,1,0:T(8,128)(2,1)}), bf16[64,6,448]{2,1,0:T(8,128)(2,1)S(1)}, u32[]{:S(2)}, u32[]{:S(2)}) async-start(bf16[64,6,448]{2,1,0:T(8,128)(2,1)} %all_to_all.8), calls=%async_computation | async-start | bytes 1048576 | tf_op jit(solution)/shard_map/all_to_all | solution.py:155
  57.0 4.6 %copy.76 = bf16[448,3072]{0,1:T(8,128)(2,1)} copy(bf16[448,3072]{1,0:T(8,128)(2,1)} %param.9) | data formatting | bytes 5505024 | tf_op args[4]
  61.6 1.3 slice.23
  63.2 11.1 %all-to-all-done = bf16[64,6,448]{2,1,0:T(8,128)(2,1)S(1)} async-done(((bf16[64,6,448]{2,1,0:T(8,128)(2,1)}), bf16[64,6,448]{2,1,0:T(8,128)(2,1)S(1)}, u32[]{:S(2)}, u32[]{:S(2)}) %all-to-all-start) | async-done | bytes 344096 | tf_op jit(solution)/shard_map/all_to_all | solution.py:155
  74.3 0.2 all_to_all.10
  74.5 1.2 gather_fusion.1
  75.7 0.5 convolution_bitcast_fusion.1
  76.2 1.5 broadcast_in_dim.12
  77.8 34.2 %reduce-scatter.2.cloned.1.call-done = f32[1,256,256]{2,1,0:T(8,128)} async-done(((f32[8,256,256]{2,1,0:T(8,128)}), f32[1,256,256]{2,1,0:T(8,128)}) %reduce-scatter.2.cloned.1.call-update) | async-done | bytes 262160 | tf_op jit(solution)/shard_map/reduce_scatter | solution.py:169
  112.0 1.6 convert_element_type.27
  113.9 1.8 slice.20
  115.7 0.7 convolution_bitcast_fusion
  116.5 0.2 fusion.23
  116.7 0.2 constant_dynamic-slice_fusion
  117.0 2.4 %collective-permute-start = (f32[256,128]{1,0:T(8,128)S(1)}, f32[256,128]{1,0:T(8,128)S(1)}, u32[]{:S(2)}, u32[]{:S(2)}) collective-permute-start(f32[256,128]{1,0:T(8,128)S(1)} %bitcast.78), channel_id=1, source_target_pairs={{0,1},{1,2},{2,3},{3,4},{4,5},{5,6},{6,7},{7,0},{8,9},{9,10},{10,1... | collective-permute-start | bytes 393224 | tf_op jit(solution)/shard_map/ppermute | solution.py:120
  121.0 4.1 %collective-permute-start.7 = (f32[256,128]{1,0:T(8,128)S(1)}, f32[256,128]{1,0:T(8,128)S(1)}, u32[]{:S(2)}, u32[]{:S(2)}) collective-permute-start(f32[256,128]{1,0:T(8,128)S(1)} %bitcast.79), channel_id=1, source_target_pairs={{0,7},{1,0},{2,1},{3,2},{4,3},{5,4},{6,5},{7,6},{8,15},{9,8},{10,9... | collective-permute-start | bytes 393224 | tf_op jit(solution)/shard_map/ppermute | solution.py:120
  125.1 1.9 collective-permute-start.1
  127.0 4.9 %collective-permute-start.8 = (f32[256,128]{1,0:T(8,128)S(1)}, f32[256,128]{1,0:T(8,128)S(1)}, u32[]{:S(2)}, u32[]{:S(2)}) collective-permute-start(f32[256,128]{1,0:T(8,128)S(1)} %bitcast_add_fusion.6), channel_id=1, source_target_pairs={{0,7},{1,0},{2,1},{3,2},{4,3},{5,4},{6,5},{7,6},{8,15},{9,8},{10,9... | collective-permute-start | bytes 393224 | tf_op jit(solution)/shard_map/ppermute | solution.py:120
  132.0 1.9 collective-permute-start.2
  133.9 0.3 collective-permute-done.8
  134.2 4.7 %collective-permute-start.9 = (f32[256,128]{1,0:T(8,128)S(1)}, f32[256,128]{1,0:T(8,128)S(1)}, u32[]{:S(2)}, u32[]{:S(2)}) collective-permute-start(f32[256,128]{1,0:T(8,128)S(1)} %bitcast_add_fusion.5), channel_id=1, source_target_pairs={{0,7},{1,0},{2,1},{3,2},{4,3},{5,4},{6,5},{7,6},{8,15},{9,8},{10,9... | collective-permute-start | bytes 393224 | tf_op jit(solution)/shard_map/ppermute | solution.py:120
  139.0 1.9 collective-permute-start.3
  140.9 0.7 collective-permute-done.9
  141.6 5.0 %collective-permute-start.10 = (f32[256,128]{1,0:T(8,128)S(1)}, f32[256,128]{1,0:T(8,128)S(1)}, u32[]{:S(2)}, u32[]{:S(2)}) collective-permute-start(f32[256,128]{1,0:T(8,128)S(1)} %bitcast_add_fusion.4), channel_id=1, source_target_pairs={{0,7},{1,0},{2,1},{3,2},{4,3},{5,4},{6,5},{7,6},{8,15},{9,8},{10,9... | collective-permute-start | bytes 393224 | tf_op jit(solution)/shard_map/ppermute | solution.py:120
  146.6 0.3 collective-permute-done.3
  146.9 1.9 collective-permute-start.4
  148.9 0.6 collective-permute-done.10
  149.5 5.3 %collective-permute-start.11 = (f32[256,128]{1,0:T(8,128)S(1)}, f32[256,128]{1,0:T(8,128)S(1)}, u32[]{:S(2)}, u32[]{:S(2)}) collective-permute-start(f32[256,128]{1,0:T(8,128)S(1)} %bitcast_add_fusion.3), channel_id=1, source_target_pairs={{0,7},{1,0},{2,1},{3,2},{4,3},{5,4},{6,5},{7,6},{8,15},{9,8},{10,9... | collective-permute-start | bytes 393224 | tf_op jit(solution)/shard_map/ppermute | solution.py:120
  154.8 1.9 collective-permute-start.5
  156.8 5.3 %collective-permute-start.12 = (f32[256,128]{1,0:T(8,128)S(1)}, f32[256,128]{1,0:T(8,128)S(1)}, u32[]{:S(2)}, u32[]{:S(2)}) collective-permute-start(f32[256,128]{1,0:T(8,128)S(1)} %bitcast_add_fusion.2), channel_id=1, source_target_pairs={{0,7},{1,0},{2,1},{3,2},{4,3},{5,4},{6,5},{7,6},{8,15},{9,8},{10,9... | collective-permute-start | bytes 393224 | tf_op jit(solution)/shard_map/ppermute | solution.py:120
  162.1 1.9 collective-permute-start.6
  164.1 5.1 %collective-permute-start.13 = (f32[256,128]{1,0:T(8,128)S(1)}, f32[256,128]{1,0:T(8,128)S(1)}, u32[]{:S(2)}, u32[]{:S(2)}) collective-permute-start(f32[256,128]{1,0:T(8,128)S(1)} %bitcast_add_fusion.1), channel_id=1, source_target_pairs={{0,7},{1,0},{2,1},{3,2},{4,3},{5,4},{6,5},{7,6},{8,15},{9,8},{10,9... | collective-permute-start | bytes 393224 | tf_op jit(solution)/shard_map/ppermute | solution.py:120
  169.2 1.7 collective-permute-done.13
  171.0 37.7 %all-gather.2.cloned.1.call-done = bf16[64,256,256]{2,1,0:T(8,128)(2,1)} async-done(((bf16[1,256,256]{2,1,0:T(8,128)(2,1)}), bf16[64,256,256]{2,1,0:T(8,128)(2,1)}) %all-gather.2.cloned.1.call-update) | async-done | bytes 8388624 | tf_op jit(solution)/shard_map/all_gather | solution.py:175
  208.7 21.6 %shard_map.55 = bf16[512,128]{1,0:T(8,128)(2,1)S(1)} custom-call(s32[1]{0:T(128)} %bitcast.seq_ref, bf16[512,128]{1,0:T(8,128)(2,1)S(1)} %bitcast.69, bf16[16384,256]{1,0:T(8,128)(2,1)} %bitcast.84), custom_call_target="tpu_custom_call" | custom-call | flops 3221225472 | bytes 8650752 | tf_op jit(solution)/shard_map/pallas_call | solution.py:87
  230.5 0.7 reshape.324
  (65 shorter events, 2.7 us)
Async XLA Ops:
  6.5 28.6 %copy-start = (bf16[1152,448]{0,1:T(8,128)(2,1)S(1)}, bf16[1152,448]{0,1:T(8,128)(2,1)}, u32[]{:S(2)}) copy-start(bf16[1152,448]{0,1:T(8,128)(2,1)} %param.8) | copy-start | bytes 3096580
  40.5 33.8 %all-to-all-start = ((bf16[64,6,448]{2,1,0:T(8,128)(2,1)}), bf16[64,6,448]{2,1,0:T(8,128)(2,1)S(1)}, u32[]{:S(2)}, u32[]{:S(2)}) async-start(bf16[64,6,448]{2,1,0:T(8,128)(2,1)} %all_to_all.8), calls=%async_computation | async-start | bytes 1048576 | tf_op jit(solution)/shard_map/all_to_all | solution.py:155
  57.0 55.0 %reduce-scatter.2.cloned.1.call-start = ((), (), s32[]{:S(2)}) async-start(), calls=%async_computation.2 | async-start | bytes 2359296 | tf_op jit(solution)/shard_map/reduce_scatter | solution.py:169
  61.6 1.4 copy-start.1
  77.7 131.0 %all-gather.2.cloned.1.call-start = ((), (), s32[]{:S(2)}) async-start(), calls=%async_computation.3 | async-start | bytes 8519680 | tf_op jit(solution)/shard_map/all_gather | solution.py:175
  117.0 8.0 %collective-permute-start = (f32[256,128]{1,0:T(8,128)S(1)}, f32[256,128]{1,0:T(8,128)S(1)}, u32[]{:S(2)}, u32[]{:S(2)}) collective-permute-start(f32[256,128]{1,0:T(8,128)S(1)} %bitcast.78), channel_id=1, source_target_pairs={{0,1},{1,2},{2,3},{3,4},{4,5},{5,6},{6,7},{7,0},{8,9},{9,10},{10,1... | collective-permute-start | bytes 393224 | tf_op jit(solution)/shard_map/ppermute | solution.py:120
  121.0 6.0 %collective-permute-start.7 = (f32[256,128]{1,0:T(8,128)S(1)}, f32[256,128]{1,0:T(8,128)S(1)}, u32[]{:S(2)}, u32[]{:S(2)}) collective-permute-start(f32[256,128]{1,0:T(8,128)S(1)} %bitcast.79), channel_id=1, source_target_pairs={{0,7},{1,0},{2,1},{3,2},{4,3},{5,4},{6,5},{7,6},{8,15},{9,8},{10,9... | collective-permute-start | bytes 393224 | tf_op jit(solution)/shard_map/ppermute | solution.py:120
  125.1 6.9 %collective-permute-start.1 = (f32[256,128]{1,0:T(8,128)S(1)}, f32[256,128]{1,0:T(8,128)S(1)}, u32[]{:S(2)}, u32[]{:S(2)}) collective-permute-start(f32[256,128]{1,0:T(8,128)S(1)} %bitcast_add_fusion.13), channel_id=1, source_target_pairs={{0,1},{1,2},{2,3},{3,4},{4,5},{5,6},{6,7},{7,0},{8,9},{9,10},{10,1... | collective-permute-start | bytes 393224 | tf_op jit(solution)/shard_map/ppermute | solution.py:120
  127.0 7.2 %collective-permute-start.8 = (f32[256,128]{1,0:T(8,128)S(1)}, f32[256,128]{1,0:T(8,128)S(1)}, u32[]{:S(2)}, u32[]{:S(2)}) collective-permute-start(f32[256,128]{1,0:T(8,128)S(1)} %bitcast_add_fusion.6), channel_id=1, source_target_pairs={{0,7},{1,0},{2,1},{3,2},{4,3},{5,4},{6,5},{7,6},{8,15},{9,8},{10,9... | collective-permute-start | bytes 393224 | tf_op jit(solution)/shard_map/ppermute | solution.py:120
  132.0 7.0 %collective-permute-start.2 = (f32[256,128]{1,0:T(8,128)S(1)}, f32[256,128]{1,0:T(8,128)S(1)}, u32[]{:S(2)}, u32[]{:S(2)}) collective-permute-start(f32[256,128]{1,0:T(8,128)S(1)} %bitcast_add_fusion.12), channel_id=1, source_target_pairs={{0,1},{1,2},{2,3},{3,4},{4,5},{5,6},{6,7},{7,0},{8,9},{9,10},{10,1... | collective-permute-start | bytes 393224 | tf_op jit(solution)/shard_map/ppermute | solution.py:120
  134.2 7.4 %collective-permute-start.9 = (f32[256,128]{1,0:T(8,128)S(1)}, f32[256,128]{1,0:T(8,128)S(1)}, u32[]{:S(2)}, u32[]{:S(2)}) collective-permute-start(f32[256,128]{1,0:T(8,128)S(1)} %bitcast_add_fusion.5), channel_id=1, source_target_pairs={{0,7},{1,0},{2,1},{3,2},{4,3},{5,4},{6,5},{7,6},{8,15},{9,8},{10,9... | collective-permute-start | bytes 393224 | tf_op jit(solution)/shard_map/ppermute | solution.py:120
  139.0 7.9 %collective-permute-start.3 = (f32[256,128]{1,0:T(8,128)S(1)}, f32[256,128]{1,0:T(8,128)S(1)}, u32[]{:S(2)}, u32[]{:S(2)}) collective-permute-start(f32[256,128]{1,0:T(8,128)S(1)} %bitcast_add_fusion.11), channel_id=1, source_target_pairs={{0,1},{1,2},{2,3},{3,4},{4,5},{5,6},{6,7},{7,0},{8,9},{9,10},{10,1... | collective-permute-start | bytes 393224 | tf_op jit(solution)/shard_map/ppermute | solution.py:120
  141.6 7.9 %collective-permute-start.10 = (f32[256,128]{1,0:T(8,128)S(1)}, f32[256,128]{1,0:T(8,128)S(1)}, u32[]{:S(2)}, u32[]{:S(2)}) collective-permute-start(f32[256,128]{1,0:T(8,128)S(1)} %bitcast_add_fusion.4), channel_id=1, source_target_pairs={{0,7},{1,0},{2,1},{3,2},{4,3},{5,4},{6,5},{7,6},{8,15},{9,8},{10,9... | collective-permute-start | bytes 393224 | tf_op jit(solution)/shard_map/ppermute | solution.py:120
  146.9 7.9 %collective-permute-start.4 = (f32[256,128]{1,0:T(8,128)S(1)}, f32[256,128]{1,0:T(8,128)S(1)}, u32[]{:S(2)}, u32[]{:S(2)}) collective-permute-start(f32[256,128]{1,0:T(8,128)S(1)} %bitcast_add_fusion.10), channel_id=1, source_target_pairs={{0,1},{1,2},{2,3},{3,4},{4,5},{5,6},{6,7},{7,0},{8,9},{9,10},{10,1... | collective-permute-start | bytes 393224 | tf_op jit(solution)/shard_map/ppermute | solution.py:120
  149.5 7.3 %collective-permute-start.11 = (f32[256,128]{1,0:T(8,128)S(1)}, f32[256,128]{1,0:T(8,128)S(1)}, u32[]{:S(2)}, u32[]{:S(2)}) collective-permute-start(f32[256,128]{1,0:T(8,128)S(1)} %bitcast_add_fusion.3), channel_id=1, source_target_pairs={{0,7},{1,0},{2,1},{3,2},{4,3},{5,4},{6,5},{7,6},{8,15},{9,8},{10,9... | collective-permute-start | bytes 393224 | tf_op jit(solution)/shard_map/ppermute | solution.py:120
  154.8 7.2 %collective-permute-start.5 = (f32[256,128]{1,0:T(8,128)S(1)}, f32[256,128]{1,0:T(8,128)S(1)}, u32[]{:S(2)}, u32[]{:S(2)}) collective-permute-start(f32[256,128]{1,0:T(8,128)S(1)} %bitcast_add_fusion.9), channel_id=1, source_target_pairs={{0,1},{1,2},{2,3},{3,4},{4,5},{5,6},{6,7},{7,0},{8,9},{9,10},{10,1... | collective-permute-start | bytes 393224 | tf_op jit(solution)/shard_map/ppermute | solution.py:120
  156.8 7.2 %collective-permute-start.12 = (f32[256,128]{1,0:T(8,128)S(1)}, f32[256,128]{1,0:T(8,128)S(1)}, u32[]{:S(2)}, u32[]{:S(2)}) collective-permute-start(f32[256,128]{1,0:T(8,128)S(1)} %bitcast_add_fusion.2), channel_id=1, source_target_pairs={{0,7},{1,0},{2,1},{3,2},{4,3},{5,4},{6,5},{7,6},{8,15},{9,8},{10,9... | collective-permute-start | bytes 393224 | tf_op jit(solution)/shard_map/ppermute | solution.py:120
  162.1 7.1 %collective-permute-start.6 = (f32[256,128]{1,0:T(8,128)S(1)}, f32[256,128]{1,0:T(8,128)S(1)}, u32[]{:S(2)}, u32[]{:S(2)}) collective-permute-start(f32[256,128]{1,0:T(8,128)S(1)} %bitcast_add_fusion.8), channel_id=1, source_target_pairs={{0,1},{1,2},{2,3},{3,4},{4,5},{5,6},{6,7},{7,0},{8,9},{9,10},{10,1... | collective-permute-start | bytes 393224 | tf_op jit(solution)/shard_map/ppermute | solution.py:120
  164.1 6.9 %collective-permute-start.13 = (f32[256,128]{1,0:T(8,128)S(1)}, f32[256,128]{1,0:T(8,128)S(1)}, u32[]{:S(2)}, u32[]{:S(2)}) collective-permute-start(f32[256,128]{1,0:T(8,128)S(1)} %bitcast_add_fusion.1), channel_id=1, source_target_pairs={{0,7},{1,0},{2,1},{3,2},{4,3},{5,4},{6,5},{7,6},{8,15},{9,8},{10,9... | collective-permute-start | bytes 393224 | tf_op jit(solution)/shard_map/ppermute | solution.py:120
Sparse Core Ops, SparseCore 0:
  77.8 34.0 reduce-scatter.1
  115.3 93.3 all-gather.1

commit v8 on v7

--- a/solution.py
+++ b/solution.py
@@ -167,8 +167,8 @@
         pair_part[:, None], (KV_HEADS, rep_count) + pair_part.shape[1:]
     ).reshape((KV_HEADS * rep_count,) + pair_part.shape[1:])
     pair_own = lax.psum_scatter(
-        pair_part, ("kvh", "rep"), scatter_dimension=0, tiled=True
-    )[0].astype(jnp.bfloat16)
+        pair_part.astype(jnp.bfloat16), ("kvh", "rep"), scatter_dimension=0, tiled=True
+    )[0]
     query_part = jnp.einsum("tc,cpw->ptw", visual, query_w, preferred_element_type=jnp.float32)
     queries = ring_reduce_scatter(query_part).astype(jnp.bfloat16)
     queries = queries.reshape(tok_rows, heads_local, HEAD_DIM)

time: 239 us -> 235 us (0.983)
  waiting for transfers between devices: 86.6 us -> 84.2 us
    reduce_scatter x1, waiting for transfers between devices: 34.2 us -> 30.3 us  [local(): lax.psum_scatter(pair_part.astype(jnp.bfloat16), ('kvh', 'rep'), scatter_...]
  transfers between devices with their start and end apart: 17 -> 17, of which waited for: 8 -> 9; matrix products, arithmetic and copies ran while one was open for 5% -> 5% of each run, Pallas kernels for 0% -> 0%
where the time goes in v8:
time: 235 us; the launch traced here: 234 us
  waiting for transfers between devices  84.2 us (36%)
  starting transfers between devices  65.5 us (28%)
  blocking collectives  22 us (9%)
  Pallas kernels  21.6 us (9%)
  local copies, waits for them, and re-layouts  17.7 us (8%)
  between operations  14.3 us (6%)
  other arithmetic  5.4 us (2%)
  matrix products  3.34 us (1%)
    ppermute x14, starting transfers between devices, ring_reduce_scatter(): buf = lax.ppermute(buf, axes, perm)  48.9 us
    all_gather x1, waiting for transfers between devices, local(): pair_all = lax.all_gather(pair_own, 'seq', axis=0, tiled=False)  38.8 us
    reduce_scatter x1, waiting for transfers between devices, local(): lax.psum_scatter(pair_part.astype(jnp.bfloat16), ('kvh', 'rep'), scatter_...  30.3 us
    all_gather x1, blocking collectives, local(): lax.all_gather(normed[0], 'kvh', axis=0, tiled=False)  22 us
    pallas_call x1, Pallas kernels, causal_attention(): pl.pallas_call(functools.partial(attention_kernel, shards=shards, tok_row...  21.6 us
    all_to_all x1, starting transfers between devices, local(): lax.all_to_all(outgoing, 'seq', split_axis=0, concat_axis=0, tiled=True)  16.5 us
    all_to_all x1, waiting for transfers between devices, local(): lax.all_to_all(outgoing, 'seq', split_axis=0, concat_axis=0, tiled=True)  11.1 us
  transfers between devices with their start and end apart: 17, of which 9 were waited for; matrix products, arithmetic and copies ran while one was open for 5% of the time, Pallas kernels for 0%

profile of v8, /device:TPU:1, one launch (start us, length us, event | category | flops | bytes accessed | tf_op | source)
XLA Modules:
  0.0 234.1 jit_solution(868152760406672258)
XLA Ops:
  6.5 1.1 convert_reduce_fusion
  7.7 1.2 fusion.13
  8.9 0.8 copy.74
  9.8 0.7 sub.92
  10.5 0.6 dynamic_slice.52
  11.1 0.6 and_select_fusion.1
  11.8 0.1 add.283
  12.0 1.1 fusion.15
  13.1 22.0 %all_gather.6 = bf16[4,96,1152]{2,1,0:T(8,128)(2,1)S(1)} all-gather(bf16[1,96,1152]{2,1,0:T(8,128)(2,1)S(1)} %fusion.15), channel_id=1, replica_groups=mesh['seq'=64,'kvh'=4,'rep'=2] {'kvh'}, dimensions={0}, use_global_device_ids=true | all-gather | bytes 1105920 | tf_op jit(solution)/shard_map/all_gather | solution.py:138
  35.2 2.1 fusion.3
  37.3 0.2 copy.75
  37.5 2.1 gather_fusion
  39.5 1.0 all_to_all.8
  40.5 16.5 %all-to-all-start = ((bf16[64,6,448]{2,1,0:T(8,128)(2,1)}), bf16[64,6,448]{2,1,0:T(8,128)(2,1)S(1)}, u32[]{:S(2)}, u32[]{:S(2)}) async-start(bf16[64,6,448]{2,1,0:T(8,128)(2,1)} %all_to_all.8), calls=%async_computation | async-start | bytes 1048576 | tf_op jit(solution)/shard_map/all_to_all | solution.py:155
  57.0 4.6 %copy.76 = bf16[448,3072]{0,1:T(8,128)(2,1)} copy(bf16[448,3072]{1,0:T(8,128)(2,1)} %param.9) | data formatting | bytes 5505024 | tf_op args[4]
  61.6 1.3 slice.23
  63.1 11.1 %all-to-all-done = bf16[64,6,448]{2,1,0:T(8,128)(2,1)S(1)} async-done(((bf16[64,6,448]{2,1,0:T(8,128)(2,1)}), bf16[64,6,448]{2,1,0:T(8,128)(2,1)S(1)}, u32[]{:S(2)}, u32[]{:S(2)}) %all-to-all-start) | async-done | bytes 344096 | tf_op jit(solution)/shard_map/all_to_all | solution.py:155
  74.3 0.2 all_to_all.10
  74.5 1.2 gather_fusion.1
  75.7 0.5 fusion
  76.2 1.0 broadcast_in_dim.12
  77.3 30.3 %reduce-scatter.2.cloned.1.call-done = bf16[1,256,256]{2,1,0:T(8,128)(2,1)} async-done(((bf16[8,256,256]{2,1,0:T(8,128)(2,1)}), bf16[1,256,256]{2,1,0:T(8,128)(2,1)}) %reduce-scatter.2.cloned.1.call-update) | async-done | bytes 131088 | tf_op jit(solution)/shard_map/reduce_scatter | solution.py:169
  107.9 1.8 slice.20
  109.8 0.7 convolution_bitcast_fusion
  110.6 0.2 fusion.24
  110.7 0.2 constant_dynamic-slice_fusion
  111.1 2.4 %collective-permute-start = (f32[256,128]{1,0:T(8,128)S(1)}, f32[256,128]{1,0:T(8,128)S(1)}, u32[]{:S(2)}, u32[]{:S(2)}) collective-permute-start(f32[256,128]{1,0:T(8,128)S(1)} %bitcast.78), channel_id=1, source_target_pairs={{0,1},{1,2},{2,3},{3,4},{4,5},{5,6},{6,7},{7,0},{8,9},{9,10},{10,1... | collective-permute-start | bytes 393224 | tf_op jit(solution)/shard_map/ppermute | solution.py:120
  115.0 4.1 %collective-permute-start.7 = (f32[256,128]{1,0:T(8,128)S(1)}, f32[256,128]{1,0:T(8,128)S(1)}, u32[]{:S(2)}, u32[]{:S(2)}) collective-permute-start(f32[256,128]{1,0:T(8,128)S(1)} %bitcast.79), channel_id=1, source_target_pairs={{0,7},{1,0},{2,1},{3,2},{4,3},{5,4},{6,5},{7,6},{8,15},{9,8},{10,9... | collective-permute-start | bytes 393224 | tf_op jit(solution)/shard_map/ppermute | solution.py:120
  119.1 1.9 collective-permute-start.1
  121.1 4.9 %collective-permute-start.8 = (f32[256,128]{1,0:T(8,128)S(1)}, f32[256,128]{1,0:T(8,128)S(1)}, u32[]{:S(2)}, u32[]{:S(2)}) collective-permute-start(f32[256,128]{1,0:T(8,128)S(1)} %bitcast_add_fusion.6), channel_id=1, source_target_pairs={{0,7},{1,0},{2,1},{3,2},{4,3},{5,4},{6,5},{7,6},{8,15},{9,8},{10,9... | collective-permute-start | bytes 393224 | tf_op jit(solution)/shard_map/ppermute | solution.py:120
  126.1 1.9 collective-permute-start.2
  128.0 0.3 collective-permute-done.8
  128.3 5.0 %collective-permute-start.9 = (f32[256,128]{1,0:T(8,128)S(1)}, f32[256,128]{1,0:T(8,128)S(1)}, u32[]{:S(2)}, u32[]{:S(2)}) collective-permute-start(f32[256,128]{1,0:T(8,128)S(1)} %bitcast_add_fusion.5), channel_id=1, source_target_pairs={{0,7},{1,0},{2,1},{3,2},{4,3},{5,4},{6,5},{7,6},{8,15},{9,8},{10,9... | collective-permute-start | bytes 393224 | tf_op jit(solution)/shard_map/ppermute | solution.py:120
  133.3 0.3 collective-permute-done.2
  133.6 1.9 collective-permute-start.3
  135.5 1.0 collective-permute-done.9
  136.5 5.3 %collective-permute-start.10 = (f32[256,128]{1,0:T(8,128)S(1)}, f32[256,128]{1,0:T(8,128)S(1)}, u32[]{:S(2)}, u32[]{:S(2)}) collective-permute-start(f32[256,128]{1,0:T(8,128)S(1)} %bitcast_add_fusion.4), channel_id=1, source_target_pairs={{0,7},{1,0},{2,1},{3,2},{4,3},{5,4},{6,5},{7,6},{8,15},{9,8},{10,9... | collective-permute-start | bytes 393224 | tf_op jit(solution)/shard_map/ppermute | solution.py:120
  142.0 1.9 collective-permute-start.4
  143.9 0.4 collective-permute-done.10
  144.3 5.3 %collective-permute-start.11 = (f32[256,128]{1,0:T(8,128)S(1)}, f32[256,128]{1,0:T(8,128)S(1)}, u32[]{:S(2)}, u32[]{:S(2)}) collective-permute-start(f32[256,128]{1,0:T(8,128)S(1)} %bitcast_add_fusion.3), channel_id=1, source_target_pairs={{0,7},{1,0},{2,1},{3,2},{4,3},{5,4},{6,5},{7,6},{8,15},{9,8},{10,9... | collective-permute-start | bytes 393224 | tf_op jit(solution)/shard_map/ppermute | solution.py:120
  149.7 1.9 collective-permute-start.5
  151.6 5.3 %collective-permute-start.12 = (f32[256,128]{1,0:T(8,128)S(1)}, f32[256,128]{1,0:T(8,128)S(1)}, u32[]{:S(2)}, u32[]{:S(2)}) collective-permute-start(f32[256,128]{1,0:T(8,128)S(1)} %bitcast_add_fusion.2), channel_id=1, source_target_pairs={{0,7},{1,0},{2,1},{3,2},{4,3},{5,4},{6,5},{7,6},{8,15},{9,8},{10,9... | collective-permute-start | bytes 393224 | tf_op jit(solution)/shard_map/ppermute | solution.py:120
  156.9 1.9 collective-permute-start.6
  158.9 5.1 %collective-permute-start.13 = (f32[256,128]{1,0:T(8,128)S(1)}, f32[256,128]{1,0:T(8,128)S(1)}, u32[]{:S(2)}, u32[]{:S(2)}) collective-permute-start(f32[256,128]{1,0:T(8,128)S(1)} %bitcast_add_fusion.1), channel_id=1, source_target_pairs={{0,7},{1,0},{2,1},{3,2},{4,3},{5,4},{6,5},{7,6},{8,15},{9,8},{10,9... | collective-permute-start | bytes 393224 | tf_op jit(solution)/shard_map/ppermute | solution.py:120
  164.1 1.7 collective-permute-done.13
  165.9 38.8 %all-gather.2.cloned.1.call-done = bf16[64,256,256]{2,1,0:T(8,128)(2,1)} async-done(((bf16[1,256,256]{2,1,0:T(8,128)(2,1)}), bf16[64,256,256]{2,1,0:T(8,128)(2,1)}) %all-gather.2.cloned.1.call-update) | async-done | bytes 8388624 | tf_op jit(solution)/shard_map/all_gather | solution.py:175
  204.7 21.6 %shard_map.55 = bf16[512,128]{1,0:T(8,128)(2,1)S(1)} custom-call(s32[1]{0:T(128)} %bitcast.seq_ref, bf16[512,128]{1,0:T(8,128)(2,1)S(1)} %bitcast.69, bf16[16384,256]{1,0:T(8,128)(2,1)} %bitcast.84), custom_call_target="tpu_custom_call" | custom-call | flops 3221225472 | bytes 8650752 | tf_op jit(solution)/shard_map/pallas_call | solution.py:87
  226.5 0.7 reshape.322
  (64 shorter events, 2.6 us)
Async XLA Ops:
  6.5 28.6 %copy-start = (bf16[1152,448]{0,1:T(8,128)(2,1)S(1)}, bf16[1152,448]{0,1:T(8,128)(2,1)}, u32[]{:S(2)}) copy-start(bf16[1152,448]{0,1:T(8,128)(2,1)} %param.8) | copy-start | bytes 3096580
  40.5 33.8 %all-to-all-start = ((bf16[64,6,448]{2,1,0:T(8,128)(2,1)}), bf16[64,6,448]{2,1,0:T(8,128)(2,1)S(1)}, u32[]{:S(2)}, u32[]{:S(2)}) async-start(bf16[64,6,448]{2,1,0:T(8,128)(2,1)} %all_to_all.8), calls=%async_computation | async-start | bytes 1048576 | tf_op jit(solution)/shard_map/all_to_all | solution.py:155
  57.0 50.7 %reduce-scatter.2.cloned.1.call-start = ((), (), s32[]{:S(2)}) async-start(), calls=%async_computation.2 | async-start | bytes 1179648 | tf_op jit(solution)/shard_map/reduce_scatter | solution.py:169
  61.6 1.4 copy-start.1
  77.2 127.5 %all-gather.2.cloned.1.call-start = ((), (), s32[]{:S(2)}) async-start(), calls=%async_computation.3 | async-start | bytes 8519680 | tf_op jit(solution)/shard_map/all_gather | solution.py:175
  111.1 8.0 %collective-permute-start = (f32[256,128]{1,0:T(8,128)S(1)}, f32[256,128]{1,0:T(8,128)S(1)}, u32[]{:S(2)}, u32[]{:S(2)}) collective-permute-start(f32[256,128]{1,0:T(8,128)S(1)} %bitcast.78), channel_id=1, source_target_pairs={{0,1},{1,2},{2,3},{3,4},{4,5},{5,6},{6,7},{7,0},{8,9},{9,10},{10,1... | collective-permute-start | bytes 393224 | tf_op jit(solution)/shard_map/ppermute | solution.py:120
  115.0 6.1 %collective-permute-start.7 = (f32[256,128]{1,0:T(8,128)S(1)}, f32[256,128]{1,0:T(8,128)S(1)}, u32[]{:S(2)}, u32[]{:S(2)}) collective-permute-start(f32[256,128]{1,0:T(8,128)S(1)} %bitcast.79), channel_id=1, source_target_pairs={{0,7},{1,0},{2,1},{3,2},{4,3},{5,4},{6,5},{7,6},{8,15},{9,8},{10,9... | collective-permute-start | bytes 393224 | tf_op jit(solution)/shard_map/ppermute | solution.py:120
  119.1 6.9 %collective-permute-start.1 = (f32[256,128]{1,0:T(8,128)S(1)}, f32[256,128]{1,0:T(8,128)S(1)}, u32[]{:S(2)}, u32[]{:S(2)}) collective-permute-start(f32[256,128]{1,0:T(8,128)S(1)} %bitcast_add_fusion.13), channel_id=1, source_target_pairs={{0,1},{1,2},{2,3},{3,4},{4,5},{5,6},{6,7},{7,0},{8,9},{9,10},{10,1... | collective-permute-start | bytes 393224 | tf_op jit(solution)/shard_map/ppermute | solution.py:120
  121.1 7.2 %collective-permute-start.8 = (f32[256,128]{1,0:T(8,128)S(1)}, f32[256,128]{1,0:T(8,128)S(1)}, u32[]{:S(2)}, u32[]{:S(2)}) collective-permute-start(f32[256,128]{1,0:T(8,128)S(1)} %bitcast_add_fusion.6), channel_id=1, source_target_pairs={{0,7},{1,0},{2,1},{3,2},{4,3},{5,4},{6,5},{7,6},{8,15},{9,8},{10,9... | collective-permute-start | bytes 393224 | tf_op jit(solution)/shard_map/ppermute | solution.py:120
  126.1 7.5 %collective-permute-start.2 = (f32[256,128]{1,0:T(8,128)S(1)}, f32[256,128]{1,0:T(8,128)S(1)}, u32[]{:S(2)}, u32[]{:S(2)}) collective-permute-start(f32[256,128]{1,0:T(8,128)S(1)} %bitcast_add_fusion.12), channel_id=1, source_target_pairs={{0,1},{1,2},{2,3},{3,4},{4,5},{5,6},{6,7},{7,0},{8,9},{9,10},{10,1... | collective-permute-start | bytes 393224 | tf_op jit(solution)/shard_map/ppermute | solution.py:120
  128.3 8.2 %collective-permute-start.9 = (f32[256,128]{1,0:T(8,128)S(1)}, f32[256,128]{1,0:T(8,128)S(1)}, u32[]{:S(2)}, u32[]{:S(2)}) collective-permute-start(f32[256,128]{1,0:T(8,128)S(1)} %bitcast_add_fusion.5), channel_id=1, source_target_pairs={{0,7},{1,0},{2,1},{3,2},{4,3},{5,4},{6,5},{7,6},{8,15},{9,8},{10,9... | collective-permute-start | bytes 393224 | tf_op jit(solution)/shard_map/ppermute | solution.py:120
  133.6 8.4 %collective-permute-start.3 = (f32[256,128]{1,0:T(8,128)S(1)}, f32[256,128]{1,0:T(8,128)S(1)}, u32[]{:S(2)}, u32[]{:S(2)}) collective-permute-start(f32[256,128]{1,0:T(8,128)S(1)} %bitcast_add_fusion.11), channel_id=1, source_target_pairs={{0,1},{1,2},{2,3},{3,4},{4,5},{5,6},{6,7},{7,0},{8,9},{9,10},{10,1... | collective-permute-start | bytes 393224 | tf_op jit(solution)/shard_map/ppermute | solution.py:120
  136.5 7.7 %collective-permute-start.10 = (f32[256,128]{1,0:T(8,128)S(1)}, f32[256,128]{1,0:T(8,128)S(1)}, u32[]{:S(2)}, u32[]{:S(2)}) collective-permute-start(f32[256,128]{1,0:T(8,128)S(1)} %bitcast_add_fusion.4), channel_id=1, source_target_pairs={{0,7},{1,0},{2,1},{3,2},{4,3},{5,4},{6,5},{7,6},{8,15},{9,8},{10,9... | collective-permute-start | bytes 393224 | tf_op jit(solution)/shard_map/ppermute | solution.py:120
  142.0 7.7 %collective-permute-start.4 = (f32[256,128]{1,0:T(8,128)S(1)}, f32[256,128]{1,0:T(8,128)S(1)}, u32[]{:S(2)}, u32[]{:S(2)}) collective-permute-start(f32[256,128]{1,0:T(8,128)S(1)} %bitcast_add_fusion.10), channel_id=1, source_target_pairs={{0,1},{1,2},{2,3},{3,4},{4,5},{5,6},{6,7},{7,0},{8,9},{9,10},{10,1... | collective-permute-start | bytes 393224 | tf_op jit(solution)/shard_map/ppermute | solution.py:120
  144.3 7.3 %collective-permute-start.11 = (f32[256,128]{1,0:T(8,128)S(1)}, f32[256,128]{1,0:T(8,128)S(1)}, u32[]{:S(2)}, u32[]{:S(2)}) collective-permute-start(f32[256,128]{1,0:T(8,128)S(1)} %bitcast_add_fusion.3), channel_id=1, source_target_pairs={{0,7},{1,0},{2,1},{3,2},{4,3},{5,4},{6,5},{7,6},{8,15},{9,8},{10,9... | collective-permute-start | bytes 393224 | tf_op jit(solution)/shard_map/ppermute | solution.py:120
  149.7 7.2 %collective-permute-start.5 = (f32[256,128]{1,0:T(8,128)S(1)}, f32[256,128]{1,0:T(8,128)S(1)}, u32[]{:S(2)}, u32[]{:S(2)}) collective-permute-start(f32[256,128]{1,0:T(8,128)S(1)} %bitcast_add_fusion.9), channel_id=1, source_target_pairs={{0,1},{1,2},{2,3},{3,4},{4,5},{5,6},{6,7},{7,0},{8,9},{9,10},{10,1... | collective-permute-start | bytes 393224 | tf_op jit(solution)/shard_map/ppermute | solution.py:120
  151.6 7.2 %collective-permute-start.12 = (f32[256,128]{1,0:T(8,128)S(1)}, f32[256,128]{1,0:T(8,128)S(1)}, u32[]{:S(2)}, u32[]{:S(2)}) collective-permute-start(f32[256,128]{1,0:T(8,128)S(1)} %bitcast_add_fusion.2), channel_id=1, source_target_pairs={{0,7},{1,0},{2,1},{3,2},{4,3},{5,4},{6,5},{7,6},{8,15},{9,8},{10,9... | collective-permute-start | bytes 393224 | tf_op jit(solution)/shard_map/ppermute | solution.py:120
  156.9 7.1 %collective-permute-start.6 = (f32[256,128]{1,0:T(8,128)S(1)}, f32[256,128]{1,0:T(8,128)S(1)}, u32[]{:S(2)}, u32[]{:S(2)}) collective-permute-start(f32[256,128]{1,0:T(8,128)S(1)} %bitcast_add_fusion.8), channel_id=1, source_target_pairs={{0,1},{1,2},{2,3},{3,4},{4,5},{5,6},{6,7},{7,0},{8,9},{9,10},{10,1... | collective-permute-start | bytes 393224 | tf_op jit(solution)/shard_map/ppermute | solution.py:120
  158.9 6.9 %collective-permute-start.13 = (f32[256,128]{1,0:T(8,128)S(1)}, f32[256,128]{1,0:T(8,128)S(1)}, u32[]{:S(2)}, u32[]{:S(2)}) collective-permute-start(f32[256,128]{1,0:T(8,128)S(1)} %bitcast_add_fusion.1), channel_id=1, source_target_pairs={{0,7},{1,0},{2,1},{3,2},{4,3},{5,4},{6,5},{7,6},{8,15},{9,8},{10,9... | collective-permute-start | bytes 393224 | tf_op jit(solution)/shard_map/ppermute | solution.py:120
Sparse Core Ops, SparseCore 0:
  77.4 30.2 reduce-scatter.1
  111.0 93.6 all-gather.1

commit v9 on v7

--- a/solution.py
+++ b/solution.py
@@ -161,11 +161,11 @@
     visual = received[slot_index]
     wide = head_weights.reshape(d_cols, KV_HEADS, GROUP_HEADS + 2, HEAD_DIM)
     query_w = wide[:, :, :GROUP_HEADS].reshape(d_cols, KV_HEADS * rep_count, heads_local * HEAD_DIM)
-    pair_w = wide[:, :, GROUP_HEADS:].reshape(d_cols, KV_HEADS, 2 * HEAD_DIM)
-    pair_part = jnp.einsum("tc,cgw->gtw", visual, pair_w, preferred_element_type=jnp.float32)
-    pair_part = jnp.broadcast_to(
-        pair_part[:, None], (KV_HEADS, rep_count) + pair_part.shape[1:]
-    ).reshape((KV_HEADS * rep_count,) + pair_part.shape[1:])
+    pair_w = wide[:, :, GROUP_HEADS:].reshape(d_cols, KV_HEADS, 1, 2 * HEAD_DIM)
+    pair_w = jnp.broadcast_to(pair_w, (d_cols, KV_HEADS, rep_count, 2 * HEAD_DIM)).reshape(
+        d_cols, KV_HEADS * rep_count, 2 * HEAD_DIM
+    )
+    pair_part = jnp.einsum("tc,cpw->ptw", visual, pair_w, preferred_element_type=jnp.float32)
     pair_own = lax.psum_scatter(
         pair_part, ("kvh", "rep"), scatter_dimension=0, tiled=True
     )[0].astype(jnp.bfloat16)

time: 239 us -> 239 us (level)
  transfers between devices with their start and end apart: 17 -> 17, of which waited for: 8 -> 12; matrix products, arithmetic and copies ran while one was open for 5% -> 5% of each run, Pallas kernels for 0% -> 0%
where the time goes in v9:
time: 239 us; the launch traced here: 238 us
  waiting for transfers between devices  87.5 us (37%)
  starting transfers between devices  63.5 us (27%)
  blocking collectives  22 us (9%)
  Pallas kernels  21.6 us (9%)
  local copies, waits for them, and re-layouts  17.3 us (7%)
  between operations  14.3 us (6%)
  other arithmetic  7.05 us (3%)
  matrix products  4.9 us (2%)
    ppermute x14, starting transfers between devices, ring_reduce_scatter(): buf = lax.ppermute(buf, axes, perm)  47 us
    all_gather x1, waiting for transfers between devices, local(): pair_all = lax.all_gather(pair_own, 'seq', axis=0, tiled=False)  38.7 us
    reduce_scatter x1, waiting for transfers between devices, local(): lax.psum_scatter(pair_part, ('kvh', 'rep'), scatter_dimension=0, tiled=True)  33.3 us
    all_gather x1, blocking collectives, local(): lax.all_gather(normed[0], 'kvh', axis=0, tiled=False)  22 us
    pallas_call x1, Pallas kernels, causal_attention(): pl.pallas_call(functools.partial(attention_kernel, shards=shards, tok_row...  21.6 us
    all_to_all x1, starting transfers between devices, local(): lax.all_to_all(outgoing, 'seq', split_axis=0, concat_axis=0, tiled=True)  16.4 us
    all_to_all x1, waiting for transfers between devices, local(): lax.all_to_all(outgoing, 'seq', split_axis=0, concat_axis=0, tiled=True)  10.6 us
    ppermute x14, waiting for transfers between devices, ring_reduce_scatter(): buf = lax.ppermute(buf, axes, perm)  4.95 us
  transfers between devices with their start and end apart: 17, of which 12 were waited for; matrix products, arithmetic and copies ran while one was open for 5% of the time, Pallas kernels for 0%

profile of v9, /device:TPU:1, one launch (start us, length us, event | category | flops | bytes accessed | tf_op | source)
XLA Modules:
  0.0 238.3 jit_solution(8727778770419199426)
XLA Ops:
  6.5 1.1 convert_reduce_fusion
  7.7 1.2 fusion.12
  8.9 0.8 copy.74
  9.8 0.7 sub.92
  10.5 0.6 dynamic_slice.52
  11.1 0.7 and_select_fusion.1
  12.0 1.1 fusion.14
  13.1 22.0 %all_gather.7 = bf16[4,96,1152]{2,1,0:T(8,128)(2,1)S(1)} all-gather(bf16[1,96,1152]{2,1,0:T(8,128)(2,1)S(1)} %fusion.14), channel_id=1, replica_groups=mesh['seq'=64,'kvh'=4,'rep'=2] {'kvh'}, dimensions={0}, use_global_device_ids=true | all-gather | bytes 1105920 | tf_op jit(solution)/shard_map/all_gather | solution.py:138
  35.2 2.1 fusion.2
  37.5 2.1 gather_fusion
  39.5 1.0 all_to_all.8
  40.5 16.4 %all-to-all-start = ((bf16[64,6,448]{2,1,0:T(8,128)(2,1)}), bf16[64,6,448]{2,1,0:T(8,128)(2,1)S(1)}, u32[]{:S(2)}, u32[]{:S(2)}) async-start(bf16[64,6,448]{2,1,0:T(8,128)(2,1)} %all_to_all.8), calls=%async_computation | async-start | bytes 1048576 | tf_op jit(solution)/shard_map/all_to_all | solution.py:155
  57.0 4.6 %copy.76 = bf16[448,3072]{0,1:T(8,128)(2,1)} copy(bf16[448,3072]{1,0:T(8,128)(2,1)} %param.9) | data formatting | bytes 5505024 | tf_op args[4]
  61.6 1.3 slice.23
  63.0 0.5 copy.97
  63.7 10.6 %all-to-all-done = bf16[64,6,448]{2,1,0:T(8,128)(2,1)S(1)} async-done(((bf16[64,6,448]{2,1,0:T(8,128)(2,1)}), bf16[64,6,448]{2,1,0:T(8,128)(2,1)S(1)}, u32[]{:S(2)}, u32[]{:S(2)}) %all-to-all-start) | async-done | bytes 344096 | tf_op jit(solution)/shard_map/all_to_all | solution.py:155
  74.3 0.2 all_to_all.10
  74.5 1.2 gather_fusion.1
  75.8 2.0 convolution_bitcast_fusion
  77.9 33.3 %reduce-scatter.2.cloned.1.call-done = f32[1,256,256]{2,1,0:T(8,128)} async-done(((f32[8,256,256]{2,1,0:T(8,128)}), f32[1,256,256]{2,1,0:T(8,128)}) %reduce-scatter.2.cloned.1.call-update) | async-done | bytes 262160 | tf_op jit(solution)/shard_map/reduce_scatter | solution.py:169
  111.2 1.6 convert_element_type.27
  113.1 1.8 slice.20
  115.0 0.7 convolution_bitcast_fusion.1
  115.9 0.2 constant_dynamic-slice_fusion
  116.3 3.5 %collective-permute-start = (f32[256,128]{1,0:T(8,128)S(1)}, f32[256,128]{1,0:T(8,128)S(1)}, u32[]{:S(2)}, u32[]{:S(2)}) collective-permute-start(f32[256,128]{1,0:T(8,128)S(1)} %bitcast.78), channel_id=1, source_target_pairs={{0,1},{1,2},{2,3},{3,4},{4,5},{5,6},{6,7},{7,0},{8,9},{9,10},{10,1... | collective-permute-start | bytes 393224 | tf_op jit(solution)/shard_map/ppermute | solution.py:120
  121.2 3.0 %collective-permute-start.7 = (f32[256,128]{1,0:T(8,128)S(1)}, f32[256,128]{1,0:T(8,128)S(1)}, u32[]{:S(2)}, u32[]{:S(2)}) collective-permute-start(f32[256,128]{1,0:T(8,128)S(1)} %bitcast.79), channel_id=1, source_target_pairs={{0,7},{1,0},{2,1},{3,2},{4,3},{5,4},{6,5},{7,6},{8,15},{9,8},{10,9... | collective-permute-start | bytes 393224 | tf_op jit(solution)/shard_map/ppermute | solution.py:120
  124.3 2.3 collective-permute-start.1
  126.6 0.4 collective-permute-done.7
  127.0 4.2 %collective-permute-start.8 = (f32[256,128]{1,0:T(8,128)S(1)}, f32[256,128]{1,0:T(8,128)S(1)}, u32[]{:S(2)}, u32[]{:S(2)}) collective-permute-start(f32[256,128]{1,0:T(8,128)S(1)} %bitcast_add_fusion.6), channel_id=1, source_target_pairs={{0,7},{1,0},{2,1},{3,2},{4,3},{5,4},{6,5},{7,6},{8,15},{9,8},{10,9... | collective-permute-start | bytes 393224 | tf_op jit(solution)/shard_map/ppermute | solution.py:120
  131.2 1.9 collective-permute-start.2
  133.2 1.0 collective-permute-done.8
  134.2 4.9 %collective-permute-start.9 = (f32[256,128]{1,0:T(8,128)S(1)}, f32[256,128]{1,0:T(8,128)S(1)}, u32[]{:S(2)}, u32[]{:S(2)}) collective-permute-start(f32[256,128]{1,0:T(8,128)S(1)} %bitcast_add_fusion.5), channel_id=1, source_target_pairs={{0,7},{1,0},{2,1},{3,2},{4,3},{5,4},{6,5},{7,6},{8,15},{9,8},{10,9... | collective-permute-start | bytes 393224 | tf_op jit(solution)/shard_map/ppermute | solution.py:120
  139.1 0.4 collective-permute-done.2
  139.4 1.9 collective-permute-start.3
  141.4 0.3 collective-permute-done.9
  141.7 5.3 %collective-permute-start.10 = (f32[256,128]{1,0:T(8,128)S(1)}, f32[256,128]{1,0:T(8,128)S(1)}, u32[]{:S(2)}, u32[]{:S(2)}) collective-permute-start(f32[256,128]{1,0:T(8,128)S(1)} %bitcast_add_fusion.4), channel_id=1, source_target_pairs={{0,7},{1,0},{2,1},{3,2},{4,3},{5,4},{6,5},{7,6},{8,15},{9,8},{10,9... | collective-permute-start | bytes 393224 | tf_op jit(solution)/shard_map/ppermute | solution.py:120
  147.2 1.9 collective-permute-start.4
  149.2 4.8 %collective-permute-start.11 = (f32[256,128]{1,0:T(8,128)S(1)}, f32[256,128]{1,0:T(8,128)S(1)}, u32[]{:S(2)}, u32[]{:S(2)}) collective-permute-start(f32[256,128]{1,0:T(8,128)S(1)} %bitcast_add_fusion.3), channel_id=1, source_target_pairs={{0,7},{1,0},{2,1},{3,2},{4,3},{5,4},{6,5},{7,6},{8,15},{9,8},{10,9... | collective-permute-start | bytes 393224 | tf_op jit(solution)/shard_map/ppermute | solution.py:120
  154.0 0.4 collective-permute-done.4
  154.4 1.9 collective-permute-start.5
  156.4 4.7 %collective-permute-start.12 = (f32[256,128]{1,0:T(8,128)S(1)}, f32[256,128]{1,0:T(8,128)S(1)}, u32[]{:S(2)}, u32[]{:S(2)}) collective-permute-start(f32[256,128]{1,0:T(8,128)S(1)} %bitcast_add_fusion.2), channel_id=1, source_target_pairs={{0,7},{1,0},{2,1},{3,2},{4,3},{5,4},{6,5},{7,6},{8,15},{9,8},{10,9... | collective-permute-start | bytes 393224 | tf_op jit(solution)/shard_map/ppermute | solution.py:120
  161.1 0.5 collective-permute-done.5
  161.6 1.9 collective-permute-start.6
  163.6 4.8 %collective-permute-start.13 = (f32[256,128]{1,0:T(8,128)S(1)}, f32[256,128]{1,0:T(8,128)S(1)}, u32[]{:S(2)}, u32[]{:S(2)}) collective-permute-start(f32[256,128]{1,0:T(8,128)S(1)} %bitcast_add_fusion.1), channel_id=1, source_target_pairs={{0,7},{1,0},{2,1},{3,2},{4,3},{5,4},{6,5},{7,6},{8,15},{9,8},{10,9... | collective-permute-start | bytes 393224 | tf_op jit(solution)/shard_map/ppermute | solution.py:120
  168.6 1.5 collective-permute-done.13
  170.2 38.7 %all-gather.2.cloned.1.call-done = bf16[64,256,256]{2,1,0:T(8,128)(2,1)} async-done(((bf16[1,256,256]{2,1,0:T(8,128)(2,1)}), bf16[64,256,256]{2,1,0:T(8,128)(2,1)}) %all-gather.2.cloned.1.call-update) | async-done | bytes 8388624 | tf_op jit(solution)/shard_map/all_gather | solution.py:175
  208.9 21.6 %shard_map.55 = bf16[512,128]{1,0:T(8,128)(2,1)S(1)} custom-call(s32[1]{0:T(128)} %bitcast.seq_ref, bf16[512,128]{1,0:T(8,128)(2,1)S(1)} %bitcast.69, bf16[16384,256]{1,0:T(8,128)(2,1)} %bitcast.84), custom_call_target="tpu_custom_call" | custom-call | flops 3221225472 | bytes 8650752 | tf_op jit(solution)/shard_map/pallas_call | solution.py:87
  230.7 0.7 reshape.321
  (66 shorter events, 3.5 us)
Async XLA Ops:
  6.5 28.6 %copy-start = (bf16[1152,448]{0,1:T(8,128)(2,1)S(1)}, bf16[1152,448]{0,1:T(8,128)(2,1)}, u32[]{:S(2)}) copy-start(bf16[1152,448]{0,1:T(8,128)(2,1)} %param.8) | copy-start | bytes 3096580
  40.5 33.8 %all-to-all-start = ((bf16[64,6,448]{2,1,0:T(8,128)(2,1)}), bf16[64,6,448]{2,1,0:T(8,128)(2,1)S(1)}, u32[]{:S(2)}, u32[]{:S(2)}) async-start(bf16[64,6,448]{2,1,0:T(8,128)(2,1)} %all_to_all.8), calls=%async_computation | async-start | bytes 1048576 | tf_op jit(solution)/shard_map/all_to_all | solution.py:155
  57.0 54.2 %reduce-scatter.2.cloned.1.call-start = ((), (), s32[]{:S(2)}) async-start(), calls=%async_computation.2 | async-start | bytes 2359296 | tf_op jit(solution)/shard_map/reduce_scatter | solution.py:169
  61.6 1.9 copy-start.1
  77.9 131.0 %all-gather.2.cloned.1.call-start = ((), (), s32[]{:S(2)}) async-start(), calls=%async_computation.3 | async-start | bytes 8519680 | tf_op jit(solution)/shard_map/all_gather | solution.py:175
  116.3 8.0 %collective-permute-start = (f32[256,128]{1,0:T(8,128)S(1)}, f32[256,128]{1,0:T(8,128)S(1)}, u32[]{:S(2)}, u32[]{:S(2)}) collective-permute-start(f32[256,128]{1,0:T(8,128)S(1)} %bitcast.78), channel_id=1, source_target_pairs={{0,1},{1,2},{2,3},{3,4},{4,5},{5,6},{6,7},{7,0},{8,9},{9,10},{10,1... | collective-permute-start | bytes 393224 | tf_op jit(solution)/shard_map/ppermute | solution.py:120
  121.2 5.7 %collective-permute-start.7 = (f32[256,128]{1,0:T(8,128)S(1)}, f32[256,128]{1,0:T(8,128)S(1)}, u32[]{:S(2)}, u32[]{:S(2)}) collective-permute-start(f32[256,128]{1,0:T(8,128)S(1)} %bitcast.79), channel_id=1, source_target_pairs={{0,7},{1,0},{2,1},{3,2},{4,3},{5,4},{6,5},{7,6},{8,15},{9,8},{10,9... | collective-permute-start | bytes 393224 | tf_op jit(solution)/shard_map/ppermute | solution.py:120
  124.3 6.9 %collective-permute-start.1 = (f32[256,128]{1,0:T(8,128)S(1)}, f32[256,128]{1,0:T(8,128)S(1)}, u32[]{:S(2)}, u32[]{:S(2)}) collective-permute-start(f32[256,128]{1,0:T(8,128)S(1)} %bitcast_add_fusion.13), channel_id=1, source_target_pairs={{0,1},{1,2},{2,3},{3,4},{4,5},{5,6},{6,7},{7,0},{8,9},{9,10},{10,1... | collective-permute-start | bytes 393224 | tf_op jit(solution)/shard_map/ppermute | solution.py:120
  127.0 7.2 %collective-permute-start.8 = (f32[256,128]{1,0:T(8,128)S(1)}, f32[256,128]{1,0:T(8,128)S(1)}, u32[]{:S(2)}, u32[]{:S(2)}) collective-permute-start(f32[256,128]{1,0:T(8,128)S(1)} %bitcast_add_fusion.6), channel_id=1, source_target_pairs={{0,7},{1,0},{2,1},{3,2},{4,3},{5,4},{6,5},{7,6},{8,15},{9,8},{10,9... | collective-permute-start | bytes 393224 | tf_op jit(solution)/shard_map/ppermute | solution.py:120
  131.2 8.2 %collective-permute-start.2 = (f32[256,128]{1,0:T(8,128)S(1)}, f32[256,128]{1,0:T(8,128)S(1)}, u32[]{:S(2)}, u32[]{:S(2)}) collective-permute-start(f32[256,128]{1,0:T(8,128)S(1)} %bitcast_add_fusion.12), channel_id=1, source_target_pairs={{0,1},{1,2},{2,3},{3,4},{4,5},{5,6},{6,7},{7,0},{8,9},{9,10},{10,1... | collective-permute-start | bytes 393224 | tf_op jit(solution)/shard_map/ppermute | solution.py:120
  134.2 7.5 %collective-permute-start.9 = (f32[256,128]{1,0:T(8,128)S(1)}, f32[256,128]{1,0:T(8,128)S(1)}, u32[]{:S(2)}, u32[]{:S(2)}) collective-permute-start(f32[256,128]{1,0:T(8,128)S(1)} %bitcast_add_fusion.5), channel_id=1, source_target_pairs={{0,7},{1,0},{2,1},{3,2},{4,3},{5,4},{6,5},{7,6},{8,15},{9,8},{10,9... | collective-permute-start | bytes 393224 | tf_op jit(solution)/shard_map/ppermute | solution.py:120
  139.4 7.8 %collective-permute-start.3 = (f32[256,128]{1,0:T(8,128)S(1)}, f32[256,128]{1,0:T(8,128)S(1)}, u32[]{:S(2)}, u32[]{:S(2)}) collective-permute-start(f32[256,128]{1,0:T(8,128)S(1)} %bitcast_add_fusion.11), channel_id=1, source_target_pairs={{0,1},{1,2},{2,3},{3,4},{4,5},{5,6},{6,7},{7,0},{8,9},{9,10},{10,1... | collective-permute-start | bytes 393224 | tf_op jit(solution)/shard_map/ppermute | solution.py:120
  141.7 7.5 %collective-permute-start.10 = (f32[256,128]{1,0:T(8,128)S(1)}, f32[256,128]{1,0:T(8,128)S(1)}, u32[]{:S(2)}, u32[]{:S(2)}) collective-permute-start(f32[256,128]{1,0:T(8,128)S(1)} %bitcast_add_fusion.4), channel_id=1, source_target_pairs={{0,7},{1,0},{2,1},{3,2},{4,3},{5,4},{6,5},{7,6},{8,15},{9,8},{10,9... | collective-permute-start | bytes 393224 | tf_op jit(solution)/shard_map/ppermute | solution.py:120
  147.2 7.2 %collective-permute-start.4 = (f32[256,128]{1,0:T(8,128)S(1)}, f32[256,128]{1,0:T(8,128)S(1)}, u32[]{:S(2)}, u32[]{:S(2)}) collective-permute-start(f32[256,128]{1,0:T(8,128)S(1)} %bitcast_add_fusion.10), channel_id=1, source_target_pairs={{0,1},{1,2},{2,3},{3,4},{4,5},{5,6},{6,7},{7,0},{8,9},{9,10},{10,1... | collective-permute-start | bytes 393224 | tf_op jit(solution)/shard_map/ppermute | solution.py:120
  149.2 7.1 %collective-permute-start.11 = (f32[256,128]{1,0:T(8,128)S(1)}, f32[256,128]{1,0:T(8,128)S(1)}, u32[]{:S(2)}, u32[]{:S(2)}) collective-permute-start(f32[256,128]{1,0:T(8,128)S(1)} %bitcast_add_fusion.3), channel_id=1, source_target_pairs={{0,7},{1,0},{2,1},{3,2},{4,3},{5,4},{6,5},{7,6},{8,15},{9,8},{10,9... | collective-permute-start | bytes 393224 | tf_op jit(solution)/shard_map/ppermute | solution.py:120
  154.4 7.2 %collective-permute-start.5 = (f32[256,128]{1,0:T(8,128)S(1)}, f32[256,128]{1,0:T(8,128)S(1)}, u32[]{:S(2)}, u32[]{:S(2)}) collective-permute-start(f32[256,128]{1,0:T(8,128)S(1)} %bitcast_add_fusion.9), channel_id=1, source_target_pairs={{0,1},{1,2},{2,3},{3,4},{4,5},{5,6},{6,7},{7,0},{8,9},{9,10},{10,1... | collective-permute-start | bytes 393224 | tf_op jit(solution)/shard_map/ppermute | solution.py:120
  156.4 7.2 %collective-permute-start.12 = (f32[256,128]{1,0:T(8,128)S(1)}, f32[256,128]{1,0:T(8,128)S(1)}, u32[]{:S(2)}, u32[]{:S(2)}) collective-permute-start(f32[256,128]{1,0:T(8,128)S(1)} %bitcast_add_fusion.2), channel_id=1, source_target_pairs={{0,7},{1,0},{2,1},{3,2},{4,3},{5,4},{6,5},{7,6},{8,15},{9,8},{10,9... | collective-permute-start | bytes 393224 | tf_op jit(solution)/shard_map/ppermute | solution.py:120
  161.6 6.9 %collective-permute-start.6 = (f32[256,128]{1,0:T(8,128)S(1)}, f32[256,128]{1,0:T(8,128)S(1)}, u32[]{:S(2)}, u32[]{:S(2)}) collective-permute-start(f32[256,128]{1,0:T(8,128)S(1)} %bitcast_add_fusion.8), channel_id=1, source_target_pairs={{0,1},{1,2},{2,3},{3,4},{4,5},{5,6},{6,7},{7,0},{8,9},{9,10},{10,1... | collective-permute-start | bytes 393224 | tf_op jit(solution)/shard_map/ppermute | solution.py:120
  163.6 6.5 %collective-permute-start.13 = (f32[256,128]{1,0:T(8,128)S(1)}, f32[256,128]{1,0:T(8,128)S(1)}, u32[]{:S(2)}, u32[]{:S(2)}) collective-permute-start(f32[256,128]{1,0:T(8,128)S(1)} %bitcast_add_fusion.1), channel_id=1, source_target_pairs={{0,7},{1,0},{2,1},{3,2},{4,3},{5,4},{6,5},{7,6},{8,15},{9,8},{10,9... | collective-permute-start | bytes 393224 | tf_op jit(solution)/shard_map/ppermute | solution.py:120
Sparse Core Ops, SparseCore 0:
  78.0 33.1 reduce-scatter.1
  114.6 94.2 all-gather.1

commit v10 on v9

--- a/solution.py
+++ b/solution.py
@@ -14,7 +14,7 @@
 
 norm_eps = 1e-06
 masked_score = -1e30
-UNROLL = 8
+UNROLL = 16
 
 
 def layer_norm(states, norm_gain):

time: 239 us -> 238 us (level)
  no operation moved by 1% of the time
where the time goes in v10:
time: 238 us; the launch traced here: 237 us
  waiting for transfers between devices  87.5 us (37%)
  starting transfers between devices  63.5 us (27%)
  blocking collectives  22 us (9%)
  Pallas kernels  20.7 us (9%)
  local copies, waits for them, and re-layouts  17.3 us (7%)
  between operations  14.3 us (6%)
  other arithmetic  7.05 us (3%)
  matrix products  4.9 us (2%)
    ppermute x14, starting transfers between devices, ring_reduce_scatter(): buf = lax.ppermute(buf, axes, perm)  47 us
    all_gather x1, waiting for transfers between devices, local(): pair_all = lax.all_gather(pair_own, 'seq', axis=0, tiled=False)  38.7 us
    reduce_scatter x1, waiting for transfers between devices, local(): lax.psum_scatter(pair_part, ('kvh', 'rep'), scatter_dimension=0, tiled=True)  33.3 us
    all_gather x1, blocking collectives, local(): lax.all_gather(normed[0], 'kvh', axis=0, tiled=False)  22 us
    pallas_call x1, Pallas kernels, causal_attention(): pl.pallas_call(functools.partial(attention_kernel, shards=shards, tok_row...  20.7 us
    all_to_all x1, starting transfers between devices, local(): lax.all_to_all(outgoing, 'seq', split_axis=0, concat_axis=0, tiled=True)  16.4 us
    all_to_all x1, waiting for transfers between devices, local(): lax.all_to_all(outgoing, 'seq', split_axis=0, concat_axis=0, tiled=True)  10.6 us
    ppermute x14, waiting for transfers between devices, ring_reduce_scatter(): buf = lax.ppermute(buf, axes, perm)  4.95 us
  transfers between devices with their start and end apart: 17, of which 12 were waited for; matrix products, arithmetic and copies ran while one was open for 5% of the time, Pallas kernels for 0%

profile of v10, /device:TPU:1, one launch (start us, length us, event | category | flops | bytes accessed | tf_op | source)
XLA Modules:
  0.0 237.4 jit_solution(3522029617632988153)
XLA Ops:
  6.5 1.1 convert_reduce_fusion
  7.7 1.2 fusion.12
  8.9 0.8 copy.74
  9.8 0.7 sub.92
  10.5 0.6 dynamic_slice.52
  11.1 0.7 and_select_fusion.1
  12.0 1.1 fusion.14
  13.1 22.0 %all_gather.7 = bf16[4,96,1152]{2,1,0:T(8,128)(2,1)S(1)} all-gather(bf16[1,96,1152]{2,1,0:T(8,128)(2,1)S(1)} %fusion.14), channel_id=1, replica_groups=mesh['seq'=64,'kvh'=4,'rep'=2] {'kvh'}, dimensions={0}, use_global_device_ids=true | all-gather | bytes 1105920 | tf_op jit(solution)/shard_map/all_gather | solution.py:138
  35.2 2.1 fusion.2
  37.5 2.1 gather_fusion
  39.5 1.0 all_to_all.8
  40.5 16.4 %all-to-all-start = ((bf16[64,6,448]{2,1,0:T(8,128)(2,1)}), bf16[64,6,448]{2,1,0:T(8,128)(2,1)S(1)}, u32[]{:S(2)}, u32[]{:S(2)}) async-start(bf16[64,6,448]{2,1,0:T(8,128)(2,1)} %all_to_all.8), calls=%async_computation | async-start | bytes 1048576 | tf_op jit(solution)/shard_map/all_to_all | solution.py:155
  57.0 4.6 %copy.76 = bf16[448,3072]{0,1:T(8,128)(2,1)} copy(bf16[448,3072]{1,0:T(8,128)(2,1)} %param.9) | data formatting | bytes 5505024 | tf_op args[4]
  61.6 1.3 slice.23
  63.0 0.5 copy.97
  63.7 10.6 %all-to-all-done = bf16[64,6,448]{2,1,0:T(8,128)(2,1)S(1)} async-done(((bf16[64,6,448]{2,1,0:T(8,128)(2,1)}), bf16[64,6,448]{2,1,0:T(8,128)(2,1)S(1)}, u32[]{:S(2)}, u32[]{:S(2)}) %all-to-all-start) | async-done | bytes 344096 | tf_op jit(solution)/shard_map/all_to_all | solution.py:155
  74.3 0.2 all_to_all.10
  74.5 1.2 gather_fusion.1
  75.8 2.0 convolution_bitcast_fusion
  77.9 33.3 %reduce-scatter.2.cloned.1.call-done = f32[1,256,256]{2,1,0:T(8,128)} async-done(((f32[8,256,256]{2,1,0:T(8,128)}), f32[1,256,256]{2,1,0:T(8,128)}) %reduce-scatter.2.cloned.1.call-update) | async-done | bytes 262160 | tf_op jit(solution)/shard_map/reduce_scatter | solution.py:169
  111.2 1.6 convert_element_type.27
  113.1 1.8 slice.20
  115.0 0.7 convolution_bitcast_fusion.1
  115.9 0.2 constant_dynamic-slice_fusion
  116.3 3.5 %collective-permute-start = (f32[256,128]{1,0:T(8,128)S(1)}, f32[256,128]{1,0:T(8,128)S(1)}, u32[]{:S(2)}, u32[]{:S(2)}) collective-permute-start(f32[256,128]{1,0:T(8,128)S(1)} %bitcast.78), channel_id=1, source_target_pairs={{0,1},{1,2},{2,3},{3,4},{4,5},{5,6},{6,7},{7,0},{8,9},{9,10},{10,1... | collective-permute-start | bytes 393224 | tf_op jit(solution)/shard_map/ppermute | solution.py:120
  121.2 3.0 %collective-permute-start.7 = (f32[256,128]{1,0:T(8,128)S(1)}, f32[256,128]{1,0:T(8,128)S(1)}, u32[]{:S(2)}, u32[]{:S(2)}) collective-permute-start(f32[256,128]{1,0:T(8,128)S(1)} %bitcast.79), channel_id=1, source_target_pairs={{0,7},{1,0},{2,1},{3,2},{4,3},{5,4},{6,5},{7,6},{8,15},{9,8},{10,9... | collective-permute-start | bytes 393224 | tf_op jit(solution)/shard_map/ppermute | solution.py:120
  124.3 2.3 collective-permute-start.1
  126.6 0.4 collective-permute-done.7
  127.0 4.2 %collective-permute-start.8 = (f32[256,128]{1,0:T(8,128)S(1)}, f32[256,128]{1,0:T(8,128)S(1)}, u32[]{:S(2)}, u32[]{:S(2)}) collective-permute-start(f32[256,128]{1,0:T(8,128)S(1)} %bitcast_add_fusion.6), channel_id=1, source_target_pairs={{0,7},{1,0},{2,1},{3,2},{4,3},{5,4},{6,5},{7,6},{8,15},{9,8},{10,9... | collective-permute-start | bytes 393224 | tf_op jit(solution)/shard_map/ppermute | solution.py:120
  131.2 1.9 collective-permute-start.2
  133.2 1.0 collective-permute-done.8
  134.2 4.9 %collective-permute-start.9 = (f32[256,128]{1,0:T(8,128)S(1)}, f32[256,128]{1,0:T(8,128)S(1)}, u32[]{:S(2)}, u32[]{:S(2)}) collective-permute-start(f32[256,128]{1,0:T(8,128)S(1)} %bitcast_add_fusion.5), channel_id=1, source_target_pairs={{0,7},{1,0},{2,1},{3,2},{4,3},{5,4},{6,5},{7,6},{8,15},{9,8},{10,9... | collective-permute-start | bytes 393224 | tf_op jit(solution)/shard_map/ppermute | solution.py:120
  139.1 0.4 collective-permute-done.2
  139.4 1.9 collective-permute-start.3
  141.4 0.3 collective-permute-done.9
  141.7 5.3 %collective-permute-start.10 = (f32[256,128]{1,0:T(8,128)S(1)}, f32[256,128]{1,0:T(8,128)S(1)}, u32[]{:S(2)}, u32[]{:S(2)}) collective-permute-start(f32[256,128]{1,0:T(8,128)S(1)} %bitcast_add_fusion.4), channel_id=1, source_target_pairs={{0,7},{1,0},{2,1},{3,2},{4,3},{5,4},{6,5},{7,6},{8,15},{9,8},{10,9... | collective-permute-start | bytes 393224 | tf_op jit(solution)/shard_map/ppermute | solution.py:120
  147.2 1.9 collective-permute-start.4
  149.2 4.8 %collective-permute-start.11 = (f32[256,128]{1,0:T(8,128)S(1)}, f32[256,128]{1,0:T(8,128)S(1)}, u32[]{:S(2)}, u32[]{:S(2)}) collective-permute-start(f32[256,128]{1,0:T(8,128)S(1)} %bitcast_add_fusion.3), channel_id=1, source_target_pairs={{0,7},{1,0},{2,1},{3,2},{4,3},{5,4},{6,5},{7,6},{8,15},{9,8},{10,9... | collective-permute-start | bytes 393224 | tf_op jit(solution)/shard_map/ppermute | solution.py:120
  154.0 0.4 collective-permute-done.4
  154.4 1.9 collective-permute-start.5
  156.4 4.7 %collective-permute-start.12 = (f32[256,128]{1,0:T(8,128)S(1)}, f32[256,128]{1,0:T(8,128)S(1)}, u32[]{:S(2)}, u32[]{:S(2)}) collective-permute-start(f32[256,128]{1,0:T(8,128)S(1)} %bitcast_add_fusion.2), channel_id=1, source_target_pairs={{0,7},{1,0},{2,1},{3,2},{4,3},{5,4},{6,5},{7,6},{8,15},{9,8},{10,9... | collective-permute-start | bytes 393224 | tf_op jit(solution)/shard_map/ppermute | solution.py:120
  161.1 0.5 collective-permute-done.5
  161.6 1.9 collective-permute-start.6
  163.6 4.8 %collective-permute-start.13 = (f32[256,128]{1,0:T(8,128)S(1)}, f32[256,128]{1,0:T(8,128)S(1)}, u32[]{:S(2)}, u32[]{:S(2)}) collective-permute-start(f32[256,128]{1,0:T(8,128)S(1)} %bitcast_add_fusion.1), channel_id=1, source_target_pairs={{0,7},{1,0},{2,1},{3,2},{4,3},{5,4},{6,5},{7,6},{8,15},{9,8},{10,9... | collective-permute-start | bytes 393224 | tf_op jit(solution)/shard_map/ppermute | solution.py:120
  168.6 1.5 collective-permute-done.13
  170.2 38.7 %all-gather.2.cloned.1.call-done = bf16[64,256,256]{2,1,0:T(8,128)(2,1)} async-done(((bf16[1,256,256]{2,1,0:T(8,128)(2,1)}), bf16[64,256,256]{2,1,0:T(8,128)(2,1)}) %all-gather.2.cloned.1.call-update) | async-done | bytes 8388624 | tf_op jit(solution)/shard_map/all_gather | solution.py:175
  208.9 20.7 %shard_map.55 = bf16[512,128]{1,0:T(8,128)(2,1)S(1)} custom-call(s32[1]{0:T(128)} %bitcast.seq_ref, bf16[512,128]{1,0:T(8,128)(2,1)S(1)} %bitcast.69, bf16[16384,256]{1,0:T(8,128)(2,1)} %bitcast.84), custom_call_target="tpu_custom_call" | custom-call | flops 3221225472 | bytes 8650752 | tf_op jit(solution)/shard_map/pallas_call | solution.py:87
  229.8 0.7 reshape.321
  (66 shorter events, 3.5 us)
Async XLA Ops:
  6.5 28.6 %copy-start = (bf16[1152,448]{0,1:T(8,128)(2,1)S(1)}, bf16[1152,448]{0,1:T(8,128)(2,1)}, u32[]{:S(2)}) copy-start(bf16[1152,448]{0,1:T(8,128)(2,1)} %param.8) | copy-start | bytes 3096580
  40.5 33.8 %all-to-all-start = ((bf16[64,6,448]{2,1,0:T(8,128)(2,1)}), bf16[64,6,448]{2,1,0:T(8,128)(2,1)S(1)}, u32[]{:S(2)}, u32[]{:S(2)}) async-start(bf16[64,6,448]{2,1,0:T(8,128)(2,1)} %all_to_all.8), calls=%async_computation | async-start | bytes 1048576 | tf_op jit(solution)/shard_map/all_to_all | solution.py:155
  57.0 54.2 %reduce-scatter.2.cloned.1.call-start = ((), (), s32[]{:S(2)}) async-start(), calls=%async_computation.2 | async-start | bytes 2359296 | tf_op jit(solution)/shard_map/reduce_scatter | solution.py:169
  61.6 1.9 copy-start.1
  77.9 131.0 %all-gather.2.cloned.1.call-start = ((), (), s32[]{:S(2)}) async-start(), calls=%async_computation.3 | async-start | bytes 8519680 | tf_op jit(solution)/shard_map/all_gather | solution.py:175
  116.3 8.0 %collective-permute-start = (f32[256,128]{1,0:T(8,128)S(1)}, f32[256,128]{1,0:T(8,128)S(1)}, u32[]{:S(2)}, u32[]{:S(2)}) collective-permute-start(f32[256,128]{1,0:T(8,128)S(1)} %bitcast.78), channel_id=1, source_target_pairs={{0,1},{1,2},{2,3},{3,4},{4,5},{5,6},{6,7},{7,0},{8,9},{9,10},{10,1... | collective-permute-start | bytes 393224 | tf_op jit(solution)/shard_map/ppermute | solution.py:120
  121.2 5.7 %collective-permute-start.7 = (f32[256,128]{1,0:T(8,128)S(1)}, f32[256,128]{1,0:T(8,128)S(1)}, u32[]{:S(2)}, u32[]{:S(2)}) collective-permute-start(f32[256,128]{1,0:T(8,128)S(1)} %bitcast.79), channel_id=1, source_target_pairs={{0,7},{1,0},{2,1},{3,2},{4,3},{5,4},{6,5},{7,6},{8,15},{9,8},{10,9... | collective-permute-start | bytes 393224 | tf_op jit(solution)/shard_map/ppermute | solution.py:120
  124.3 6.9 %collective-permute-start.1 = (f32[256,128]{1,0:T(8,128)S(1)}, f32[256,128]{1,0:T(8,128)S(1)}, u32[]{:S(2)}, u32[]{:S(2)}) collective-permute-start(f32[256,128]{1,0:T(8,128)S(1)} %bitcast_add_fusion.13), channel_id=1, source_target_pairs={{0,1},{1,2},{2,3},{3,4},{4,5},{5,6},{6,7},{7,0},{8,9},{9,10},{10,1... | collective-permute-start | bytes 393224 | tf_op jit(solution)/shard_map/ppermute | solution.py:120
  127.0 7.2 %collective-permute-start.8 = (f32[256,128]{1,0:T(8,128)S(1)}, f32[256,128]{1,0:T(8,128)S(1)}, u32[]{:S(2)}, u32[]{:S(2)}) collective-permute-start(f32[256,128]{1,0:T(8,128)S(1)} %bitcast_add_fusion.6), channel_id=1, source_target_pairs={{0,7},{1,0},{2,1},{3,2},{4,3},{5,4},{6,5},{7,6},{8,15},{9,8},{10,9... | collective-permute-start | bytes 393224 | tf_op jit(solution)/shard_map/ppermute | solution.py:120
  131.2 8.2 %collective-permute-start.2 = (f32[256,128]{1,0:T(8,128)S(1)}, f32[256,128]{1,0:T(8,128)S(1)}, u32[]{:S(2)}, u32[]{:S(2)}) collective-permute-start(f32[256,128]{1,0:T(8,128)S(1)} %bitcast_add_fusion.12), channel_id=1, source_target_pairs={{0,1},{1,2},{2,3},{3,4},{4,5},{5,6},{6,7},{7,0},{8,9},{9,10},{10,1... | collective-permute-start | bytes 393224 | tf_op jit(solution)/shard_map/ppermute | solution.py:120
  134.2 7.5 %collective-permute-start.9 = (f32[256,128]{1,0:T(8,128)S(1)}, f32[256,128]{1,0:T(8,128)S(1)}, u32[]{:S(2)}, u32[]{:S(2)}) collective-permute-start(f32[256,128]{1,0:T(8,128)S(1)} %bitcast_add_fusion.5), channel_id=1, source_target_pairs={{0,7},{1,0},{2,1},{3,2},{4,3},{5,4},{6,5},{7,6},{8,15},{9,8},{10,9... | collective-permute-start | bytes 393224 | tf_op jit(solution)/shard_map/ppermute | solution.py:120
  139.4 7.8 %collective-permute-start.3 = (f32[256,128]{1,0:T(8,128)S(1)}, f32[256,128]{1,0:T(8,128)S(1)}, u32[]{:S(2)}, u32[]{:S(2)}) collective-permute-start(f32[256,128]{1,0:T(8,128)S(1)} %bitcast_add_fusion.11), channel_id=1, source_target_pairs={{0,1},{1,2},{2,3},{3,4},{4,5},{5,6},{6,7},{7,0},{8,9},{9,10},{10,1... | collective-permute-start | bytes 393224 | tf_op jit(solution)/shard_map/ppermute | solution.py:120
  141.7 7.5 %collective-permute-start.10 = (f32[256,128]{1,0:T(8,128)S(1)}, f32[256,128]{1,0:T(8,128)S(1)}, u32[]{:S(2)}, u32[]{:S(2)}) collective-permute-start(f32[256,128]{1,0:T(8,128)S(1)} %bitcast_add_fusion.4), channel_id=1, source_target_pairs={{0,7},{1,0},{2,1},{3,2},{4,3},{5,4},{6,5},{7,6},{8,15},{9,8},{10,9... | collective-permute-start | bytes 393224 | tf_op jit(solution)/shard_map/ppermute | solution.py:120
  147.2 7.2 %collective-permute-start.4 = (f32[256,128]{1,0:T(8,128)S(1)}, f32[256,128]{1,0:T(8,128)S(1)}, u32[]{:S(2)}, u32[]{:S(2)}) collective-permute-start(f32[256,128]{1,0:T(8,128)S(1)} %bitcast_add_fusion.10), channel_id=1, source_target_pairs={{0,1},{1,2},{2,3},{3,4},{4,5},{5,6},{6,7},{7,0},{8,9},{9,10},{10,1... | collective-permute-start | bytes 393224 | tf_op jit(solution)/shard_map/ppermute | solution.py:120
  149.2 7.1 %collective-permute-start.11 = (f32[256,128]{1,0:T(8,128)S(1)}, f32[256,128]{1,0:T(8,128)S(1)}, u32[]{:S(2)}, u32[]{:S(2)}) collective-permute-start(f32[256,128]{1,0:T(8,128)S(1)} %bitcast_add_fusion.3), channel_id=1, source_target_pairs={{0,7},{1,0},{2,1},{3,2},{4,3},{5,4},{6,5},{7,6},{8,15},{9,8},{10,9... | collective-permute-start | bytes 393224 | tf_op jit(solution)/shard_map/ppermute | solution.py:120
  154.4 7.2 %collective-permute-start.5 = (f32[256,128]{1,0:T(8,128)S(1)}, f32[256,128]{1,0:T(8,128)S(1)}, u32[]{:S(2)}, u32[]{:S(2)}) collective-permute-start(f32[256,128]{1,0:T(8,128)S(1)} %bitcast_add_fusion.9), channel_id=1, source_target_pairs={{0,1},{1,2},{2,3},{3,4},{4,5},{5,6},{6,7},{7,0},{8,9},{9,10},{10,1... | collective-permute-start | bytes 393224 | tf_op jit(solution)/shard_map/ppermute | solution.py:120
  156.4 7.2 %collective-permute-start.12 = (f32[256,128]{1,0:T(8,128)S(1)}, f32[256,128]{1,0:T(8,128)S(1)}, u32[]{:S(2)}, u32[]{:S(2)}) collective-permute-start(f32[256,128]{1,0:T(8,128)S(1)} %bitcast_add_fusion.2), channel_id=1, source_target_pairs={{0,7},{1,0},{2,1},{3,2},{4,3},{5,4},{6,5},{7,6},{8,15},{9,8},{10,9... | collective-permute-start | bytes 393224 | tf_op jit(solution)/shard_map/ppermute | solution.py:120
  161.6 6.9 %collective-permute-start.6 = (f32[256,128]{1,0:T(8,128)S(1)}, f32[256,128]{1,0:T(8,128)S(1)}, u32[]{:S(2)}, u32[]{:S(2)}) collective-permute-start(f32[256,128]{1,0:T(8,128)S(1)} %bitcast_add_fusion.8), channel_id=1, source_target_pairs={{0,1},{1,2},{2,3},{3,4},{4,5},{5,6},{6,7},{7,0},{8,9},{9,10},{10,1... | collective-permute-start | bytes 393224 | tf_op jit(solution)/shard_map/ppermute | solution.py:120
  163.6 6.5 %collective-permute-start.13 = (f32[256,128]{1,0:T(8,128)S(1)}, f32[256,128]{1,0:T(8,128)S(1)}, u32[]{:S(2)}, u32[]{:S(2)}) collective-permute-start(f32[256,128]{1,0:T(8,128)S(1)} %bitcast_add_fusion.1), channel_id=1, source_target_pairs={{0,7},{1,0},{2,1},{3,2},{4,3},{5,4},{6,5},{7,6},{8,15},{9,8},{10,9... | collective-permute-start | bytes 393224 | tf_op jit(solution)/shard_map/ppermute | solution.py:120
Sparse Core Ops, SparseCore 0:
  78.0 33.1 reduce-scatter.1
  114.6 94.2 all-gather.1

commit v11 on v10

--- a/solution.py
+++ b/solution.py
@@ -48,8 +48,10 @@
             scores = lax.dot_general(
                 q, key, (((1,), (1,)), ((), ())), preferred_element_type=jnp.float32
             ) * scale
-            allowed = lane_pos <= query_pos - src
-            scores = jnp.where(allowed, scores, masked_score)
+            free = (qb * block // 128) * 128
+            allowed = lane_pos[:, free:] <= query_pos - src
+            edge = jnp.where(allowed, scores[:, free:], masked_score)
+            scores = jnp.concatenate([scores[:, :free], edge], axis=1) if free else edge
             new_top = jnp.maximum(top, jnp.max(scores, axis=1, keepdims=True))
             shrink = jnp.exp(top - new_top)
             weights = jnp.exp(scores - new_top)

time: 238 us -> 238 us (level)
  no operation moved by 1% of the time
where the time goes in v11:
time: 238 us; the launch traced here: 237 us
  waiting for transfers between devices  87.5 us (37%)
  starting transfers between devices  63.5 us (27%)
  blocking collectives  22 us (9%)
  Pallas kernels  20.2 us (8%)
  local copies, waits for them, and re-layouts  17.3 us (7%)
  between operations  14.3 us (6%)
  other arithmetic  7.05 us (3%)
  matrix products  4.9 us (2%)
    ppermute x14, starting transfers between devices, ring_reduce_scatter(): buf = lax.ppermute(buf, axes, perm)  47 us
    all_gather x1, waiting for transfers between devices, local(): pair_all = lax.all_gather(pair_own, 'seq', axis=0, tiled=False)  38.7 us
    reduce_scatter x1, waiting for transfers between devices, local(): lax.psum_scatter(pair_part, ('kvh', 'rep'), scatter_dimension=0, tiled=True)  33.3 us
    all_gather x1, blocking collectives, local(): lax.all_gather(normed[0], 'kvh', axis=0, tiled=False)  22 us
    pallas_call x1, Pallas kernels, causal_attention(): pl.pallas_call(functools.partial(attention_kernel, shards=shards, tok_row...  20.2 us
    all_to_all x1, starting transfers between devices, local(): lax.all_to_all(outgoing, 'seq', split_axis=0, concat_axis=0, tiled=True)  16.4 us
    all_to_all x1, waiting for transfers between devices, local(): lax.all_to_all(outgoing, 'seq', split_axis=0, concat_axis=0, tiled=True)  10.6 us
    ppermute x14, waiting for transfers between devices, ring_reduce_scatter(): buf = lax.ppermute(buf, axes, perm)  4.95 us
  transfers between devices with their start and end apart: 17, of which 12 were waited for; matrix products, arithmetic and copies ran while one was open for 5% of the time, Pallas kernels for 0%

profile of v11, /device:TPU:1, one launch (start us, length us, event | category | flops | bytes accessed | tf_op | source)
XLA Modules:
  0.0 236.8 jit_solution(8797858985466933036)
XLA Ops:
  6.5 1.1 convert_reduce_fusion
  7.7 1.2 fusion.12
  8.9 0.8 copy.74
  9.8 0.7 sub.92
  10.5 0.6 dynamic_slice.52
  11.1 0.7 and_select_fusion.1
  12.0 1.1 fusion.14
  13.1 22.0 %all_gather.7 = bf16[4,96,1152]{2,1,0:T(8,128)(2,1)S(1)} all-gather(bf16[1,96,1152]{2,1,0:T(8,128)(2,1)S(1)} %fusion.14), channel_id=1, replica_groups=mesh['seq'=64,'kvh'=4,'rep'=2] {'kvh'}, dimensions={0}, use_global_device_ids=true | all-gather | bytes 1105920 | tf_op jit(solution)/shard_map/all_gather | solution.py:140
  35.2 2.1 fusion.2
  37.5 2.1 gather_fusion
  39.5 1.0 all_to_all.8
  40.5 16.4 %all-to-all-start = ((bf16[64,6,448]{2,1,0:T(8,128)(2,1)}), bf16[64,6,448]{2,1,0:T(8,128)(2,1)S(1)}, u32[]{:S(2)}, u32[]{:S(2)}) async-start(bf16[64,6,448]{2,1,0:T(8,128)(2,1)} %all_to_all.8), calls=%async_computation | async-start | bytes 1048576 | tf_op jit(solution)/shard_map/all_to_all | solution.py:157
  57.0 4.6 %copy.76 = bf16[448,3072]{0,1:T(8,128)(2,1)} copy(bf16[448,3072]{1,0:T(8,128)(2,1)} %param.9) | data formatting | bytes 5505024 | tf_op args[4]
  61.6 1.3 slice.23
  63.0 0.5 copy.97
  63.7 10.6 %all-to-all-done = bf16[64,6,448]{2,1,0:T(8,128)(2,1)S(1)} async-done(((bf16[64,6,448]{2,1,0:T(8,128)(2,1)}), bf16[64,6,448]{2,1,0:T(8,128)(2,1)S(1)}, u32[]{:S(2)}, u32[]{:S(2)}) %all-to-all-start) | async-done | bytes 344096 | tf_op jit(solution)/shard_map/all_to_all | solution.py:157
  74.3 0.2 all_to_all.10
  74.5 1.2 gather_fusion.1
  75.8 2.0 convolution_bitcast_fusion
  77.9 33.3 %reduce-scatter.2.cloned.1.call-done = f32[1,256,256]{2,1,0:T(8,128)} async-done(((f32[8,256,256]{2,1,0:T(8,128)}), f32[1,256,256]{2,1,0:T(8,128)}) %reduce-scatter.2.cloned.1.call-update) | async-done | bytes 262160 | tf_op jit(solution)/shard_map/reduce_scatter | solution.py:171
  111.2 1.6 convert_element_type.27
  113.1 1.8 slice.20
  115.0 0.7 convolution_bitcast_fusion.1
  115.9 0.2 constant_dynamic-slice_fusion
  116.3 3.5 %collective-permute-start = (f32[256,128]{1,0:T(8,128)S(1)}, f32[256,128]{1,0:T(8,128)S(1)}, u32[]{:S(2)}, u32[]{:S(2)}) collective-permute-start(f32[256,128]{1,0:T(8,128)S(1)} %bitcast.78), channel_id=1, source_target_pairs={{0,1},{1,2},{2,3},{3,4},{4,5},{5,6},{6,7},{7,0},{8,9},{9,10},{10,1... | collective-permute-start | bytes 393224 | tf_op jit(solution)/shard_map/ppermute | solution.py:122
  121.2 3.0 %collective-permute-start.7 = (f32[256,128]{1,0:T(8,128)S(1)}, f32[256,128]{1,0:T(8,128)S(1)}, u32[]{:S(2)}, u32[]{:S(2)}) collective-permute-start(f32[256,128]{1,0:T(8,128)S(1)} %bitcast.79), channel_id=1, source_target_pairs={{0,7},{1,0},{2,1},{3,2},{4,3},{5,4},{6,5},{7,6},{8,15},{9,8},{10,9... | collective-permute-start | bytes 393224 | tf_op jit(solution)/shard_map/ppermute | solution.py:122
  124.3 2.3 collective-permute-start.1
  126.6 0.4 collective-permute-done.7
  127.0 4.2 %collective-permute-start.8 = (f32[256,128]{1,0:T(8,128)S(1)}, f32[256,128]{1,0:T(8,128)S(1)}, u32[]{:S(2)}, u32[]{:S(2)}) collective-permute-start(f32[256,128]{1,0:T(8,128)S(1)} %bitcast_add_fusion.6), channel_id=1, source_target_pairs={{0,7},{1,0},{2,1},{3,2},{4,3},{5,4},{6,5},{7,6},{8,15},{9,8},{10,9... | collective-permute-start | bytes 393224 | tf_op jit(solution)/shard_map/ppermute | solution.py:122
  131.2 1.9 collective-permute-start.2
  133.2 1.0 collective-permute-done.8
  134.2 4.9 %collective-permute-start.9 = (f32[256,128]{1,0:T(8,128)S(1)}, f32[256,128]{1,0:T(8,128)S(1)}, u32[]{:S(2)}, u32[]{:S(2)}) collective-permute-start(f32[256,128]{1,0:T(8,128)S(1)} %bitcast_add_fusion.5), channel_id=1, source_target_pairs={{0,7},{1,0},{2,1},{3,2},{4,3},{5,4},{6,5},{7,6},{8,15},{9,8},{10,9... | collective-permute-start | bytes 393224 | tf_op jit(solution)/shard_map/ppermute | solution.py:122
  139.1 0.4 collective-permute-done.2
  139.4 1.9 collective-permute-start.3
  141.4 0.3 collective-permute-done.9
  141.7 5.3 %collective-permute-start.10 = (f32[256,128]{1,0:T(8,128)S(1)}, f32[256,128]{1,0:T(8,128)S(1)}, u32[]{:S(2)}, u32[]{:S(2)}) collective-permute-start(f32[256,128]{1,0:T(8,128)S(1)} %bitcast_add_fusion.4), channel_id=1, source_target_pairs={{0,7},{1,0},{2,1},{3,2},{4,3},{5,4},{6,5},{7,6},{8,15},{9,8},{10,9... | collective-permute-start | bytes 393224 | tf_op jit(solution)/shard_map/ppermute | solution.py:122
  147.2 1.9 collective-permute-start.4
  149.2 4.8 %collective-permute-start.11 = (f32[256,128]{1,0:T(8,128)S(1)}, f32[256,128]{1,0:T(8,128)S(1)}, u32[]{:S(2)}, u32[]{:S(2)}) collective-permute-start(f32[256,128]{1,0:T(8,128)S(1)} %bitcast_add_fusion.3), channel_id=1, source_target_pairs={{0,7},{1,0},{2,1},{3,2},{4,3},{5,4},{6,5},{7,6},{8,15},{9,8},{10,9... | collective-permute-start | bytes 393224 | tf_op jit(solution)/shard_map/ppermute | solution.py:122
  154.0 0.4 collective-permute-done.4
  154.4 1.9 collective-permute-start.5
  156.4 4.7 %collective-permute-start.12 = (f32[256,128]{1,0:T(8,128)S(1)}, f32[256,128]{1,0:T(8,128)S(1)}, u32[]{:S(2)}, u32[]{:S(2)}) collective-permute-start(f32[256,128]{1,0:T(8,128)S(1)} %bitcast_add_fusion.2), channel_id=1, source_target_pairs={{0,7},{1,0},{2,1},{3,2},{4,3},{5,4},{6,5},{7,6},{8,15},{9,8},{10,9... | collective-permute-start | bytes 393224 | tf_op jit(solution)/shard_map/ppermute | solution.py:122
  161.1 0.5 collective-permute-done.5
  161.6 1.9 collective-permute-start.6
  163.6 4.8 %collective-permute-start.13 = (f32[256,128]{1,0:T(8,128)S(1)}, f32[256,128]{1,0:T(8,128)S(1)}, u32[]{:S(2)}, u32[]{:S(2)}) collective-permute-start(f32[256,128]{1,0:T(8,128)S(1)} %bitcast_add_fusion.1), channel_id=1, source_target_pairs={{0,7},{1,0},{2,1},{3,2},{4,3},{5,4},{6,5},{7,6},{8,15},{9,8},{10,9... | collective-permute-start | bytes 393224 | tf_op jit(solution)/shard_map/ppermute | solution.py:122
  168.6 1.5 collective-permute-done.13
  170.2 38.7 %all-gather.2.cloned.1.call-done = bf16[64,256,256]{2,1,0:T(8,128)(2,1)} async-done(((bf16[1,256,256]{2,1,0:T(8,128)(2,1)}), bf16[64,256,256]{2,1,0:T(8,128)(2,1)}) %all-gather.2.cloned.1.call-update) | async-done | bytes 8388624 | tf_op jit(solution)/shard_map/all_gather | solution.py:177
  208.9 20.2 %shard_map.55 = bf16[512,128]{1,0:T(8,128)(2,1)S(1)} custom-call(s32[1]{0:T(128)} %bitcast.seq_ref, bf16[512,128]{1,0:T(8,128)(2,1)S(1)} %bitcast.69, bf16[16384,256]{1,0:T(8,128)(2,1)} %bitcast.84), custom_call_target="tpu_custom_call" | custom-call | flops 3221225472 | bytes 8650752 | tf_op jit(solution)/shard_map/pallas_call | solution.py:89
  229.3 0.7 reshape.321
  (66 shorter events, 3.5 us)
Async XLA Ops:
  6.5 28.6 %copy-start = (bf16[1152,448]{0,1:T(8,128)(2,1)S(1)}, bf16[1152,448]{0,1:T(8,128)(2,1)}, u32[]{:S(2)}) copy-start(bf16[1152,448]{0,1:T(8,128)(2,1)} %param.8) | copy-start | bytes 3096580
  40.5 33.8 %all-to-all-start = ((bf16[64,6,448]{2,1,0:T(8,128)(2,1)}), bf16[64,6,448]{2,1,0:T(8,128)(2,1)S(1)}, u32[]{:S(2)}, u32[]{:S(2)}) async-start(bf16[64,6,448]{2,1,0:T(8,128)(2,1)} %all_to_all.8), calls=%async_computation | async-start | bytes 1048576 | tf_op jit(solution)/shard_map/all_to_all | solution.py:157
  57.0 54.2 %reduce-scatter.2.cloned.1.call-start = ((), (), s32[]{:S(2)}) async-start(), calls=%async_computation.2 | async-start | bytes 2359296 | tf_op jit(solution)/shard_map/reduce_scatter | solution.py:171
  61.6 1.9 copy-start.1
  77.9 131.0 %all-gather.2.cloned.1.call-start = ((), (), s32[]{:S(2)}) async-start(), calls=%async_computation.3 | async-start | bytes 8519680 | tf_op jit(solution)/shard_map/all_gather | solution.py:177
  116.3 8.0 %collective-permute-start = (f32[256,128]{1,0:T(8,128)S(1)}, f32[256,128]{1,0:T(8,128)S(1)}, u32[]{:S(2)}, u32[]{:S(2)}) collective-permute-start(f32[256,128]{1,0:T(8,128)S(1)} %bitcast.78), channel_id=1, source_target_pairs={{0,1},{1,2},{2,3},{3,4},{4,5},{5,6},{6,7},{7,0},{8,9},{9,10},{10,1... | collective-permute-start | bytes 393224 | tf_op jit(solution)/shard_map/ppermute | solution.py:122
  121.2 5.7 %collective-permute-start.7 = (f32[256,128]{1,0:T(8,128)S(1)}, f32[256,128]{1,0:T(8,128)S(1)}, u32[]{:S(2)}, u32[]{:S(2)}) collective-permute-start(f32[256,128]{1,0:T(8,128)S(1)} %bitcast.79), channel_id=1, source_target_pairs={{0,7},{1,0},{2,1},{3,2},{4,3},{5,4},{6,5},{7,6},{8,15},{9,8},{10,9... | collective-permute-start | bytes 393224 | tf_op jit(solution)/shard_map/ppermute | solution.py:122
  124.3 6.9 %collective-permute-start.1 = (f32[256,128]{1,0:T(8,128)S(1)}, f32[256,128]{1,0:T(8,128)S(1)}, u32[]{:S(2)}, u32[]{:S(2)}) collective-permute-start(f32[256,128]{1,0:T(8,128)S(1)} %bitcast_add_fusion.13), channel_id=1, source_target_pairs={{0,1},{1,2},{2,3},{3,4},{4,5},{5,6},{6,7},{7,0},{8,9},{9,10},{10,1... | collective-permute-start | bytes 393224 | tf_op jit(solution)/shard_map/ppermute | solution.py:122
  127.0 7.2 %collective-permute-start.8 = (f32[256,128]{1,0:T(8,128)S(1)}, f32[256,128]{1,0:T(8,128)S(1)}, u32[]{:S(2)}, u32[]{:S(2)}) collective-permute-start(f32[256,128]{1,0:T(8,128)S(1)} %bitcast_add_fusion.6), channel_id=1, source_target_pairs={{0,7},{1,0},{2,1},{3,2},{4,3},{5,4},{6,5},{7,6},{8,15},{9,8},{10,9... | collective-permute-start | bytes 393224 | tf_op jit(solution)/shard_map/ppermute | solution.py:122
  131.2 8.2 %collective-permute-start.2 = (f32[256,128]{1,0:T(8,128)S(1)}, f32[256,128]{1,0:T(8,128)S(1)}, u32[]{:S(2)}, u32[]{:S(2)}) collective-permute-start(f32[256,128]{1,0:T(8,128)S(1)} %bitcast_add_fusion.12), channel_id=1, source_target_pairs={{0,1},{1,2},{2,3},{3,4},{4,5},{5,6},{6,7},{7,0},{8,9},{9,10},{10,1... | collective-permute-start | bytes 393224 | tf_op jit(solution)/shard_map/ppermute | solution.py:122
  134.2 7.5 %collective-permute-start.9 = (f32[256,128]{1,0:T(8,128)S(1)}, f32[256,128]{1,0:T(8,128)S(1)}, u32[]{:S(2)}, u32[]{:S(2)}) collective-permute-start(f32[256,128]{1,0:T(8,128)S(1)} %bitcast_add_fusion.5), channel_id=1, source_target_pairs={{0,7},{1,0},{2,1},{3,2},{4,3},{5,4},{6,5},{7,6},{8,15},{9,8},{10,9... | collective-permute-start | bytes 393224 | tf_op jit(solution)/shard_map/ppermute | solution.py:122
  139.4 7.8 %collective-permute-start.3 = (f32[256,128]{1,0:T(8,128)S(1)}, f32[256,128]{1,0:T(8,128)S(1)}, u32[]{:S(2)}, u32[]{:S(2)}) collective-permute-start(f32[256,128]{1,0:T(8,128)S(1)} %bitcast_add_fusion.11), channel_id=1, source_target_pairs={{0,1},{1,2},{2,3},{3,4},{4,5},{5,6},{6,7},{7,0},{8,9},{9,10},{10,1... | collective-permute-start | bytes 393224 | tf_op jit(solution)/shard_map/ppermute | solution.py:122
  141.7 7.5 %collective-permute-start.10 = (f32[256,128]{1,0:T(8,128)S(1)}, f32[256,128]{1,0:T(8,128)S(1)}, u32[]{:S(2)}, u32[]{:S(2)}) collective-permute-start(f32[256,128]{1,0:T(8,128)S(1)} %bitcast_add_fusion.4), channel_id=1, source_target_pairs={{0,7},{1,0},{2,1},{3,2},{4,3},{5,4},{6,5},{7,6},{8,15},{9,8},{10,9... | collective-permute-start | bytes 393224 | tf_op jit(solution)/shard_map/ppermute | solution.py:122
  147.2 7.2 %collective-permute-start.4 = (f32[256,128]{1,0:T(8,128)S(1)}, f32[256,128]{1,0:T(8,128)S(1)}, u32[]{:S(2)}, u32[]{:S(2)}) collective-permute-start(f32[256,128]{1,0:T(8,128)S(1)} %bitcast_add_fusion.10), channel_id=1, source_target_pairs={{0,1},{1,2},{2,3},{3,4},{4,5},{5,6},{6,7},{7,0},{8,9},{9,10},{10,1... | collective-permute-start | bytes 393224 | tf_op jit(solution)/shard_map/ppermute | solution.py:122
  149.2 7.1 %collective-permute-start.11 = (f32[256,128]{1,0:T(8,128)S(1)}, f32[256,128]{1,0:T(8,128)S(1)}, u32[]{:S(2)}, u32[]{:S(2)}) collective-permute-start(f32[256,128]{1,0:T(8,128)S(1)} %bitcast_add_fusion.3), channel_id=1, source_target_pairs={{0,7},{1,0},{2,1},{3,2},{4,3},{5,4},{6,5},{7,6},{8,15},{9,8},{10,9... | collective-permute-start | bytes 393224 | tf_op jit(solution)/shard_map/ppermute | solution.py:122
  154.4 7.2 %collective-permute-start.5 = (f32[256,128]{1,0:T(8,128)S(1)}, f32[256,128]{1,0:T(8,128)S(1)}, u32[]{:S(2)}, u32[]{:S(2)}) collective-permute-start(f32[256,128]{1,0:T(8,128)S(1)} %bitcast_add_fusion.9), channel_id=1, source_target_pairs={{0,1},{1,2},{2,3},{3,4},{4,5},{5,6},{6,7},{7,0},{8,9},{9,10},{10,1... | collective-permute-start | bytes 393224 | tf_op jit(solution)/shard_map/ppermute | solution.py:122
  156.4 7.2 %collective-permute-start.12 = (f32[256,128]{1,0:T(8,128)S(1)}, f32[256,128]{1,0:T(8,128)S(1)}, u32[]{:S(2)}, u32[]{:S(2)}) collective-permute-start(f32[256,128]{1,0:T(8,128)S(1)} %bitcast_add_fusion.2), channel_id=1, source_target_pairs={{0,7},{1,0},{2,1},{3,2},{4,3},{5,4},{6,5},{7,6},{8,15},{9,8},{10,9... | collective-permute-start | bytes 393224 | tf_op jit(solution)/shard_map/ppermute | solution.py:122
  161.6 6.9 %collective-permute-start.6 = (f32[256,128]{1,0:T(8,128)S(1)}, f32[256,128]{1,0:T(8,128)S(1)}, u32[]{:S(2)}, u32[]{:S(2)}) collective-permute-start(f32[256,128]{1,0:T(8,128)S(1)} %bitcast_add_fusion.8), channel_id=1, source_target_pairs={{0,1},{1,2},{2,3},{3,4},{4,5},{5,6},{6,7},{7,0},{8,9},{9,10},{10,1... | collective-permute-start | bytes 393224 | tf_op jit(solution)/shard_map/ppermute | solution.py:122
  163.6 6.5 %collective-permute-start.13 = (f32[256,128]{1,0:T(8,128)S(1)}, f32[256,128]{1,0:T(8,128)S(1)}, u32[]{:S(2)}, u32[]{:S(2)}) collective-permute-start(f32[256,128]{1,0:T(8,128)S(1)} %bitcast_add_fusion.1), channel_id=1, source_target_pairs={{0,7},{1,0},{2,1},{3,2},{4,3},{5,4},{6,5},{7,6},{8,15},{9,8},{10,9... | collective-permute-start | bytes 393224 | tf_op jit(solution)/shard_map/ppermute | solution.py:122
Sparse Core Ops, SparseCore 0:
  78.0 33.1 reduce-scatter.1
  114.6 94.2 all-gather.1

commit v12 on v11

--- a/solution.py
+++ b/solution.py
@@ -71,9 +71,14 @@
         for _ in range(blocks)
     )
     final = lax.fori_loop(0, shards, body, start, unroll=UNROLL)
+    heads = rows // block
     for qb in range(blocks):
         _, total, context = final[qb]
-        o_ref[qb * rows : (qb + 1) * rows, :] = (context / total).astype(o_ref.dtype)
+        result = (context / total).astype(o_ref.dtype)
+        for h in range(heads):
+            o_ref[qb * block : (qb + 1) * block, h * HEAD_DIM : (h + 1) * HEAD_DIM] = result[
+                h * block : (h + 1) * block
+            ]
 
 
 def causal_attention(seq_index, queries, pair_all, block=128):
@@ -88,7 +93,7 @@
     kv_rows = pair_all.reshape(shards * tok_rows, 2 * HEAD_DIM)
     out = pl.pallas_call(
         functools.partial(attention_kernel, shards=shards, tok_rows=tok_rows, block=block),
-        out_shape=jax.ShapeDtypeStruct((tok_rows * heads_local, HEAD_DIM), jnp.bfloat16),
+        out_shape=jax.ShapeDtypeStruct((tok_rows, heads_local * HEAD_DIM), jnp.bfloat16),
         in_specs=[
             pl.BlockSpec(memory_space=pltpu.SMEM),
             pl.BlockSpec(memory_space=pltpu.VMEM),
@@ -102,11 +107,7 @@
             bytes_accessed=kv_rows.size * 2 + 2 * q_rows.size * 2,
         ),
     )(jnp.reshape(seq_index, (1,)).astype(jnp.int32), q_rows, kv_rows)
-    return (
-        out.reshape(blocks, heads_local, block, HEAD_DIM)
-        .transpose(0, 2, 1, 3)
-        .reshape(tok_rows, 1, heads_local * HEAD_DIM)
-    )
+    return out.reshape(tok_rows, 1, heads_local * HEAD_DIM)
 
 
 def ring_reduce_scatter(parts):

time: 238 us -> 237 us (level)
  no operation moved by 1% of the time
where the time goes in v12:
time: 237 us
  waiting for transfers between devices  87.5 us (37%)
  starting transfers between devices  63.5 us (27%)
  blocking collectives  22 us (9%)
  Pallas kernels  20.9 us (9%)
  local copies, waits for them, and re-layouts  16.4 us (7%)
  between operations  14.3 us (6%)
  other arithmetic  7.05 us (3%)
  matrix products  4.9 us (2%)
    ppermute x14, starting transfers between devices, ring_reduce_scatter(): buf = lax.ppermute(buf, axes, perm)  47 us
    all_gather x1, waiting for transfers between devices, local(): pair_all = lax.all_gather(pair_own, 'seq', axis=0, tiled=False)  38.7 us
    reduce_scatter x1, waiting for transfers between devices, local(): lax.psum_scatter(pair_part, ('kvh', 'rep'), scatter_dimension=0, tiled=True)  33.3 us
    all_gather x1, blocking collectives, local(): lax.all_gather(normed[0], 'kvh', axis=0, tiled=False)  22 us
    pallas_call x1, Pallas kernels, causal_attention(): pl.pallas_call(functools.partial(attention_kernel, shards=shards, tok_row...  20.9 us
    all_to_all x1, starting transfers between devices, local(): lax.all_to_all(outgoing, 'seq', split_axis=0, concat_axis=0, tiled=True)  16.4 us
    all_to_all x1, waiting for transfers between devices, local(): lax.all_to_all(outgoing, 'seq', split_axis=0, concat_axis=0, tiled=True)  10.6 us
    ppermute x14, waiting for transfers between devices, ring_reduce_scatter(): buf = lax.ppermute(buf, axes, perm)  4.95 us
  transfers between devices with their start and end apart: 17, of which 12 were waited for; matrix products, arithmetic and copies ran while one was open for 5% of the time, Pallas kernels for 0%

profile of v12, /device:TPU:1, one launch (start us, length us, event | category | flops | bytes accessed | tf_op | source)
XLA Modules:
  0.0 236.6 jit_solution(6857887681145751201)
XLA Ops:
  6.5 1.1 convert_reduce_fusion
  7.7 1.2 fusion.12
  8.9 0.8 copy.70
  9.8 0.7 sub.92
  10.5 0.6 dynamic_slice.52
  11.1 0.7 and_select_fusion.1
  12.0 1.1 fusion.14
  13.1 22.0 %all_gather.7 = bf16[4,96,1152]{2,1,0:T(8,128)(2,1)S(1)} all-gather(bf16[1,96,1152]{2,1,0:T(8,128)(2,1)S(1)} %fusion.14), channel_id=1, replica_groups=mesh['seq'=64,'kvh'=4,'rep'=2] {'kvh'}, dimensions={0}, use_global_device_ids=true | all-gather | bytes 1105920 | tf_op jit(solution)/shard_map/all_gather | solution.py:141
  35.2 2.1 fusion.2
  37.5 2.1 gather_fusion
  39.5 1.0 all_to_all.8
  40.5 16.4 %all-to-all-start = ((bf16[64,6,448]{2,1,0:T(8,128)(2,1)}), bf16[64,6,448]{2,1,0:T(8,128)(2,1)S(1)}, u32[]{:S(2)}, u32[]{:S(2)}) async-start(bf16[64,6,448]{2,1,0:T(8,128)(2,1)} %all_to_all.8), calls=%async_computation | async-start | bytes 1048576 | tf_op jit(solution)/shard_map/all_to_all | solution.py:158
  57.0 4.6 %copy.72 = bf16[448,3072]{0,1:T(8,128)(2,1)} copy(bf16[448,3072]{1,0:T(8,128)(2,1)} %param.9) | data formatting | bytes 5505024 | tf_op args[4]
  61.6 1.3 slice.23
  63.0 0.5 copy.93
  63.7 10.6 %all-to-all-done = bf16[64,6,448]{2,1,0:T(8,128)(2,1)S(1)} async-done(((bf16[64,6,448]{2,1,0:T(8,128)(2,1)}), bf16[64,6,448]{2,1,0:T(8,128)(2,1)S(1)}, u32[]{:S(2)}, u32[]{:S(2)}) %all-to-all-start) | async-done | bytes 344096 | tf_op jit(solution)/shard_map/all_to_all | solution.py:158
  74.3 0.2 all_to_all.10
  74.5 1.2 gather_fusion.1
  75.8 2.0 convolution_bitcast_fusion
  77.9 33.3 %reduce-scatter.2.cloned.1.call-done = f32[1,256,256]{2,1,0:T(8,128)} async-done(((f32[8,256,256]{2,1,0:T(8,128)}), f32[1,256,256]{2,1,0:T(8,128)}) %reduce-scatter.2.cloned.1.call-update) | async-done | bytes 262160 | tf_op jit(solution)/shard_map/reduce_scatter | solution.py:172
  111.2 1.6 convert_element_type.27
  113.1 1.8 slice.20
  115.0 0.7 convolution_bitcast_fusion.1
  115.9 0.2 constant_dynamic-slice_fusion
  116.3 3.5 %collective-permute-start = (f32[256,128]{1,0:T(8,128)S(1)}, f32[256,128]{1,0:T(8,128)S(1)}, u32[]{:S(2)}, u32[]{:S(2)}) collective-permute-start(f32[256,128]{1,0:T(8,128)S(1)} %bitcast.75), channel_id=1, source_target_pairs={{0,1},{1,2},{2,3},{3,4},{4,5},{5,6},{6,7},{7,0},{8,9},{9,10},{10,1... | collective-permute-start | bytes 393224 | tf_op jit(solution)/shard_map/ppermute | solution.py:123
  121.2 3.0 %collective-permute-start.7 = (f32[256,128]{1,0:T(8,128)S(1)}, f32[256,128]{1,0:T(8,128)S(1)}, u32[]{:S(2)}, u32[]{:S(2)}) collective-permute-start(f32[256,128]{1,0:T(8,128)S(1)} %bitcast.76), channel_id=1, source_target_pairs={{0,7},{1,0},{2,1},{3,2},{4,3},{5,4},{6,5},{7,6},{8,15},{9,8},{10,9... | collective-permute-start | bytes 393224 | tf_op jit(solution)/shard_map/ppermute | solution.py:123
  124.3 2.3 collective-permute-start.1
  126.6 0.4 collective-permute-done.7
  127.0 4.2 %collective-permute-start.8 = (f32[256,128]{1,0:T(8,128)S(1)}, f32[256,128]{1,0:T(8,128)S(1)}, u32[]{:S(2)}, u32[]{:S(2)}) collective-permute-start(f32[256,128]{1,0:T(8,128)S(1)} %bitcast_add_fusion.6), channel_id=1, source_target_pairs={{0,7},{1,0},{2,1},{3,2},{4,3},{5,4},{6,5},{7,6},{8,15},{9,8},{10,9... | collective-permute-start | bytes 393224 | tf_op jit(solution)/shard_map/ppermute | solution.py:123
  131.2 1.9 collective-permute-start.2
  133.2 1.0 collective-permute-done.8
  134.2 4.9 %collective-permute-start.9 = (f32[256,128]{1,0:T(8,128)S(1)}, f32[256,128]{1,0:T(8,128)S(1)}, u32[]{:S(2)}, u32[]{:S(2)}) collective-permute-start(f32[256,128]{1,0:T(8,128)S(1)} %bitcast_add_fusion.5), channel_id=1, source_target_pairs={{0,7},{1,0},{2,1},{3,2},{4,3},{5,4},{6,5},{7,6},{8,15},{9,8},{10,9... | collective-permute-start | bytes 393224 | tf_op jit(solution)/shard_map/ppermute | solution.py:123
  139.1 0.4 collective-permute-done.2
  139.4 1.9 collective-permute-start.3
  141.4 0.3 collective-permute-done.9
  141.7 5.3 %collective-permute-start.10 = (f32[256,128]{1,0:T(8,128)S(1)}, f32[256,128]{1,0:T(8,128)S(1)}, u32[]{:S(2)}, u32[]{:S(2)}) collective-permute-start(f32[256,128]{1,0:T(8,128)S(1)} %bitcast_add_fusion.4), channel_id=1, source_target_pairs={{0,7},{1,0},{2,1},{3,2},{4,3},{5,4},{6,5},{7,6},{8,15},{9,8},{10,9... | collective-permute-start | bytes 393224 | tf_op jit(solution)/shard_map/ppermute | solution.py:123
  147.2 1.9 collective-permute-start.4
  149.2 4.8 %collective-permute-start.11 = (f32[256,128]{1,0:T(8,128)S(1)}, f32[256,128]{1,0:T(8,128)S(1)}, u32[]{:S(2)}, u32[]{:S(2)}) collective-permute-start(f32[256,128]{1,0:T(8,128)S(1)} %bitcast_add_fusion.3), channel_id=1, source_target_pairs={{0,7},{1,0},{2,1},{3,2},{4,3},{5,4},{6,5},{7,6},{8,15},{9,8},{10,9... | collective-permute-start | bytes 393224 | tf_op jit(solution)/shard_map/ppermute | solution.py:123
  154.0 0.4 collective-permute-done.4
  154.4 1.9 collective-permute-start.5
  156.4 4.7 %collective-permute-start.12 = (f32[256,128]{1,0:T(8,128)S(1)}, f32[256,128]{1,0:T(8,128)S(1)}, u32[]{:S(2)}, u32[]{:S(2)}) collective-permute-start(f32[256,128]{1,0:T(8,128)S(1)} %bitcast_add_fusion.2), channel_id=1, source_target_pairs={{0,7},{1,0},{2,1},{3,2},{4,3},{5,4},{6,5},{7,6},{8,15},{9,8},{10,9... | collective-permute-start | bytes 393224 | tf_op jit(solution)/shard_map/ppermute | solution.py:123
  161.1 0.5 collective-permute-done.5
  161.6 1.9 collective-permute-start.6
  163.6 4.8 %collective-permute-start.13 = (f32[256,128]{1,0:T(8,128)S(1)}, f32[256,128]{1,0:T(8,128)S(1)}, u32[]{:S(2)}, u32[]{:S(2)}) collective-permute-start(f32[256,128]{1,0:T(8,128)S(1)} %bitcast_add_fusion.1), channel_id=1, source_target_pairs={{0,7},{1,0},{2,1},{3,2},{4,3},{5,4},{6,5},{7,6},{8,15},{9,8},{10,9... | collective-permute-start | bytes 393224 | tf_op jit(solution)/shard_map/ppermute | solution.py:123
  168.4 0.2 collective-permute-done.6
  168.6 1.5 collective-permute-done.13
  170.2 38.7 %all-gather.2.cloned.1.call-done = bf16[64,256,256]{2,1,0:T(8,128)(2,1)} async-done(((bf16[1,256,256]{2,1,0:T(8,128)(2,1)}), bf16[64,256,256]{2,1,0:T(8,128)(2,1)}) %all-gather.2.cloned.1.call-update) | async-done | bytes 8388624 | tf_op jit(solution)/shard_map/all_gather | solution.py:178
  208.9 20.9 %shard_map.55 = bf16[256,256]{1,0:T(8,128)(2,1)} custom-call(s32[1]{0:T(128)} %bitcast.seq_ref, bf16[512,128]{1,0:T(8,128)(2,1)S(1)} %bitcast.67, bf16[16384,256]{1,0:T(8,128)(2,1)} %bitcast.81), custom_call_target="tpu_custom_call" | custom-call | flops 3221225472 | bytes 8650752 | tf_op jit(solution)/shard_map/pallas_call | solution.py:94
  (64 shorter events, 3.2 us)
Async XLA Ops:
  6.5 28.6 %copy-start = (bf16[1152,448]{0,1:T(8,128)(2,1)S(1)}, bf16[1152,448]{0,1:T(8,128)(2,1)}, u32[]{:S(2)}) copy-start(bf16[1152,448]{0,1:T(8,128)(2,1)} %param.8) | copy-start | bytes 3096580
  40.5 33.8 %all-to-all-start = ((bf16[64,6,448]{2,1,0:T(8,128)(2,1)}), bf16[64,6,448]{2,1,0:T(8,128)(2,1)S(1)}, u32[]{:S(2)}, u32[]{:S(2)}) async-start(bf16[64,6,448]{2,1,0:T(8,128)(2,1)} %all_to_all.8), calls=%async_computation | async-start | bytes 1048576 | tf_op jit(solution)/shard_map/all_to_all | solution.py:158
  57.0 54.2 %reduce-scatter.2.cloned.1.call-start = ((), (), s32[]{:S(2)}) async-start(), calls=%async_computation.2 | async-start | bytes 2359296 | tf_op jit(solution)/shard_map/reduce_scatter | solution.py:172
  61.6 1.9 copy-start.1
  77.9 131.0 %all-gather.2.cloned.1.call-start = ((), (), s32[]{:S(2)}) async-start(), calls=%async_computation.3 | async-start | bytes 8519680 | tf_op jit(solution)/shard_map/all_gather | solution.py:178
  116.3 8.0 %collective-permute-start = (f32[256,128]{1,0:T(8,128)S(1)}, f32[256,128]{1,0:T(8,128)S(1)}, u32[]{:S(2)}, u32[]{:S(2)}) collective-permute-start(f32[256,128]{1,0:T(8,128)S(1)} %bitcast.75), channel_id=1, source_target_pairs={{0,1},{1,2},{2,3},{3,4},{4,5},{5,6},{6,7},{7,0},{8,9},{9,10},{10,1... | collective-permute-start | bytes 393224 | tf_op jit(solution)/shard_map/ppermute | solution.py:123
  121.2 5.7 %collective-permute-start.7 = (f32[256,128]{1,0:T(8,128)S(1)}, f32[256,128]{1,0:T(8,128)S(1)}, u32[]{:S(2)}, u32[]{:S(2)}) collective-permute-start(f32[256,128]{1,0:T(8,128)S(1)} %bitcast.76), channel_id=1, source_target_pairs={{0,7},{1,0},{2,1},{3,2},{4,3},{5,4},{6,5},{7,6},{8,15},{9,8},{10,9... | collective-permute-start | bytes 393224 | tf_op jit(solution)/shard_map/ppermute | solution.py:123
  124.3 6.9 %collective-permute-start.1 = (f32[256,128]{1,0:T(8,128)S(1)}, f32[256,128]{1,0:T(8,128)S(1)}, u32[]{:S(2)}, u32[]{:S(2)}) collective-permute-start(f32[256,128]{1,0:T(8,128)S(1)} %bitcast_add_fusion.13), channel_id=1, source_target_pairs={{0,1},{1,2},{2,3},{3,4},{4,5},{5,6},{6,7},{7,0},{8,9},{9,10},{10,1... | collective-permute-start | bytes 393224 | tf_op jit(solution)/shard_map/ppermute | solution.py:123
  127.0 7.2 %collective-permute-start.8 = (f32[256,128]{1,0:T(8,128)S(1)}, f32[256,128]{1,0:T(8,128)S(1)}, u32[]{:S(2)}, u32[]{:S(2)}) collective-permute-start(f32[256,128]{1,0:T(8,128)S(1)} %bitcast_add_fusion.6), channel_id=1, source_target_pairs={{0,7},{1,0},{2,1},{3,2},{4,3},{5,4},{6,5},{7,6},{8,15},{9,8},{10,9... | collective-permute-start | bytes 393224 | tf_op jit(solution)/shard_map/ppermute | solution.py:123
  131.2 8.2 %collective-permute-start.2 = (f32[256,128]{1,0:T(8,128)S(1)}, f32[256,128]{1,0:T(8,128)S(1)}, u32[]{:S(2)}, u32[]{:S(2)}) collective-permute-start(f32[256,128]{1,0:T(8,128)S(1)} %bitcast_add_fusion.12), channel_id=1, source_target_pairs={{0,1},{1,2},{2,3},{3,4},{4,5},{5,6},{6,7},{7,0},{8,9},{9,10},{10,1... | collective-permute-start | bytes 393224 | tf_op jit(solution)/shard_map/ppermute | solution.py:123
  134.2 7.5 %collective-permute-start.9 = (f32[256,128]{1,0:T(8,128)S(1)}, f32[256,128]{1,0:T(8,128)S(1)}, u32[]{:S(2)}, u32[]{:S(2)}) collective-permute-start(f32[256,128]{1,0:T(8,128)S(1)} %bitcast_add_fusion.5), channel_id=1, source_target_pairs={{0,7},{1,0},{2,1},{3,2},{4,3},{5,4},{6,5},{7,6},{8,15},{9,8},{10,9... | collective-permute-start | bytes 393224 | tf_op jit(solution)/shard_map/ppermute | solution.py:123
  139.4 7.8 %collective-permute-start.3 = (f32[256,128]{1,0:T(8,128)S(1)}, f32[256,128]{1,0:T(8,128)S(1)}, u32[]{:S(2)}, u32[]{:S(2)}) collective-permute-start(f32[256,128]{1,0:T(8,128)S(1)} %bitcast_add_fusion.11), channel_id=1, source_target_pairs={{0,1},{1,2},{2,3},{3,4},{4,5},{5,6},{6,7},{7,0},{8,9},{9,10},{10,1... | collective-permute-start | bytes 393224 | tf_op jit(solution)/shard_map/ppermute | solution.py:123
  141.7 7.5 %collective-permute-start.10 = (f32[256,128]{1,0:T(8,128)S(1)}, f32[256,128]{1,0:T(8,128)S(1)}, u32[]{:S(2)}, u32[]{:S(2)}) collective-permute-start(f32[256,128]{1,0:T(8,128)S(1)} %bitcast_add_fusion.4), channel_id=1, source_target_pairs={{0,7},{1,0},{2,1},{3,2},{4,3},{5,4},{6,5},{7,6},{8,15},{9,8},{10,9... | collective-permute-start | bytes 393224 | tf_op jit(solution)/shard_map/ppermute | solution.py:123
  147.2 7.2 %collective-permute-start.4 = (f32[256,128]{1,0:T(8,128)S(1)}, f32[256,128]{1,0:T(8,128)S(1)}, u32[]{:S(2)}, u32[]{:S(2)}) collective-permute-start(f32[256,128]{1,0:T(8,128)S(1)} %bitcast_add_fusion.10), channel_id=1, source_target_pairs={{0,1},{1,2},{2,3},{3,4},{4,5},{5,6},{6,7},{7,0},{8,9},{9,10},{10,1... | collective-permute-start | bytes 393224 | tf_op jit(solution)/shard_map/ppermute | solution.py:123
  149.2 7.1 %collective-permute-start.11 = (f32[256,128]{1,0:T(8,128)S(1)}, f32[256,128]{1,0:T(8,128)S(1)}, u32[]{:S(2)}, u32[]{:S(2)}) collective-permute-start(f32[256,128]{1,0:T(8,128)S(1)} %bitcast_add_fusion.3), channel_id=1, source_target_pairs={{0,7},{1,0},{2,1},{3,2},{4,3},{5,4},{6,5},{7,6},{8,15},{9,8},{10,9... | collective-permute-start | bytes 393224 | tf_op jit(solution)/shard_map/ppermute | solution.py:123
  154.4 7.2 %collective-permute-start.5 = (f32[256,128]{1,0:T(8,128)S(1)}, f32[256,128]{1,0:T(8,128)S(1)}, u32[]{:S(2)}, u32[]{:S(2)}) collective-permute-start(f32[256,128]{1,0:T(8,128)S(1)} %bitcast_add_fusion.9), channel_id=1, source_target_pairs={{0,1},{1,2},{2,3},{3,4},{4,5},{5,6},{6,7},{7,0},{8,9},{9,10},{10,1... | collective-permute-start | bytes 393224 | tf_op jit(solution)/shard_map/ppermute | solution.py:123
  156.4 7.2 %collective-permute-start.12 = (f32[256,128]{1,0:T(8,128)S(1)}, f32[256,128]{1,0:T(8,128)S(1)}, u32[]{:S(2)}, u32[]{:S(2)}) collective-permute-start(f32[256,128]{1,0:T(8,128)S(1)} %bitcast_add_fusion.2), channel_id=1, source_target_pairs={{0,7},{1,0},{2,1},{3,2},{4,3},{5,4},{6,5},{7,6},{8,15},{9,8},{10,9... | collective-permute-start | bytes 393224 | tf_op jit(solution)/shard_map/ppermute | solution.py:123
  161.6 6.9 %collective-permute-start.6 = (f32[256,128]{1,0:T(8,128)S(1)}, f32[256,128]{1,0:T(8,128)S(1)}, u32[]{:S(2)}, u32[]{:S(2)}) collective-permute-start(f32[256,128]{1,0:T(8,128)S(1)} %bitcast_add_fusion.8), channel_id=1, source_target_pairs={{0,1},{1,2},{2,3},{3,4},{4,5},{5,6},{6,7},{7,0},{8,9},{9,10},{10,1... | collective-permute-start | bytes 393224 | tf_op jit(solution)/shard_map/ppermute | solution.py:123
  163.6 6.5 %collective-permute-start.13 = (f32[256,128]{1,0:T(8,128)S(1)}, f32[256,128]{1,0:T(8,128)S(1)}, u32[]{:S(2)}, u32[]{:S(2)}) collective-permute-start(f32[256,128]{1,0:T(8,128)S(1)} %bitcast_add_fusion.1), channel_id=1, source_target_pairs={{0,7},{1,0},{2,1},{3,2},{4,3},{5,4},{6,5},{7,6},{8,15},{9,8},{10,9... | collective-permute-start | bytes 393224 | tf_op jit(solution)/shard_map/ppermute | solution.py:123
Sparse Core Ops, SparseCore 0:
  78.0 33.1 reduce-scatter.1
  114.6 94.2 all-gather.1
